TPU v7x, 32 devices: a whole 2x2x4 slice. The times are simulated.
32 devices in a mesh: grp: 2 (over x), suf: 4 (over y, core), head: 4 (over z).
Axes of the slice: x: 2, y: 2, z: 4, core: 2. Of those that a mesh axis runs over, the one named last changes fastest.
Arguments:
- prefix_x: bfloat16 [1024, 8192], P(('grp', 'suf'), 'head'), parts along dimension 0, may hold values from -6 to 6
- prefix_b: bfloat16 [1024, 1024], P(('grp', 'suf'), 'head'), parts along dimension 0, may hold values from -6 to 6
- prefix_c: bfloat16 [1024, 1024], P(('grp', 'suf'), 'head'), parts along dimension 0, may hold values from -6 to 6
- prefix_dt: float32 [128, 1024], P('head', ('grp', 'suf')), parts along dimension 1, may hold values from -3 to 3
- prefix_grad: bfloat16 [1024, 8192], P(('grp', 'suf'), 'head'), parts along dimension 0, may hold values from -0.59765625 to 0.59765625
- suffix_x: bfloat16 [8, 128, 8192], P(('grp', 'suf'), None, 'head'), parts along dimension 0, may hold values from -6 to 6
- suffix_b: bfloat16 [8, 128, 1024], P(('grp', 'suf'), None, 'head'), parts along dimension 0, may hold values from -6 to 6
- suffix_c: bfloat16 [8, 128, 1024], P(('grp', 'suf'), None, 'head'), parts along dimension 0, may hold values from -6 to 6
- suffix_dt: float32 [128, 8, 128], P('head', ('grp', 'suf')), parts along dimension 1, may hold values from -3 to 3
- suffix_grad: bfloat16 [8, 128, 8192], P(('grp', 'suf'), None, 'head'), parts along dimension 0, may hold values from -0.59765625 to 0.59765625
- lengths: int32 [8], P(('grp', 'suf')), parts along dimension 0, may hold values from 1 to 128, 384 in all
- loss_mask: int32 [8, 128], P(('grp', 'suf')), parts along dimension 0, may hold values 0 or 1
- advantage: float32 [8], P(('grp', 'suf')), parts along dimension 0, may hold values from -3 to 3
- conv_x: bfloat16 [4, 8192], P(None, 'head'), may hold values from -3 to 3
- conv_b: bfloat16 [4, 1024], P(None, 'head'), may hold values from -3 to 3
- conv_c: bfloat16 [4, 1024], P(None, 'head'), may hold values from -3 to 3
- decay_rate: float32 [128], P('head'), may hold values from 7.8125e-05 to 0.05
- dt_bias: float32 [128], P('head'), may hold values from -1 to 0.5
- skip: float32 [128], P('head'), may hold values from 0.5 to 1.5
Outputs:
- prefix_dx: bfloat16 [1024, 8192], P(('grp', 'suf'), 'head'), parts along dimension 0
- prefix_db: bfloat16 [1024, 1024], P(('grp', 'suf'), 'head'), parts along dimension 0
- prefix_dc: bfloat16 [1024, 1024], P(('grp', 'suf'), 'head'), parts along dimension 0
- prefix_ddt: float32 [128, 1024], P('head', ('grp', 'suf')), parts along dimension 1
- suffix_dx: bfloat16 [8, 128, 8192], P(('grp', 'suf'), None, 'head'), parts along dimension 0
- suffix_db: bfloat16 [8, 128, 1024], P(('grp', 'suf'), None, 'head'), parts along dimension 0
- suffix_dc: bfloat16 [8, 128, 1024], P(('grp', 'suf'), None, 'head'), parts along dimension 0
- suffix_ddt: float32 [128, 8, 128], P('head', ('grp', 'suf')), parts along dimension 1
There are 2 independent parts, one for each index of `grp`. A program takes and returns all parts, laid end to end along the dimension named above; an argument that names none is the same for every part. Nothing has to cross between parts.
Inputs may be any that keep to these rules, and one draw needn't show every extreme that they name: `lengths`: some suffix has exactly 128 tokens.
All inputs are finite; a program needn't handle non-finite values. No bound on the sum of `lengths` or of `loss_mask` on one device may be relied on, other than what follows from the above.
Results may differ from a plain program's by a relative error of at most 0.001.
Values may be sent and summed in bfloat16 or wider, within the bound.
No kernel may reach another device: no remote copies, remote signals or barrier semaphores. Data moves between devices by JAX's collectives and lax.ppermute only.
A program may use at most 128 MiB of HBM per device.

v0:
```python
import functools

import jax
import jax.numpy as jnp
from jax import lax
from jax.experimental import pallas as pl
from jax.sharding import PartitionSpec as P

HD = 64
N = 128
KW = 4
Q = 128


EXACT_DOT = lax.Precision.HIGHEST


def from_behind(block, axis, distance):
    devices = range(lax.axis_size(axis))
    route = [(i - distance, i) for i in devices if i - distance in devices]
    return lax.ppermute(block, axis, route)


def prefix(shard, axis, combine, identity, reverse):
    length, here = (lax.axis_size(axis), lax.axis_index(axis))
    everything = jax.tree.map(lambda part: lax.all_gather(part, axis), shard)
    start = jax.tree.map(
        lambda part, zero: jnp.broadcast_to(jnp.asarray(zero, part.dtype), part.shape),
        shard,
        identity,
    )

    def lap(k, before):
        at = length - 1 - k if reverse else k
        reached = at > here if reverse else at < here
        new = combine(before, jax.tree.map(lambda part: part[at], everything))
        return jax.tree.map(lambda a, b: jnp.where(reached, a, b), new, before)

    return lax.fori_loop(0, length, lap, start)


def spread(block, axis, holder):
    block = jnp.where(lax.axis_index(axis) == holder, block, jnp.zeros_like(block))
    return lax.psum(block, axis)


def causal_conv(values, context, taps):
    padded = jnp.concatenate([context, values], axis=0)
    num_tokens = values.shape[0]
    result = padded[0:num_tokens] * taps[0].astype(jnp.float32)
    for tap_index in range(1, taps.shape[0]):
        result = result + padded[tap_index : tap_index + num_tokens] * taps[tap_index].astype(
            jnp.float32
        )
    return jax.nn.silu(result)


def run_scan(x_act, b_act, c_act, step_dt, decay_rates, skip_gain, start_state):
    tokens = x_act.shape[0]
    num_heads = x_act.shape[1]
    num_groups = b_act.shape[1]
    per_group = num_heads // num_groups
    blocks = tokens // Q
    x_blocks = x_act.reshape(blocks, Q, num_groups, per_group, HD)
    b_blocks = b_act.reshape(blocks, Q, num_groups, N)
    c_blocks = c_act.reshape(blocks, Q, num_groups, N)
    log_decay = (
        (-step_dt * decay_rates[:, None])
        .reshape(num_groups, per_group, blocks, Q)
        .transpose(2, 0, 1, 3)
    )
    dt_blocks = step_dt.reshape(num_groups, per_group, blocks, Q).transpose(2, 0, 1, 3)
    lower_tri = jnp.arange(Q)[:, None] >= jnp.arange(Q)[None, :]
    skip_shaped = skip_gain.reshape(num_groups, per_group)[:, :, None]

    def advance(current, pieces):
        x_block, b_block, c_block, log_block, dt_block = pieces
        cumulative = jnp.cumsum(log_block, axis=-1)
        log_gaps = cumulative[..., :, None] - cumulative[..., None, :]
        within = jnp.where(lower_tri, jnp.exp(jnp.where(lower_tri, log_gaps, 0.0)), 0.0)
        scores = jnp.einsum("tgn,sgn->gts", c_block, b_block, precision=EXACT_DOT)
        mixing = scores[:, None] * within * dt_block[:, :, None, :]
        inner_out = jnp.einsum("gkts,sgkp->tgkp", mixing, x_block, precision=EXACT_DOT)
        carried = jnp.einsum("tgn,gkpn->tgkp", c_block, current, precision=EXACT_DOT)
        carried = carried * jnp.exp(cumulative).transpose(2, 0, 1)[..., None]
        output = inner_out + carried + skip_shaped * x_block
        weights = jnp.exp(cumulative[..., -1:] - cumulative) * dt_block
        updated = current * jnp.exp(cumulative[..., -1])[..., None, None]
        updated = updated + jnp.einsum(
            "gks,sgkp,sgn->gkpn", weights, x_block, b_block, precision=EXACT_DOT
        )
        return (updated, output)

    last_state, outputs = lax.scan(
        jax.checkpoint(advance),
        start_state.reshape(num_groups, per_group, HD, N),
        (x_blocks, b_blocks, c_blocks, log_decay, dt_blocks),
    )
    return (outputs.reshape(tokens, num_heads * HD), last_state.reshape(num_heads, HD, N))


def block_forward(x_feat, b_feat, c_feat, dt_raw, left_x, left_b, left_c, start_state, params):
    conv_x, conv_b, conv_c, decay_rates, dt_offset, skip_gain = params
    num_heads = decay_rates.shape[0]
    num_groups = conv_b.shape[1] // N
    x_act = causal_conv(x_feat, left_x, conv_x).reshape(-1, num_heads, HD)
    b_act = causal_conv(b_feat, left_b, conv_b).reshape(-1, num_groups, N)
    c_act = causal_conv(c_feat, left_c, conv_c).reshape(-1, num_groups, N)
    step_dt = jax.nn.softplus(dt_raw + dt_offset[:, None])
    return run_scan(x_act, b_act, c_act, step_dt, decay_rates, skip_gain, start_state)


def _dot(a, b, dims):
    return lax.dot_general(a, b, (dims, ((), ())), precision=EXACT_DOT, preferred_element_type=jnp.float32)


def _grad_kernel(per_group_pairs, x_ref, g_ref, b_ref, c_ref, crow_ref, ccol_ref, srow_ref,
                 dx_ref, dstep_ref, dcum_ref, dsc_ref):
    step_id = pl.program_id(0)
    x = x_ref[...]
    g = g_ref[...]
    t_len = x.shape[0]
    tri = lax.broadcasted_iota(jnp.int32, (t_len, t_len), 0) >= lax.broadcasted_iota(jnp.int32, (t_len, t_len), 1)
    lane = lax.broadcasted_iota(jnp.int32, (1, 2 * HD), 1)
    ones = jnp.ones((8, t_len), jnp.float32)
    scores = _dot(c_ref[...], b_ref[...], ((1,), (1,)))
    dx = jnp.zeros_like(x)
    dsc = jnp.zeros((t_len, t_len), jnp.float32)
    for h in range(2):
        mask = ((lane >= h * HD) & (lane < (h + 1) * HD)).astype(jnp.float32)
        gm = g * mask
        crow = crow_ref[0, h : h + 1, :]
        ccol = ccol_ref[0, :, h : h + 1]
        srow = srow_ref[0, h : h + 1, :]
        within = jnp.where(tri, jnp.exp(jnp.where(tri, ccol - crow, 0.0)), 0.0)
        score_w = scores * within
        d_mix = _dot(gm, x, ((1,), (1,)))
        dx = dx + _dot(score_w * srow, gm, ((0,), (0,)))
        dsc = dsc + d_mix * within * srow
        q_mat = d_mix * score_w
        p_mat = q_mat * srow
        dstep_ref[0, h : h + 1, :] = jnp.sum(q_mat, axis=0, keepdims=True)
        dcum_ref[0, h : h + 1, :] = _dot(ones, p_mat, ((1,), (1,)))[0:1] - jnp.sum(
            p_mat, axis=0, keepdims=True
        )
    dx_ref[...] = dx
    first = step_id % per_group_pairs == 0

    @pl.when(first)
    def _():
        dsc_ref[0] = dsc

    @pl.when(jnp.logical_not(first))
    def _():
        dsc_ref[0] += dsc


def block_inner(xa, ba, ca, step, rate, G):
    T, ng, nk, P = xa.shape
    nh = ng * nk
    pairs = nh // 2
    per_group_pairs = nk // 2
    cum = jnp.cumsum(-step * rate[:, :, None], axis=-1)
    cum_pairs = cum.reshape(pairs, 2, T)
    row_spec = pl.BlockSpec((1, 2, T), lambda j: (j, 0, 0))
    lane_spec = pl.BlockSpec((T, 2 * P), lambda j: (0, j))
    grp_spec = pl.BlockSpec((T, N), lambda j: (0, j // per_group_pairs))
    dx2, d_direct, d_cum, d_scores = pl.pallas_call(
        functools.partial(_grad_kernel, per_group_pairs),
        grid=(pairs,),
        in_specs=[
            lane_spec, lane_spec, grp_spec, grp_spec, row_spec,
            pl.BlockSpec((1, T, 2), lambda j: (j, 0, 0)), row_spec,
        ],
        out_specs=[
            lane_spec, row_spec, row_spec,
            pl.BlockSpec((1, T, T), lambda j: (j // per_group_pairs, 0, 0)),
        ],
        out_shape=[
            jax.ShapeDtypeStruct((T, nh * P), jnp.float32),
            jax.ShapeDtypeStruct((pairs, 2, T), jnp.float32),
            jax.ShapeDtypeStruct((pairs, 2, T), jnp.float32),
            jax.ShapeDtypeStruct((ng, T, T), jnp.float32),
        ],
    )(
        xa.reshape(T, nh * P),
        G.reshape(T, nh * P),
        ba.reshape(T, ng * N),
        ca.reshape(T, ng * N),
        cum_pairs,
        jnp.swapaxes(cum_pairs, 1, 2),
        step.reshape(pairs, 2, T),
    )
    return (
        dx2.reshape(T, ng, nk, P),
        d_direct.reshape(ng, nk, T),
        d_cum.reshape(ng, nk, T),
        d_scores,
        cum,
    )


def block_outer(inner, xa, ba, ca, step, rate, skip, S0, G, lam):
    dx, d_step, d_cum, d_scores, cum = inner
    dx = dx + skip[None, :, :, None] * G
    dc = jnp.einsum("gts,sgn->tgn", d_scores, ba, precision=EXACT_DOT)
    db = jnp.einsum("gts,tgn->sgn", d_scores, ca, precision=EXACT_DOT)
    grow = jnp.exp(cum)
    g_grow = G * grow.transpose(2, 0, 1)[..., None]
    carried = jnp.einsum("tgn,gkpn->tgkp", ca, S0, precision=EXACT_DOT)
    dc = dc + jnp.einsum("tgkp,gkpn->tgn", g_grow, S0, precision=EXACT_DOT)
    d_cum = d_cum + jnp.sum(g_grow * carried, axis=-1).transpose(1, 2, 0)
    if lam is not None:
        to_end = jnp.exp(cum[..., -1:] - cum)
        push = to_end * step
        lam_b = jnp.einsum("gkpn,sgn->sgkp", lam, ba, precision=EXACT_DOT)
        dx = dx + push.transpose(2, 0, 1)[..., None] * lam_b
        db = db + jnp.einsum("gkpn,sgkp,gks->sgn", lam, xa, push, precision=EXACT_DOT)
        q_end = jnp.sum(xa * lam_b, axis=-1).transpose(1, 2, 0)
        d_step = d_step + to_end * q_end
        wq = push * q_end
        end_total = jnp.sum(wq, axis=-1) + jnp.exp(cum[..., -1]) * jnp.sum(lam * S0, axis=(-2, -1))
        d_cum = d_cum - wq
        d_cum = d_cum.at[..., -1].add(end_total)
    d_log = jnp.flip(jnp.cumsum(jnp.flip(d_cum, -1), axis=-1), -1)
    d_step = d_step - rate[:, :, None] * d_log
    return dx, db, dc, d_step


def shards(
    prefix_x,
    prefix_b,
    prefix_c,
    prefix_dt,
    prefix_grad,
    suffix_x,
    suffix_b,
    suffix_c,
    suffix_dt,
    suffix_grad,
    lengths,
    loss_mask,
    advantage,
    conv_x,
    conv_b,
    conv_c,
    decay_rate,
    dt_bias,
    skip,
):
    num_ways = lax.axis_size("suf")
    my_index = lax.axis_index("suf")
    num_heads = decay_rate.shape[0]
    num_groups = conv_b.shape[1] // N
    per_group = num_heads // num_groups
    margin = KW - 1
    prompt_len = prefix_x.shape[0]
    width_x = prefix_x.shape[1]
    width_b = prefix_b.shape[1]
    rate = decay_rate.reshape(num_groups, per_group)
    gain = skip.reshape(num_groups, per_group)

    def split_tokens(tokens):
        return (
            tokens[:, :width_x],
            tokens[:, width_x : width_x + width_b],
            tokens[:, width_x + width_b :],
        )

    def convs(ux, ub, uc, cx, cb, cc):
        return (
            causal_conv(ux, cx, conv_x),
            causal_conv(ub, cb, conv_b),
            causal_conv(uc, cc, conv_c),
        )

    def softplus_of(raw):
        return jax.nn.softplus(raw + dt_bias[:, None])

    prompt_step, step_pullback = jax.vjp(softplus_of, prefix_dt)
    cumulative = jnp.cumsum(-prompt_step * decay_rate[:, None], axis=1)
    total_log = cumulative[:, -1]
    tails = jnp.concatenate(
        [prefix_x[-margin:], prefix_b[-margin:], prefix_c[-margin:]], axis=1
    ).astype(jnp.float32)
    tail_size = tails.size
    own_pack = jnp.concatenate([tails.reshape(-1), total_log])
    received = [own_pack] + [
        lax.ppermute(own_pack, "suf", [(j, (j + shift) % num_ways) for j in range(num_ways)])
        for shift in range(1, num_ways)
    ]
    every = jnp.take(
        jnp.stack(received), (my_index - jnp.arange(num_ways)) % num_ways, axis=0
    )
    every_tails = every[:, :tail_size].reshape((num_ways,) + tails.shape)
    every_log = every[:, tail_size:]
    behind = lax.dynamic_index_in_dim(every_tails, jnp.maximum(my_index - 1, 0), 0, False)
    behind = jnp.where(my_index > 0, behind, 0.0)
    left_x, left_b, left_c = split_tokens(behind)
    ctx_x, ctx_b, ctx_c = split_tokens(every_tails[num_ways - 1])

    acts, prompt_conv_pullback = jax.vjp(
        convs,
        prefix_x.astype(jnp.float32),
        prefix_b.astype(jnp.float32),
        prefix_c.astype(jnp.float32),
        left_x,
        left_b,
        left_c,
    )
    x_act = acts[0].reshape(prompt_len, num_groups, per_group, HD)
    b_act = acts[1].reshape(prompt_len, num_groups, N)
    c_act = acts[2].reshape(prompt_len, num_groups, N)
    prompt_cot = prefix_grad.astype(jnp.float32).reshape(prompt_len, num_groups, per_group, HD)
    push_weight = (jnp.exp(total_log[:, None] - cumulative) * prompt_step).reshape(
        num_groups, per_group, prompt_len
    )
    own_state = jnp.einsum("gkt,tgkp,tgn->gkpn", push_weight, x_act, b_act, precision=EXACT_DOT)
    pull_weight = jnp.exp(cumulative).reshape(num_groups, per_group, prompt_len)
    own_adjoint = jnp.einsum(
        "gkt,tgkp,tgn->gkpn", pull_weight, prompt_cot, c_act, precision=EXACT_DOT
    )
    positions = jnp.arange(suffix_x.shape[1])[None, :]
    weight = (
        advantage[:, None]
        * loss_mask.astype(jnp.float32)
        * (positions < lengths[:, None]).astype(jnp.float32)
    )

    def suffix_parts(x_one, b_one, c_one, dt_one, grad_one, weight_one):
        suffix_len = x_one.shape[0]
        step_one, one_step_pullback = jax.vjp(softplus_of, dt_one)
        s_acts, conv_pullback = jax.vjp(convs, x_one, b_one, c_one, ctx_x, ctx_b, ctx_c)
        sx = s_acts[0].reshape(suffix_len, num_groups, per_group, HD)
        sb = s_acts[1].reshape(suffix_len, num_groups, N)
        sc = s_acts[2].reshape(suffix_len, num_groups, N)
        cot = (weight_one[:, None] * grad_one).reshape(suffix_len, num_groups, per_group, HD)
        step_g = step_one.reshape(num_groups, per_group, suffix_len)
        return one_step_pullback, conv_pullback, sx, sb, sc, cot, step_g

    def suffix_front(*items):
        unused_a, unused_b, sx, sb, sc, cot, step_g = suffix_parts(*items)
        grow = jnp.exp(jnp.cumsum(-step_g * rate[:, :, None], axis=-1))
        adjoint = jnp.einsum("gkt,tgkp,tgn->gkpn", grow, cot, sc, precision=EXACT_DOT)
        return adjoint, block_inner(sx, sb, sc, step_g, rate, cot)

    def suffix_back(end_state, inner, *items):
        one_step_pullback, conv_pullback, sx, sb, sc, cot, step_g = suffix_parts(*items)
        suffix_len = sx.shape[0]
        dx, db, dc, d_step = block_outer(inner, sx, sb, sc, step_g, rate, gain, end_state, cot, None)
        conv_grads = conv_pullback(
            (dx.reshape(suffix_len, -1), db.reshape(suffix_len, -1), dc.reshape(suffix_len, -1))
        )
        d_dt = one_step_pullback(d_step.reshape(num_heads, suffix_len))[0]
        return conv_grads, d_dt

    suffix_items = (
        suffix_x.astype(jnp.float32),
        suffix_b.astype(jnp.float32),
        suffix_c.astype(jnp.float32),
        suffix_dt,
        suffix_grad.astype(jnp.float32),
        weight,
    )
    adjoints, suffix_inner = jax.vmap(suffix_front, in_axes=(0, 0, 0, 1, 0, 0))(*suffix_items)
    step_g = prompt_step.reshape(num_groups, per_group, prompt_len)
    prompt_inner = block_inner(x_act, b_act, c_act, step_g, rate, prompt_cot)
    core = my_index % 2
    chip = my_index // 2
    num_chips = num_ways // 2
    own_triple = jnp.stack([own_state, own_adjoint, jnp.sum(adjoints, axis=0)])
    partner_triple = lax.ppermute(own_triple, "suf", [(j, j ^ 1) for j in range(num_ways)])
    even = jnp.where(core == 0, own_triple, partner_triple)
    odd = jnp.where(core == 0, partner_triple, own_triple)
    block_decay = jnp.exp(every_log).reshape(num_ways, num_groups, per_group, 1, 1)
    decay_even = lax.dynamic_index_in_dim(block_decay, 2 * chip, 0, False)
    decay_odd = lax.dynamic_index_in_dim(block_decay, 2 * chip + 1, 0, False)
    chip_log = every_log.reshape(num_chips, 2, num_heads).sum(axis=1)
    later_log = jnp.sum(jnp.where((jnp.arange(num_chips) >= chip)[:, None], chip_log, 0.0), axis=0)
    chip_state = decay_odd * even[0] + odd[0]
    chip_adjoint = even[1] + decay_even * odd[1]
    chip_suffix = even[2] + odd[2]
    chip_later = chip_adjoint + jnp.exp(later_log).reshape(num_groups, per_group, 1, 1) * chip_suffix
    got_state = [chip_state]
    got_other = [chip_suffix]
    for shift in range(1, num_chips):
        wraps = chip + shift >= num_chips
        outgoing = jnp.where(core == 0, chip_state, jnp.where(wraps, chip_later, chip_suffix))
        route = [
            (2 * c + k, 2 * ((c + shift) % num_chips) + k) for c in range(num_chips) for k in range(2)
        ]
        incoming = lax.ppermute(outgoing, "suf", route)
        shared = lax.ppermute(incoming, "suf", [(j, j ^ 1) for j in range(num_ways)])
        got_state.append(jnp.where(core == 0, incoming, shared))
        got_other.append(jnp.where(core == 0, shared, incoming))
    order = (chip - jnp.arange(num_chips)) % num_chips
    chip_states = jnp.take(jnp.stack(got_state), order, axis=0)
    chip_others = jnp.take(jnp.stack(got_other), order, axis=0)
    chip_decay = jnp.exp(chip_log).reshape(num_chips, num_groups, per_group, 1, 1)
    running = jnp.zeros_like(own_state)
    chip_start = running
    for c in range(num_chips):
        chip_start = jnp.where(chip == c, running, chip_start)
        running = chip_decay[c] * running + chip_states[c]
    prompt_end_late = running
    running = jnp.sum(
        jnp.where((jnp.arange(num_chips) <= chip).reshape(num_chips, 1, 1, 1, 1), chip_others, 0.0),
        axis=0,
    )
    chip_end_grad = running
    for c in reversed(range(num_chips)):
        chip_end_grad = jnp.where(chip == c, running, chip_end_grad)
        running = chip_others[c] + chip_decay[c] * running
    start_state = jnp.where(core == 0, chip_start, decay_even * chip_start + even[0])
    end_grad = jnp.where(core == 0, odd[1] + decay_odd * chip_end_grad, chip_end_grad)
    conv_grads, suffix_ddt = jax.vmap(
        suffix_back, in_axes=(None, 0, 0, 0, 0, 1, 0, 0), out_axes=(0, 1)
    )(prompt_end_late, suffix_inner, *suffix_items)
    dx, db, dc, d_step = block_outer(
        prompt_inner, x_act, b_act, c_act, step_g, rate, gain, start_state, prompt_cot, end_grad
    )
    prompt_grads = prompt_conv_pullback(
        (dx.reshape(prompt_len, -1), db.reshape(prompt_len, -1), dc.reshape(prompt_len, -1))
    )
    prefix_ddt = step_pullback(d_step.reshape(num_heads, prompt_len))[0]
    left_grads = jnp.concatenate([prompt_grads[3], prompt_grads[4], prompt_grads[5]], axis=1)
    from_right = from_behind(left_grads, "suf", -1)
    ctx_grads = jnp.concatenate(
        [jnp.sum(conv_grads[3], axis=0), jnp.sum(conv_grads[4], axis=0), jnp.sum(conv_grads[5], axis=0)],
        axis=1,
    )
    from_suffix = ctx_grads
    for sender in range(num_ways - 1):
        from_suffix = from_suffix + lax.ppermute(ctx_grads, "suf", [(sender, num_ways - 1)])
    last_device = my_index == num_ways - 1
    tail_add = split_tokens(from_right + jnp.where(last_device, from_suffix, 0.0))

    def finish(grad_full, extra):
        return grad_full.at[-margin:].add(extra).astype(jnp.bfloat16)

    return (
        finish(prompt_grads[0], tail_add[0]),
        finish(prompt_grads[1], tail_add[1]),
        finish(prompt_grads[2], tail_add[2]),
        prefix_ddt,
        conv_grads[0].astype(jnp.bfloat16),
        conv_grads[1].astype(jnp.bfloat16),
        conv_grads[2].astype(jnp.bfloat16),
        suffix_ddt,
    )


def solution(mesh):
    return jax.shard_map(
        shards,
        mesh=mesh,
        in_specs=(
            P(("grp", "suf"), "head"),
            P(("grp", "suf"), "head"),
            P(("grp", "suf"), "head"),
            P("head", ("grp", "suf")),
            P(("grp", "suf"), "head"),
            P(("grp", "suf"), None, "head"),
            P(("grp", "suf"), None, "head"),
            P(("grp", "suf"), None, "head"),
            P("head", ("grp", "suf"), None),
            P(("grp", "suf"), None, "head"),
            P(("grp", "suf")),
            P(("grp", "suf"), None),
            P(("grp", "suf")),
            P(None, "head"),
            P(None, "head"),
            P(None, "head"),
            P("head"),
            P("head"),
            P("head"),
        ),
        out_specs=(
            P(("grp", "suf"), "head"),
            P(("grp", "suf"), "head"),
            P(("grp", "suf"), "head"),
            P("head", ("grp", "suf")),
            P(("grp", "suf"), None, "head"),
            P(("grp", "suf"), None, "head"),
            P(("grp", "suf"), None, "head"),
            P("head", ("grp", "suf"), None),
        ),
        check_vma=False,
    )
```

profile of v0, /device:TPU:1, one launch (start us, length us, event | category | flops | bytes accessed | tf_op | source)
XLA Modules:
  0.0 241.1 jit_solution(17187771168466960452)
XLA Ops:
  3.0 1.4 compare_select_fusion.7
  4.9 2.7 %collective-permute-start.1 = (f32[7712]{0:T(1024)S(1)}, f32[7712]{0:T(1024)}, u32[]{:S(2)}, u32[]{:S(2)}) collective-permute-start(f32[7712]{0:T(1024)S(1)} %pad_maximum_fusion.12), channel_id=1, source_target_pairs={{0,8},{4,12},{8,0},{12,4},{1,9},{5,13},{9,1},{13,5},{2,10},{6,14},... | collective-permute-start | bytes 92552 | tf_op jit(solution)/shard_map/ppermute | solution.py:289
  7.7 1.4 collective-permute-start
  11.2 1.4 exponential_multiply_fusion.1
  14.6 1.4 slice_convert_fusion.14
  16.0 1.4 slice_convert_fusion.10
  18.8 1.5 slice_convert_fusion.6
  20.3 1.4 compare_select_fusion.3.srow_ref
  22.4 2.2 fusion.124.g_ref
  27.4 1.4 copy.184
  36.0 1.9 multiply_bitcast_fusion
  37.9 18.3 %vmap__.1 = (f32[128,2048]{1,0:T(8,128)}, f32[16,2,128]{2,1,0:T(2,128)}, f32[16,2,128]{2,1,0:T(2,128)}, f32[2,128,128]{2,1,0:T(8,128)}) custom-call(f32[128,2048]{1,0:T(8,128)} %get-tuple-element.90.x_ref, f32[128,2048]{1,0:T(8,128)} %fusion.124.g_ref, f32[128,256]{1,0:T(8,128)} %get-tuple-element.165.b_ref, f32[128,256]{1,0:T(8,128)} %get-tuple-element.86.c_ref, ...), custom_call_target="tpu_custom_call" | custom-call | tf_op jit(solution)/shard_map/vmap()/pallas_call | solution.py:168
  56.3 3.5 %broadcast_multiply_fusion = (f32[1,128,2048]{2,1,0:T(8,128)}, f32[1,128,2048]{2,1,0:T(8,128)}, f32[1,128,2048]{2,1,0:T(8,128)}) fusion(f32[2048]{0:T(1024)S(1)} %bitcast.322, f32[1,128,2048]{2,1,0:T(8,128)S(1)} %copy-done.16, bf16[1,128,2048]{2,1,0:T(8,128)(2,1)S(1)} %copy-done.20, f32[128]{0:T(128)S(1)} %copy-done.114, f32[2048]{0:T(1024)S(1)} %copy-done.75, ...), kind=kLoop, calls=%fused_computation.102 | loop fusion | flops 3670016 | bytes 5784064 | tf_op jit(solution)/shard_map/vmap(transpose(jvp()))/mul | solution.py:52
  59.8 1.6 copy.174
  61.5 2.8 %fusion.38 = (f32[128,2048]{1,0:T(8,128)}, f32[128,2048]{1,0:T(8,128)}) fusion(f32[128,2048]{1,0:T(8,128)S(1)} %copy-done.15, f32[2048]{0:T(1024)} %bitcast.319, f32[2048]{0:T(1024)} %bitcast.315, f32[3,2048]{1,0:T(4,128)} %slice.367, f32[2048]{0:T(1024)} %bitcast.311, f32[2048]{0:T(1024)} %bitcast.307), kind=kLoop, calls=%fused_computation.98 | loop fusion | flops 3670016 | bytes 3203072 | tf_op jit(solution)/shard_map/jvp(jit(silu))/mul | solution.py:55
  64.3 1.5 copy.171
  65.8 1.8 convolution_bitcast_fusion.4
  69.8 2.0 pad_maximum_fusion
  71.8 2.1 convert_element_type.158.g_ref
  75.3 1.6 negate_multiply_fusion
  76.9 1.6 copy.162
  78.5 1.4 reduce_window_sum.47
  80.6 1.4 copy.230
  83.3 1.5 copy.168
  84.7 1.4 copy.163
  97.3 1.4 reshape.614
  98.7 1.9 fusion.97
  100.6 1.7 copy.220
  102.3 1.8 broadcast_multiply_fusion.8
  104.1 1.6 copy.221
  106.4 3.7 %broadcast_select_fusion.1 = (f32[3,2,16,64,128]{4,3,2,1,0:T(8,128)S(1)}, f32[3,2,16,64,128]{4,3,2,1,0:T(8,128)S(1)}) fusion(f32[3,2,16,64,128]{4,3,2,1,0:T(8,128)} %collective-permute-done.3, pred[]{:T(512)S(6)} %eq.48, f32[1,2,16,64,128]{4,3,2,1,0:T(8,128)} %copy-done.13, f32[1,2,16,64,128]{4,3,2,1,0:T(8,128)} %copy-done.12, ...), kind=kLoop, calls=%fused_computation.14 | loop fusion | flops 3145728 | bytes 12582913 | tf_op jit(solution)/shard_map/jit(_where)/select_n | solution.py:374
  110.2 1.7 fusion.32
  115.2 18.2 %shard_map.242 = (f32[128,2048]{1,0:T(8,128)}, f32[16,2,128]{2,1,0:T(2,128)}, f32[16,2,128]{2,1,0:T(2,128)}, f32[2,128,128]{2,1,0:T(8,128)}) custom-call(f32[128,2048]{1,0:T(8,128)} %get-tuple-element.106.x_ref, f32[128,2048]{1,0:T(8,128)} %convert_element_type.158.g_ref, f32[128,256]{1,0:T(8,128)} %copy-done.35, f32[128,256]{1,0:T(8,128)} %copy-done.36, ...), custom_call_target="tpu_custom_call" | custom-call | tf_op jit(solution)/shard_map/pallas_call | solution.py:168
  133.4 2.6 %copy.164 = f32[128,2048]{0,1:T(8,128)} copy(f32[128,2048]{1,0:T(8,128)} %get-tuple-element.65) | data formatting | bytes 2097152 | tf_op jit(solution)/shard_map/pallas_call | solution.py:168
  136.0 1.5 copy.191
  137.5 1.5 copy.194
  138.9 1.7 broadcast_multiply_fusion.1
  145.7 2.7 %multiply_add_fusion = f32[1,2,16,64,128]{4,3,2,1,0:T(8,128)} fusion(f32[3,2,16,64,128]{4,3,2,1,0:T(8,128)} %copy-done, f32[3,2,16,64,128]{4,3,2,1,0:T(8,128)} %copy-done.1, f32[2,16]{1,0:T(2,128)S(1)} %copy-done.103), kind=kLoop, calls=%fused_computation.89 | loop fusion | flops 524288 | bytes 3145856 | tf_op jit(solution)/shard_map/add | solution.py:380
  148.4 2.5 %select_bitcast_fusion.1 = (f32[1,2,16,64,128]{4,3,2,1,0:T(8,128)S(1)}, f32[1,2,16,64,128]{4,3,2,1,0:T(8,128)}) fusion(f32[2,16,64,128]{3,2,1,0:T(8,128)S(1)} %collective-permute-done.5, f32[2,16,64,128]{3,2,1,0:T(8,128)} %collective-permute-done.4, pred[]{:T(512)S(6)} %eq.48), kind=kLoop, calls=%fused_computation.93 | loop fusion | flops 524288 | bytes 4194305 | tf_op jit(solution)/shard_map/stack | solution.py:398
  150.9 1.4 pad_maximum_fusion.1
  152.3 3.8 %gather_fusion.1 = f32[2,2,16,64,128]{4,3,2,1,0:T(8,128)} fusion(f32[2,2,16,64,128]{4,3,2,1,0:T(8,128)} %pad_maximum_fusion.1, s32[1024]{0:T(1024)} %pad_clamp_fusion), kind=kCustom, calls=%fused_computation.clone | custom fusion | bytes 4194312 | tf_op jit(solution)/shard_map/jit(_take)/gather | solution.py:398
  156.1 3.2 %pad_maximum_fusion.2 = f32[2,2,16,64,128]{4,3,2,1,0:T(8,128)} fusion(f32[1,2,16,64,128]{4,3,2,1,0:T(8,128)} %get-tuple-element.111, f32[1,2,16,64,128]{4,3,2,1,0:T(8,128)} %multiply_add_fusion), kind=kLoop, calls=%fused_computation.5 | loop fusion | flops 524288 | bytes 4194304 | tf_op jit(solution)/shard_map/stack | solution.py:397
  159.3 3.7 %gather_fusion.2 = f32[2,2,16,64,128]{4,3,2,1,0:T(8,128)} fusion(f32[2,2,16,64,128]{4,3,2,1,0:T(8,128)} %pad_maximum_fusion.2, s32[1024]{0:T(1024)} %pad_clamp_fusion), kind=kCustom, calls=%fused_computation.1.clone | custom fusion | bytes 4194312 | tf_op jit(solution)/shard_map/jit(_take)/gather | solution.py:397
  163.0 3.4 %select_reduce_fusion = (f32[2,16,64,128]{3,2,1,0:T(8,128)S(1)}, f32[2,2,16,64,128]{4,3,2,1,0:T(8,128)S(1)}, f32[2,2,16,64,128]{4,3,2,1,0:T(8,128)S(1)}) fusion(pred[2]{0:T(512)(128)(4,1)S(1)} %copy-done.118, f32[2,2,16,64,128]{4,3,2,1,0:T(8,128)} %gather_fusion.1, pred[2]{0:T(512)(128)(4,1)S(1)} %copy-done.117, f32[2,2,16,64,128]{4,3,2,1,0:T(8,128)} %gather_fusion.2), kind=kLoop, calls=%fused_computation.6 | loop fusion | flops 1835008 | bytes 9437188 | tf_op jit(solution)/shard_map/reduce_sum | solution.py:406
  166.5 4.4 %multiply_reduce_fusion = (f32[2,16]{1,0:T(2,128)}, f32[2,16,64,128]{3,2,1,0:T(8,128)S(1)}, f32[2,16,64,128]{3,2,1,0:T(8,128)}) fusion(f32[3,2,16,64,128]{4,3,2,1,0:T(8,128)} %copy-done.1, f32[2,16]{1,0:T(2,128)S(1)} %copy-done.112, f32[2,2,16,64,128]{4,3,2,1,0:T(8,128)S(1)} %get-tuple-element.162, f32[2,16]{1,0:T(2,128)S(1)} %copy-done.105, pred[]{:T(512)S(6)} %eq.50, ...), kind=kLoop, calls=%fused_computation.84 | loop fusion | flops 3407840 | bytes 7340675 | tf_op jit(solution)/shard_map/reduce_sum | solution.py:222
  170.9 1.7 fusion.3
  172.6 1.9 convolution_bitcast_fusion.9
  175.6 1.6 copy.219
  180.6 3.6 %fusion.5 = f32[1,128,2,128]{1,3,2,0:T(8,128)} fusion(f32[1,128,2,128]{1,3,2,0:T(8,128)} %convolution_bitcast_fusion.6, f32[128,2,16,64]{0,3,2,1:T(8,128)S(1)} %bitcast.283, f32[128,2,16]{0,2,1:T(8,128)S(1)} %copy-done.53, f32[2,2,16,64,128]{4,3,2,1,0:T(8,128)S(1)} %copy-done.9, f32[2,16]{1,0:T(2,128)S(1)} %copy-done.106, f32[2,16]{1,0:T(2,128)S(1)} %copy-done.109), kind=kOutput, calls=%fused_computation.32 | convolution fusion | flops 403734528 | bytes 3424512 | tf_op jit(solution)/shard_map/vmap(tgkp,gkpn->tgn)/dot_general | solution.py:211
  184.2 1.7 copy.222
  188.3 1.4 pad_maximum_fusion.11
  189.7 3.6 %collective-permute-start.8 = (f32[3,2560]{1,0:T(4,128)}, f32[3,2560]{1,0:T(4,128)}, u32[]{:S(2)}, u32[]{:S(2)}) collective-permute-start(f32[3,2560]{1,0:T(4,128)} %pad_maximum_fusion.11), channel_id=1, source_target_pairs={{4,12},{5,13},{6,14},{7,15},{20,28},{21,29},{22,30},{23,31}} | collective-permute-start | bytes 92168 | tf_op jit(solution)/shard_map/ppermute | solution.py:434
  195.8 2.0 multiply_reduce_fusion.1
  197.9 1.7 fusion.110
  201.0 2.8 %multiply_add_fusion.1 = f32[128,2,16,64]{0,3,2,1:T(8,128)} fusion(f32[128,2,16,64]{0,3,2,1:T(8,128)} %get-tuple-element.164, f32[128,2,16,64]{0,3,2,1:T(8,128)} %bitcast.285, f32[128,2,16]{0,2,1:T(8,128)} %copy.170, f32[2,16]{1,0:T(2,128)} %copy-done.115, f32[128,2048]{0,1:T(8,128)S(1)} %copy.165), kind=kLoop, calls=%fused_computation.91 | loop fusion | flops 1048576 | bytes 4210816 | tf_op jit(solution)/shard_map/add | solution.py:217
  203.8 2.5 %copy.177 = f32[128,2048]{1,0:T(8,128)} copy(f32[128,2048]{0,1:T(8,128)} %bitcast.286) | data formatting | bytes 2097152 | tf_op jit(solution)/shard_map/reshape | solution.py:423
  206.3 2.0 broadcast_multiply_fusion.4
  215.0 1.5 exponential_multiply_fusion
  219.9 3.1 %convolution_bitcast_fusion.10 = f32[128,2,128]{0,2,1:T(8,128)S(1)} fusion(f32[2,16,64,128]{3,2,1,0:T(8,128)} %get-tuple-element.79, f32[2,16,128,64]{2,3,1,0:T(8,128)S(1)} %bitcast.281, f32[2,16,128]{2,1,0:T(8,128)} %copy.180), kind=kOutput, calls=%fused_computation.31 | convolution fusion | flops 402915328 | bytes 2244608 | tf_op jit(solution)/shard_map/gkpn,sgkp,gks->sgn/dot_general | solution.py:218
  226.4 2.4 collective-permute-start.6
  229.7 1.6 split.67
  231.3 1.5 split.56
  233.5 2.0 split.51
  237.1 1.4 scatter-add.14
  (381 shorter events, 72.7 us)
Async XLA Ops:
  0.6 24.5 %copy-start.67 = (bf16[128,256]{1,0:T(8,128)(2,1)S(1)}, bf16[128,256]{1,0:T(8,128)(2,1)}, u32[]{:S(2)}) copy-start(bf16[128,256]{1,0:T(8,128)(2,1)} %param.30) | copy-start | bytes 196612
  0.6 24.5 %copy-start.68 = (bf16[128,256]{1,0:T(8,128)(2,1)S(1)}, bf16[128,256]{1,0:T(8,128)(2,1)}, u32[]{:S(2)}) copy-start(bf16[128,256]{1,0:T(8,128)(2,1)} %param.31) | copy-start | bytes 196612
  0.7 24.5 %copy-start.38 = (bf16[128,2048]{1,0:T(8,128)(2,1)S(1)}, bf16[128,2048]{1,0:T(8,128)(2,1)}, u32[]{:S(2)}) copy-start(bf16[128,2048]{1,0:T(8,128)(2,1)} %param.29) | copy-start | bytes 1572868
  2.9 23.4 %copy-start.120 = (f32[32]{0:T(128)S(1)}, f32[32]{0:T(128)}, u32[]{:S(2)}) copy-start(f32[32]{0:T(128)} %param.47) | copy-start | bytes 388
  2.9 24.2 %copy-start.70 = (bf16[1,128,256]{2,1,0:T(8,128)(2,1)S(1)}, bf16[1,128,256]{2,1,0:T(8,128)(2,1)}, u32[]{:S(2)}) copy-start(bf16[1,128,256]{2,1,0:T(8,128)(2,1)} %param.35) | copy-start | bytes 196612
  4.9 22.3 %copy-start.71 = (bf16[1,128,256]{2,1,0:T(8,128)(2,1)S(1)}, bf16[1,128,256]{2,1,0:T(8,128)(2,1)}, u32[]{:S(2)}) copy-start(bf16[1,128,256]{2,1,0:T(8,128)(2,1)} %param.36) | copy-start | bytes 196612
  4.9 24.1 %collective-permute-start.2 = (f32[7712]{0:T(1024)S(1)}, f32[7712]{0:T(1024)}, u32[]{:S(2)}, u32[]{:S(2)}) collective-permute-start(f32[7712]{0:T(1024)S(1)} %pad_maximum_fusion.12), channel_id=1, source_target_pairs={{0,12},{4,0},{8,4},{12,8},{1,13},{5,1},{9,5},{13,9},{2,14},{6,2},{... | collective-permute-start | bytes 92552 | tf_op jit(solution)/shard_map/ppermute | solution.py:289
  4.9 24.8 %collective-permute-start.1 = (f32[7712]{0:T(1024)S(1)}, f32[7712]{0:T(1024)}, u32[]{:S(2)}, u32[]{:S(2)}) collective-permute-start(f32[7712]{0:T(1024)S(1)} %pad_maximum_fusion.12), channel_id=1, source_target_pairs={{0,8},{4,12},{8,0},{12,4},{1,9},{5,13},{9,1},{13,5},{2,10},{6,14},... | collective-permute-start | bytes 92552 | tf_op jit(solution)/shard_map/ppermute | solution.py:289
  7.7 22.9 %collective-permute-start = (f32[7712]{0:T(1024)S(1)}, f32[7712]{0:T(1024)S(1)}, u32[]{:S(2)}, u32[]{:S(2)}) collective-permute-start(f32[7712]{0:T(1024)S(1)} %pad_maximum_fusion.12), channel_id=1, source_target_pairs={{0,4},{4,8},{8,12},{12,0},{1,5},{5,9},{9,13},{13,1},{2,6},{6,10},{... | collective-permute-start | bytes 92552 | tf_op jit(solution)/shard_map/ppermute | solution.py:289
  9.8 16.5 %copy-start.99 = (f32[2,16]{1,0:T(2,128)}, f32[2,16]{1,0:T(2,128)S(1)}, u32[]{:S(2)}) copy-start(f32[2,16]{1,0:T(2,128)S(1)} %mul.867) | copy-start | bytes 388
  16.0 18.4 %copy-start.76 = (f32[1,256]{1,0:T(1,128)}, f32[1,256]{1,0:T(1,128)S(1)}, u32[]{:S(2)}) copy-start(f32[1,256]{1,0:T(1,128)S(1)} %get-tuple-element.152) | copy-start | bytes 3076
  18.8 8.6 %copy-start.54 = (f32[1,2,16,128]{3,2,1,0:T(8,128)}, f32[1,2,16,128]{3,2,1,0:T(8,128)S(1)}, u32[]{:S(2)}) copy-start(f32[1,2,16,128]{3,2,1,0:T(8,128)S(1)} %reduce_window_sum.48) | copy-start | bytes 49156
  18.8 8.4 %copy-start.19 = (bf16[128,2048]{1,0:T(8,128)(2,1)S(1)}, bf16[128,2048]{1,0:T(8,128)(2,1)}, u32[]{:S(2)}) copy-start(bf16[128,2048]{1,0:T(8,128)(2,1)} %param.33) | copy-start | bytes 1572868
  18.8 48.8 %copy-start.52 = (f32[128,2,16]{0,2,1:T(8,128)}, f32[128,2,16]{0,2,1:T(8,128)S(1)}, u32[]{:S(2)}) copy-start(f32[128,2,16]{0,2,1:T(8,128)S(1)} %exponential_bitcast_fusion.1) | copy-start | bytes 49156
  22.4 3.9 %copy-start.113 = (f32[128]{0:T(128)}, f32[128]{0:T(128)S(1)}, u32[]{:S(2)}) copy-start(f32[128]{0:T(128)S(1)} %fusion.119) | copy-start | bytes 1540
  27.4 4.1 %copy-start.119 = (pred[4]{0:T(512)(128)(4,1)S(1)}, pred[4]{0:T(512)(128)(4,1)}, u32[]{:S(2)}) copy-start(pred[4]{0:T(512)(128)(4,1)} %compare_and_fusion.1) | copy-start | bytes 16
  30.6 3.8 %copy-start.80 = (f32[1,256]{1,0:T(1,128)S(1)}, f32[1,256]{1,0:T(1,128)}, u32[]{:S(2)}) copy-start(f32[1,256]{1,0:T(1,128)} %get-tuple-element.153) | copy-start | bytes 3076
  31.5 4.5 %copy-start.55 = (f32[1,2048]{1,0:T(1,128)S(1)}, f32[1,2048]{1,0:T(1,128)}, u32[]{:S(2)}) copy-start(f32[1,2048]{1,0:T(1,128)} %get-tuple-element.146) | copy-start | bytes 24580
  31.5 4.5 %copy-start.58 = (f32[1,2048]{1,0:T(1,128)S(1)}, f32[1,2048]{1,0:T(1,128)}, u32[]{:S(2)}) copy-start(f32[1,2048]{1,0:T(1,128)} %get-tuple-element.147) | copy-start | bytes 24580
  31.5 4.5 %copy-start.61 = (f32[1,2048]{1,0:T(1,128)S(1)}, f32[1,2048]{1,0:T(1,128)}, u32[]{:S(2)}) copy-start(f32[1,2048]{1,0:T(1,128)} %get-tuple-element.149) | copy-start | bytes 24580
  31.5 4.5 %copy-start.63 = (f32[1,2048]{1,0:T(1,128)S(1)}, f32[1,2048]{1,0:T(1,128)}, u32[]{:S(2)}) copy-start(f32[1,2048]{1,0:T(1,128)} %get-tuple-element.148) | copy-start | bytes 24580
  37.9 18.3 %copy-start.16 = (f32[1,128,2048]{2,1,0:T(8,128)S(1)}, f32[1,128,2048]{2,1,0:T(8,128)}, u32[]{:S(2)}) copy-start(f32[1,128,2048]{2,1,0:T(8,128)} %get-tuple-element.91) | copy-start | bytes 3145732
  37.9 18.3 %copy-start.20 = (bf16[1,128,2048]{2,1,0:T(8,128)(2,1)S(1)}, bf16[1,128,2048]{2,1,0:T(8,128)(2,1)}, u32[]{:S(2)}) copy-start(bf16[1,128,2048]{2,1,0:T(8,128)(2,1)} %param.38) | copy-start | bytes 1572868
  37.9 18.3 %copy-start.75 = (f32[2048]{0:T(1024)S(1)}, f32[2048]{0:T(1024)}, u32[]{:S(2)}) copy-start(f32[2048]{0:T(1024)} %mul.959) | copy-start | bytes 24580
  37.9 18.3 %copy-start.114 = (f32[128]{0:T(128)S(1)}, f32[128]{0:T(128)}, u32[]{:S(2)}) copy-start(f32[128]{0:T(128)} %copy-done.113) | copy-start | bytes 1540
  69.8 4.1 %copy-start.65 = (f32[32,128]{1,0:T(8,128)S(1)}, f32[32,128]{1,0:T(8,128)}, u32[]{:S(2)}) copy-start(f32[32,128]{1,0:T(8,128)} %get-tuple-element.140) | copy-start | bytes 49156
  71.8 34.7 %collective-permute-start.3 = (f32[3,2,16,64,128]{4,3,2,1,0:T(8,128)}, f32[3,2,16,64,128]{4,3,2,1,0:T(8,128)}, u32[]{:S(2)}, u32[]{:S(2)}) collective-permute-start(f32[3,2,16,64,128]{4,3,2,1,0:T(8,128)} %pad_maximum_fusion), channel_id=1, source_target_pairs={{0,4},{4,0},{8,12},{12,8},{1,5},{5,1},{9,13},{13,9},{2,6},{6,2},{1... | collective-permute-start | bytes 9437192 | tf_op jit(solution)/shard_map/ppermute | solution.py:372
  79.9 30.3 %copy-start.49 = (f32[2,16,128]{2,1,0:T(8,128)}, f32[2,16,128]{2,1,0:T(8,128)S(1)}, u32[]{:S(2)}) copy-start(f32[2,16,128]{2,1,0:T(8,128)S(1)} %reduce_window_sum.47) | copy-start | bytes 49156
  113.5 28.5 %collective-permute-start.4 = (f32[2,16,64,128]{3,2,1,0:T(8,128)}, f32[2,16,64,128]{3,2,1,0:T(8,128)}, u32[]{:S(2)}, u32[]{:S(2)}) collective-permute-start(f32[2,16,64,128]{3,2,1,0:T(8,128)} %get-tuple-element.104), channel_id=1, source_target_pairs={{0,8},{4,12},{8,0},{12,4},{1,9},{5,13},{9,1},{13,5},{2,10},{6,14},... | collective-permute-start | bytes 3145736 | tf_op jit(solution)/shard_map/ppermute | solution.py:392
  115.2 23.7 %copy-start.56 = (f32[1,2048]{1,0:T(1,128)S(1)}, f32[1,2048]{1,0:T(1,128)}, u32[]{:S(2)}) copy-start(f32[1,2048]{1,0:T(1,128)} %get-tuple-element.146) | copy-start | bytes 24580
  115.2 23.7 %copy-start.59 = (f32[1,2048]{1,0:T(1,128)S(1)}, f32[1,2048]{1,0:T(1,128)}, u32[]{:S(2)}) copy-start(f32[1,2048]{1,0:T(1,128)} %get-tuple-element.147) | copy-start | bytes 24580
  140.6 5.0 %copy-start.103 = (f32[2,16]{1,0:T(2,128)S(1)}, f32[2,16]{1,0:T(2,128)}, u32[]{:S(2)}) copy-start(f32[2,16]{1,0:T(2,128)} %copy-done.102) | copy-start | bytes 388
  142.0 6.4 %collective-permute-start.5 = (f32[2,16,64,128]{3,2,1,0:T(8,128)}, f32[2,16,64,128]{3,2,1,0:T(8,128)S(1)}, u32[]{:S(2)}, u32[]{:S(2)}) collective-permute-start(f32[2,16,64,128]{3,2,1,0:T(8,128)} %collective-permute-done.4), channel_id=1, source_target_pairs={{0,4},{4,0},{8,12},{12,8},{1,5},{5,1},{9,13},{13,9},{2,6},{6,2},{1... | collective-permute-start | bytes 3145736 | tf_op jit(solution)/shard_map/ppermute | solution.py:393
  166.4 4.5 %copy-start.8 = (f32[2,2,16,64,128]{4,3,2,1,0:T(8,128)}, f32[2,2,16,64,128]{4,3,2,1,0:T(8,128)S(1)}, u32[]{:S(2)}) copy-start(f32[2,2,16,64,128]{4,3,2,1,0:T(8,128)S(1)} %get-tuple-element.162) | copy-start | bytes 6291460
  166.5 4.4 %copy-start.64 = (f32[128,2,16]{0,2,1:T(8,128)S(1)}, f32[128,2,16]{0,2,1:T(8,128)}, u32[]{:S(2)}) copy-start(f32[128,2,16]{0,2,1:T(8,128)} %get-tuple-element.142) | copy-start | bytes 49156
  172.6 4.6 %copy-start.34 = (f32[128,256]{1,0:T(8,128)S(1)}, f32[128,256]{1,0:T(8,128)}, u32[]{:S(2)}) copy-start(f32[128,256]{1,0:T(8,128)} %copy-done.33) | copy-start | bytes 393220
  172.6 8.0 %copy-start.53 = (f32[128,2,16]{0,2,1:T(8,128)S(1)}, f32[128,2,16]{0,2,1:T(8,128)}, u32[]{:S(2)}) copy-start(f32[128,2,16]{0,2,1:T(8,128)} %copy-done.52) | copy-start | bytes 49156
  178.4 7.5 %copy-start.32 = (f32[1,128,256]{2,1,0:T(8,128)S(1)}, f32[1,128,256]{2,1,0:T(8,128)}, u32[]{:S(2)}) copy-start(f32[1,128,256]{2,1,0:T(8,128)} %copy-done.31) | copy-start | bytes 393220
  185.8 10.0 %copy-start.11 = (f32[2,16,64,128]{3,2,1,0:T(8,128)S(1)}, f32[2,16,64,128]{3,2,1,0:T(8,128)}, u32[]{:S(2)}) copy-start(f32[2,16,64,128]{3,2,1,0:T(8,128)} %get-tuple-element.79) | copy-start | bytes 3145732
  188.3 7.5 %copy-start.73 = (f32[3,256]{1,0:T(4,128)}, f32[3,256]{1,0:T(4,128)S(1)}, u32[]{:S(2)}) copy-start(f32[3,256]{1,0:T(4,128)S(1)} %slice_bitcast_fusion.7) | copy-start | bytes 9220
  189.7 45.7 %collective-permute-start.8 = (f32[3,2560]{1,0:T(4,128)}, f32[3,2560]{1,0:T(4,128)}, u32[]{:S(2)}, u32[]{:S(2)}) collective-permute-start(f32[3,2560]{1,0:T(4,128)} %pad_maximum_fusion.11), channel_id=1, source_target_pairs={{4,12},{5,13},{6,14},{7,15},{20,28},{21,29},{22,30},{23,31}} | collective-permute-start | bytes 92168 | tf_op jit(solution)/shard_map/ppermute | solution.py:434
  193.3 42.1 %collective-permute-start.9 = (f32[3,2560]{1,0:T(4,128)}, f32[3,2560]{1,0:T(4,128)}, u32[]{:S(2)}, u32[]{:S(2)}) collective-permute-start(f32[3,2560]{1,0:T(4,128)} %pad_maximum_fusion.11), channel_id=1, source_target_pairs={{8,12},{9,13},{10,14},{11,15},{24,28},{25,29},{26,30},{27,31}} | collective-permute-start | bytes 92168 | tf_op jit(solution)/shard_map/ppermute | solution.py:434
  194.6 40.9 %collective-permute-start.7 = (f32[3,2560]{1,0:T(4,128)}, f32[3,2560]{1,0:T(4,128)}, u32[]{:S(2)}, u32[]{:S(2)}) collective-permute-start(f32[3,2560]{1,0:T(4,128)} %pad_maximum_fusion.11), channel_id=1, source_target_pairs={{0,12},{1,13},{2,14},{3,15},{16,28},{17,29},{18,30},{19,31}} | collective-permute-start | bytes 92168 | tf_op jit(solution)/shard_map/ppermute | solution.py:434
  213.4 9.6 %copy-start.43 = (f32[16,2,8,128]{3,2,1,0:T(8,128)S(1)}, f32[16,2,8,128]{3,2,1,0:T(8,128)}, u32[]{:S(2)}) copy-start(f32[16,2,8,128]{3,2,1,0:T(8,128)} %get-tuple-element.167) | copy-start | bytes 393220
  213.4 9.6 %copy-start.48 = (f32[2,128,128]{2,1,0:T(8,128)S(1)}, f32[2,128,128]{2,1,0:T(8,128)}, u32[]{:S(2)}) copy-start(f32[2,128,128]{2,1,0:T(8,128)} %get-tuple-element.66) | copy-start | bytes 393220
  217.3 6.2 %copy-start.29 = (f32[128,256]{1,0:T(8,128)S(1)}, f32[128,256]{1,0:T(8,128)}, u32[]{:S(2)}) copy-start(f32[128,256]{1,0:T(8,128)} %copy-done.28) | copy-start | bytes 393220
  217.3 6.2 %copy-start.89 = (f32[1,256]{1,0:T(1,128)S(1)}, f32[1,256]{1,0:T(1,128)}, u32[]{:S(2)}) copy-start(f32[1,256]{1,0:T(1,128)} %get-tuple-element.154) | copy-start | bytes 3076
  218.4 6.0 %copy-start.30 = (f32[2,16,128]{1,0,2:T(2,128)S(1)}, f32[2,16,128]{1,0,2:T(2,128)}, u32[]{:S(2)}) copy-start(f32[2,16,128]{1,0,2:T(2,128)} %copy.168) | copy-start | bytes 49156
  218.4 6.0 %copy-start.41 = (f32[2,16,128]{1,0,2:T(2,128)S(1)}, f32[2,16,128]{1,0,2:T(2,128)}, u32[]{:S(2)}) copy-start(f32[2,16,128]{1,0,2:T(2,128)} %copy.191) | copy-start | bytes 49156
  218.4 6.0 %copy-start.100 = (f32[2,16]{1,0:T(2,128)S(1)}, f32[2,16]{1,0:T(2,128)}, u32[]{:S(2)}) copy-start(f32[2,16]{1,0:T(2,128)} %copy-done.99) | copy-start | bytes 388
  219.9 4.7 %copy-start.66 = (f32[32,128]{1,0:T(8,128)S(1)}, f32[32,128]{1,0:T(8,128)}, u32[]{:S(2)}) copy-start(f32[32,128]{1,0:T(8,128)} %param.32) | copy-start | bytes 49156
  219.9 4.7 %copy-start.104 = (f32[32]{0:T(128)S(1)}, f32[32]{0:T(128)}, u32[]{:S(2)}) copy-start(f32[32]{0:T(128)} %param.46) | copy-start | bytes 388
  219.9 5.5 %copy-start.78 = (f32[1,256]{1,0:T(1,128)S(1)}, f32[1,256]{1,0:T(1,128)}, u32[]{:S(2)}) copy-start(f32[1,256]{1,0:T(1,128)} %copy-done.76) | copy-start | bytes 3076
  219.9 5.5 %copy-start.82 = (f32[1,256]{1,0:T(1,128)S(1)}, f32[1,256]{1,0:T(1,128)}, u32[]{:S(2)}) copy-start(f32[1,256]{1,0:T(1,128)} %get-tuple-element.153) | copy-start | bytes 3076
  219.9 5.5 %copy-start.86 = (f32[1,256]{1,0:T(1,128)S(1)}, f32[1,256]{1,0:T(1,128)}, u32[]{:S(2)}) copy-start(f32[1,256]{1,0:T(1,128)} %get-tuple-element.155) | copy-start | bytes 3076
  224.3 11.2 %copy-start.72 = (f32[3,256]{1,0:T(4,128)S(1)}, f32[3,256]{1,0:T(4,128)}, u32[]{:S(2)}) copy-start(f32[3,256]{1,0:T(4,128)} %slice_bitcast_fusion.8) | copy-start | bytes 9220
  224.3 11.2 %copy-start.74 = (f32[3,256]{1,0:T(4,128)S(1)}, f32[3,256]{1,0:T(4,128)}, u32[]{:S(2)}) copy-start(f32[3,256]{1,0:T(4,128)} %copy-done.73) | copy-start | bytes 9220
  224.4 11.9 %copy-start.22 = (f32[128,256]{1,0:T(8,128)S(1)}, f32[128,256]{1,0:T(8,128)}, u32[]{:S(2)}) copy-start(f32[128,256]{1,0:T(8,128)} %copy-done.21) | copy-start | bytes 393220
  224.4 11.9 %copy-start.24 = (f32[128,256]{1,0:T(8,128)S(1)}, f32[128,256]{1,0:T(8,128)}, u32[]{:S(2)}) copy-start(f32[128,256]{1,0:T(8,128)} %copy-done.23) | copy-start | bytes 393220
  224.6 11.8 %copy-start.26 = (f32[128,256]{1,0:T(8,128)S(1)}, f32[128,256]{1,0:T(8,128)}, u32[]{:S(2)}) copy-start(f32[128,256]{1,0:T(8,128)} %copy-done.25) | copy-start | bytes 393220
  225.4 11.7 %copy-start.3 = (f32[128,2048]{1,0:T(8,128)S(1)}, f32[128,2048]{1,0:T(8,128)}, u32[]{:S(2)}) copy-start(f32[128,2048]{1,0:T(8,128)} %copy-done.2) | copy-start | bytes 3145732
  225.4 11.7 %copy-start.5 = (f32[128,2048]{1,0:T(8,128)S(1)}, f32[128,2048]{1,0:T(8,128)}, u32[]{:S(2)}) copy-start(f32[128,2048]{1,0:T(8,128)} %copy-done.4) | copy-start | bytes 3145732
  225.4 11.7 %copy-start.7 = (f32[128,2048]{1,0:T(8,128)S(1)}, f32[128,2048]{1,0:T(8,128)}, u32[]{:S(2)}) copy-start(f32[128,2048]{1,0:T(8,128)} %copy-done.6) | copy-start | bytes 3145732
  226.4 9.1 %collective-permute-start.6 = (f32[3,2560]{1,0:T(4,128)S(1)}, f32[3,2560]{1,0:T(4,128)S(1)}, u32[]{:S(2)}, u32[]{:S(2)}) collective-permute-start(f32[3,2560]{1,0:T(4,128)S(1)} %pad_maximum_fusion.10), channel_id=1, source_target_pairs={{4,0},{8,4},{12,8},{5,1},{9,5},{13,9},{6,2},{10,6},{14,10},{7,3},{... | collective-permute-start | bytes 92168 | tf_op jit(solution)/shard_map/ppermute | solution.py:21
  (67 other events, 180.4 us)
where the time goes:
time: 244 us; the launch traced here: 241 us
  other arithmetic  91.7 us (38%)
  local copies, waits for them, and re-layouts  73.9 us (30%)
  Pallas kernels  36.5 us (15%)
  matrix products  21.7 us (9%)
  starting transfers between devices  13.8 us (6%)
  between operations  3.63 us (1%)
    pallas_call x2, Pallas kernels, block_inner(): pl.pallas_call(functools.partial(_grad_kernel, per_group_pairs), grid=(pa...  36.5 us
    mul x12, other arithmetic, causal_conv(): padded[tap_index:tap_index + num_tokens]  13.8 us
    split x6, local copies, waits for them, and re-layouts, causal_conv(): padded = jnp.concatenate([context, values], axis=0)  7.24 us
    unnamed x243, local copies, waits for them, and re-layouts  6.63 us
    ppermute x3, starting transfers between devices, shards(): lax.ppermute(ctx_grads, 'suf', [(sender, num_ways - 1)])  6.14 us
    dot_general x2, matrix products, block_outer(): dc = dc + jnp.einsum('tgkp,gkpn->tgn', g_grow, S0, precision=EXACT_DOT)  5.49 us
    reshape x3, other arithmetic, block_inner(): pl.pallas_call(functools.partial(_grad_kernel, per_group_pairs), grid=(pa...  4.96 us
  transfers between devices with their start and end apart: 10, of which 0 were waited for; matrix products, arithmetic and copies ran while one was open for 43% of the time, Pallas kernels for 8%

commit v1 on v0

--- a/solution.py
+++ b/solution.py
@@ -393,9 +393,18 @@
         shared = lax.ppermute(incoming, "suf", [(j, j ^ 1) for j in range(num_ways)])
         got_state.append(jnp.where(core == 0, incoming, shared))
         got_other.append(jnp.where(core == 0, shared, incoming))
-    order = (chip - jnp.arange(num_chips)) % num_chips
-    chip_states = jnp.take(jnp.stack(got_state), order, axis=0)
-    chip_others = jnp.take(jnp.stack(got_other), order, axis=0)
+    def chip_ordered(got):
+        ordered = []
+        for c in range(num_chips):
+            distance = (chip - c) % num_chips
+            value = got[0]
+            for shift in range(1, num_chips):
+                value = jnp.where(distance == shift, got[shift], value)
+            ordered.append(value)
+        return ordered
+
+    chip_states = chip_ordered(got_state)
+    chip_others = chip_ordered(got_other)
     chip_decay = jnp.exp(chip_log).reshape(num_chips, num_groups, per_group, 1, 1)
     running = jnp.zeros_like(own_state)
     chip_start = running
@@ -403,10 +412,9 @@
         chip_start = jnp.where(chip == c, running, chip_start)
         running = chip_decay[c] * running + chip_states[c]
     prompt_end_late = running
-    running = jnp.sum(
-        jnp.where((jnp.arange(num_chips) <= chip).reshape(num_chips, 1, 1, 1, 1), chip_others, 0.0),
-        axis=0,
-    )
+    running = jnp.zeros_like(own_state)
+    for c in range(num_chips):
+        running = running + jnp.where(c <= chip, chip_others[c], 0.0)
     chip_end_grad = running
     for c in reversed(range(num_chips)):
         chip_end_grad = jnp.where(chip == c, running, chip_end_grad)
@@ -436,7 +444,8 @@
     tail_add = split_tokens(from_right + jnp.where(last_device, from_suffix, 0.0))
 
     def finish(grad_full, extra):
-        return grad_full.at[-margin:].add(extra).astype(jnp.bfloat16)
+        placed = jnp.pad(extra, ((grad_full.shape[0] - margin, 0), (0, 0)))
+        return (grad_full + placed).astype(jnp.bfloat16)
 
     return (
         finish(prompt_grads[0], tail_add[0]),

time: 244 us -> 207 us (0.85)
  local copies, waits for them, and re-layouts: 73.9 us -> 56.2 us
  other arithmetic: 91.7 us -> 74.7 us
  matrix products: 21.7 us -> 19.2 us
    gather x2 -> x0, local copies, waits for them, and re-layouts: 7.48 us -> none  [the longest x1 3.78 us: shards(): chip_others = jnp.take(jnp.stack(got_other), order, axis=0)]
    another operation x3 -> x0, other arithmetic: 7.09 us -> none  [the longest x2 3.94 us: shards(): chip_others = jnp.take(jnp.stack(got_other), order, axis=0)]
    split x6 -> x3, local copies, waits for them, and re-layouts: 7.24 us -> 3.09 us  [causal_conv(): padded = jnp.concatenate([context, values], axis=0)]
    scatter-add x3 -> x0, local copies, waits for them, and re-layouts: 4 us -> none  [finish(): return grad_full.at[-margin:].add(extra).astype(jnp.bfloat16)]
    reduce_sum x1 -> x0, other arithmetic: 3.44 us -> none  [shards(): jnp.sum(jnp.where((jnp.arange(num_chips) <= chip).reshape(num_chips, 1, 1...]
    add x3 -> x0, other arithmetic: 3.42 us -> none  [the longest x1 2.68 us: shards(): chip_state = decay_odd * even[0] + odd[0]]
    unnamed x243 -> x221, local copies, waits for them, and re-layouts: 6.63 us -> 5.24 us
  transfers between devices with their start and end apart: 10 -> 10, of which waited for: 0 -> 1; matrix products, arithmetic and copies ran while one was open for 43% -> 46% of each run, Pallas kernels for 8% -> 9%
where the time goes in v1:
time: 207 us; the launch traced here: 205 us
  other arithmetic  74.7 us (36%)
  local copies, waits for them, and re-layouts  56.2 us (27%)
  Pallas kernels  36.5 us (18%)
  matrix products  19.2 us (9%)
  starting transfers between devices  13.9 us (7%)
  between operations  3.44 us (2%)
    pallas_call x2, Pallas kernels, block_inner(): pl.pallas_call(functools.partial(_grad_kernel, per_group_pairs), grid=(pa...  36.5 us
    mul x12, other arithmetic, causal_conv(): padded[tap_index:tap_index + num_tokens]  11.7 us
    reshape x3, other arithmetic, block_inner(): pl.pallas_call(functools.partial(_grad_kernel, per_group_pairs), grid=(pa...  6.23 us
    ppermute x3, starting transfers between devices, shards(): lax.ppermute(ctx_grads, 'suf', [(sender, num_ways - 1)])  6.15 us
    unnamed x221, local copies, waits for them, and re-layouts  5.24 us
    dot_general x2, matrix products, block_outer(): dc = dc + jnp.einsum('tgkp,gkpn->tgn', g_grow, S0, precision=EXACT_DOT)  5.13 us
    mul x3, other arithmetic, causal_conv(): result = padded[0:num_tokens] * taps[0].astype(jnp.float32)  4.36 us
  transfers between devices with their start and end apart: 10, of which 1 were waited for; matrix products, arithmetic and copies ran while one was open for 46% of the time, Pallas kernels for 9%

profile of v1, /device:TPU:1, one launch (start us, length us, event | category | flops | bytes accessed | tf_op | source)
XLA Modules:
  0.0 204.5 jit_solution(1017853516453408897)
XLA Ops:
  2.8 1.4 compare_select_fusion.7
  4.8 2.7 %collective-permute-start.1 = (f32[7712]{0:T(1024)S(1)}, f32[7712]{0:T(1024)}, u32[]{:S(2)}, u32[]{:S(2)}) collective-permute-start(f32[7712]{0:T(1024)S(1)} %pad_maximum_fusion.10), channel_id=1, source_target_pairs={{0,8},{4,12},{8,0},{12,4},{1,9},{5,13},{9,1},{13,5},{2,10},{6,14},... | collective-permute-start | bytes 92552 | tf_op jit(solution)/shard_map/ppermute | solution.py:289
  7.6 1.4 collective-permute-start
  11.1 1.4 exponential_multiply_fusion.1
  13.9 1.4 slice_convert_fusion.14
  15.3 1.4 slice_convert_fusion.10
  18.2 1.5 slice_convert_fusion.6
  19.7 1.4 compare_select_fusion.3.srow_ref
  21.8 2.2 %fusion.123.g_ref = f32[128,2048]{1,0:T(8,128)} fusion(bf16[1,128,2048]{2,1,0:T(8,128)(2,1)} %param.30, f32[128]{0:T(128)S(1)} %fusion.119), kind=kLoop, calls=%fused_computation.307 | loop fusion | flops 524288 | bytes 1573376 | tf_op jit(solution)/shard_map/vmap()/squeeze;vmap()/reshape;vmap()/reshape | solution.py:168
  28.1 1.4 copy.184
  36.3 1.6 fusion.126
  38.6 2.5 %multiply_bitcast_fusion = (f32[128,2048]{1,0:T(8,128)}, f32[1,128,2048]{2,1,0:T(8,128)S(1)}) fusion(f32[1,128,2048]{2,1,0:T(8,128)S(1)} %convert_element_type.169, f32[2048]{0:T(1024)} %bitcast.294, f32[2048]{0:T(1024)} %bitcast.290, f32[1,3,2048]{2,1,0:T(4,128)} %slice_bitcast_fusion.5, f32[2048]{0:T(1024)} %bitcast.286, f32[2048]{0:T(1024)} %bitcast.282), kind=kLoop, calls=%fused_computation.74 | loop fusion | flops 3670016 | bytes 3203072 | tf_op jit(solution)/shard_map/vmap()/squeeze;vmap()/reshape;vmap()/reshape | solution.py:168
  41.2 18.3 %vmap__.1 = (f32[128,2048]{1,0:T(8,128)}, f32[16,2,128]{2,1,0:T(2,128)}, f32[16,2,128]{2,1,0:T(2,128)}, f32[2,128,128]{2,1,0:T(8,128)}) custom-call(f32[128,2048]{1,0:T(8,128)} %get-tuple-element.53.x_ref, f32[128,2048]{1,0:T(8,128)} %fusion.123.g_ref, f32[128,256]{1,0:T(8,128)} %get-tuple-element.124.b_ref, f32[128,256]{1,0:T(8,128)} %get-tuple-element.49.c_ref, ...), custom_call_target="tpu_custom_call" | custom-call | tf_op jit(solution)/shard_map/vmap()/pallas_call | solution.py:168
  59.5 3.5 %broadcast_multiply_fusion = (f32[1,128,2048]{2,1,0:T(8,128)}, f32[1,128,2048]{2,1,0:T(8,128)}, f32[1,128,2048]{2,1,0:T(8,128)}) fusion(f32[2048]{0:T(1024)S(1)} %bitcast.297, f32[1,128,2048]{2,1,0:T(8,128)S(1)} %get-tuple-element.54, bf16[1,128,2048]{2,1,0:T(8,128)(2,1)S(1)} %copy-done.17, f32[128]{0:T(128)S(1)} %copy-done.101, f32[2048]{0:T(1024)S(1)} %copy-done.72, ...), kind=kLoop, calls=%fused_computation.89 | loop fusion | flops 3670016 | bytes 5784064 | tf_op jit(solution)/shard_map/vmap(transpose(jvp()))/mul | solution.py:52
  63.0 1.6 copy.174
  64.6 2.8 %fusion.36 = (f32[128,2048]{1,0:T(8,128)}, f32[128,2048]{1,0:T(8,128)}) fusion(f32[128,2048]{1,0:T(8,128)S(1)} %copy-done.12, f32[2048]{0:T(1024)} %bitcast.295, f32[2048]{0:T(1024)} %bitcast.291, f32[3,2048]{1,0:T(4,128)} %slice.288, f32[2048]{0:T(1024)} %bitcast.287, f32[2048]{0:T(1024)} %bitcast.283), kind=kLoop, calls=%fused_computation.85 | loop fusion | flops 3670016 | bytes 3203072 | tf_op jit(solution)/shard_map/jvp(jit(silu))/mul | solution.py:55
  67.5 1.5 copy.171
  69.0 1.8 convolution_bitcast_fusion.4
  73.0 2.0 pad_maximum_fusion
  75.0 2.1 %convert_element_type.163.g_ref = f32[128,2048]{1,0:T(8,128)} convert(bf16[128,2048]{1,0:T(8,128)(2,1)} %param.25) | non-fusion elementwise | flops 262144 | bytes 1572864 | tf_op jit(solution)/shard_map/convert_element_type | solution.py:314
  78.5 1.6 negate_multiply_fusion
  80.1 1.6 copy.162
  81.7 1.3 reduce_window_sum.47
  83.6 1.4 copy.230
  85.0 1.4 exponential_bitcast_fusion
  86.4 1.5 copy.168
  87.8 1.3 copy.163
  89.7 1.3 fusion.141
  90.9 1.3 reduce_sum.91
  92.2 1.3 fusion.144
  94.0 1.3 mul.920
  96.5 1.3 exp.141
  97.8 1.3 mul.898
  99.1 1.4 reshape.535
  100.5 1.9 fusion.97
  102.4 1.7 copy.220
  104.8 3.7 %broadcast_select_fusion.1 = (f32[3,2,16,64,128]{4,3,2,1,0:T(8,128)S(1)}, f32[3,2,16,64,128]{4,3,2,1,0:T(8,128)S(1)}) fusion(f32[3,2,16,64,128]{4,3,2,1,0:T(8,128)} %collective-permute-done.3, pred[]{:T(512)S(6)} %eq.58, f32[1,2,16,64,128]{4,3,2,1,0:T(8,128)} %copy-done.9, f32[1,2,16,64,128]{4,3,2,1,0:T(8,128)} %copy-done.8, f32[1,2,16,64,128]{4,3,2,1,0:T(8,128)} %copy-done.10), kind=kLoop, calls=%fused_computation.9 | loop fusion | flops 3145728 | bytes 12582913 | tf_op jit(solution)/shard_map/jit(_where)/select_n | solution.py:374
  108.6 2.2 %fusion.30 = (f32[2,16,64,128]{3,2,1,0:T(8,128)}, f32[2,16,64,128]{3,2,1,0:T(8,128)}) fusion(f32[3,2,16,64,128]{4,3,2,1,0:T(8,128)S(1)} %get-tuple-element.70, f32[3,2,16,64,128]{4,3,2,1,0:T(8,128)S(1)} %get-tuple-element.69, f32[2,16]{1,0:T(2,128)S(1)} %copy-done.107, f32[2,16]{1,0:T(2,128)S(1)} %get-tuple-element.111, pred[]{:T(512)S(6)} %ge.27, ...), kind=kLoop, calls=%fused_computation.63 | loop fusion | flops 2359296 | bytes 8388994 | tf_op jit(solution)/shard_map/jit(_where)/select_n | solution.py:388
  112.9 1.7 copy.221
  117.8 18.2 %shard_map.242 = (f32[128,2048]{1,0:T(8,128)}, f32[16,2,128]{2,1,0:T(2,128)}, f32[16,2,128]{2,1,0:T(2,128)}, f32[2,128,128]{2,1,0:T(8,128)}) custom-call(f32[128,2048]{1,0:T(8,128)} %get-tuple-element.67.x_ref, f32[128,2048]{1,0:T(8,128)} %convert_element_type.163.g_ref, f32[128,256]{1,0:T(8,128)} %copy-done.25, f32[128,256]{1,0:T(8,128)} %copy-done.26, ...), custom_call_target="tpu_custom_call" | custom-call | tf_op jit(solution)/shard_map/pallas_call | solution.py:168
  136.0 2.5 %copy.164 = f32[128,2048]{0,1:T(8,128)} copy(f32[128,2048]{1,0:T(8,128)} %get-tuple-element.28) | data formatting | bytes 2097152 | tf_op jit(solution)/shard_map/pallas_call | solution.py:168
  138.5 1.5 copy.191
  140.0 1.5 copy.194
  141.5 1.7 broadcast_multiply_fusion.1
  145.8 1.6 slice_bitcast_fusion.7
  148.1 3.9 %multiply_reduce_fusion = (f32[2,16]{1,0:T(2,128)}, f32[2,16,64,128]{3,2,1,0:T(8,128)S(1)}, f32[2,16,64,128]{3,2,1,0:T(8,128)}, f32[2,16,64,128]{3,2,1,0:T(8,128)S(1)}) fusion(f32[3,2,16,64,128]{4,3,2,1,0:T(8,128)S(1)} %copy-done.3, f32[2,16]{1,0:T(2,128)S(1)} %copy-done.99, f32[2,16,64,128]{3,2,1,0:T(8,128)S(1)} %copy-done.15, ...), kind=kLoop, calls=%fused_computation.71 | loop fusion | flops 6553568 | bytes 10486407 | tf_op jit(solution)/shard_map/reduce_sum | solution.py:222
  151.9 1.7 fusion.3
  153.6 2.6 %convolution_bitcast_fusion.9 = f32[2,128,128]{2,1,0:T(8,128)} fusion(f32[2,16,64,128]{3,2,1,0:T(8,128)S(1)} %get-tuple-element.41, f32[128,2,16,64]{0,3,2,1:T(8,128)S(1)} %bitcast.254, f32[128,2,16]{0,2,1:T(8,128)S(1)} %copy-done.57), kind=kOutput, calls=%fused_computation.24 | convolution fusion | flops 402915328 | bytes 2244608 | tf_op jit(solution)/shard_map/tgkp,gkpn->tgn/dot_general | solution.py:211
  156.2 2.6 %fusion.5 = f32[1,128,2,128]{1,3,2,0:T(8,128)} fusion(f32[1,128,2,128]{1,3,2,0:T(8,128)S(1)} %convolution_bitcast_fusion.6, f32[2,16,64,128]{3,2,1,0:T(8,128)S(1)} %get-tuple-element.71, f32[128,2,16,64]{0,3,2,1:T(8,128)S(1)} %bitcast.258, f32[128,2,16]{0,2,1:T(8,128)S(1)} %copy-done.49), kind=kOutput, calls=%fused_computation.27 | convolution fusion | flops 402948096 | bytes 2375680 | tf_op jit(solution)/shard_map/vmap(tgkp,gkpn->tgn)/dot_general | solution.py:211
  158.8 1.7 copy.222
  163.6 3.6 %collective-permute-start.8 = (f32[3,2560]{1,0:T(4,128)}, f32[3,2560]{1,0:T(4,128)}, u32[]{:S(2)}, u32[]{:S(2)}) collective-permute-start(f32[3,2560]{1,0:T(4,128)} %pad_maximum_fusion.9), channel_id=1, source_target_pairs={{4,12},{5,13},{6,14},{7,15},{20,28},{21,29},{22,30},{23,31}} | collective-permute-start | bytes 92168 | tf_op jit(solution)/shard_map/ppermute | solution.py:442
  167.2 1.3 collective-permute-start.9
  168.5 1.3 collective-permute-start.7
  169.7 2.0 multiply_reduce_fusion.1
  171.8 1.7 fusion.110
  174.9 2.7 %multiply_add_fusion = f32[128,2,16,64]{0,3,2,1:T(8,128)} fusion(f32[128,2,16,64]{0,3,2,1:T(8,128)} %get-tuple-element.123, f32[128,2,16,64]{0,3,2,1:T(8,128)} %bitcast.260, f32[128,2,16]{0,2,1:T(8,128)} %copy.170, f32[2,16]{1,0:T(2,128)} %copy-done.102, f32[128,2048]{0,1:T(8,128)S(1)} %copy.165), kind=kLoop, calls=%fused_computation.79 | loop fusion | flops 1048576 | bytes 4210816 | tf_op jit(solution)/shard_map/add | solution.py:217
  177.6 2.6 %copy.177 = f32[128,2048]{1,0:T(8,128)} copy(f32[128,2048]{0,1:T(8,128)} %bitcast.261) | data formatting | bytes 2097152 | tf_op jit(solution)/shard_map/reshape | solution.py:431
  180.3 1.7 broadcast_multiply_fusion.4
  183.0 1.4 pad_add_fusion.1
  184.5 1.7 fusion.2
  189.0 1.5 exponential_multiply_fusion
  192.4 1.8 convolution_bitcast_fusion.10
  196.0 2.4 %collective-permute-start.6 = (f32[3,2560]{1,0:T(4,128)S(1)}, f32[3,2560]{1,0:T(4,128)S(1)}, u32[]{:S(2)}, u32[]{:S(2)}) collective-permute-start(f32[3,2560]{1,0:T(4,128)S(1)} %pad_maximum_fusion.8), channel_id=1, source_target_pairs={{4,0},{8,4},{12,8},{5,1},{9,5},{13,9},{6,2},{10,6},{14,10},{7,3},{... | collective-permute-start | bytes 92168 | tf_op jit(solution)/shard_map/ppermute | solution.py:21
  199.1 1.5 split.68
  (344 shorter events, 50.3 us)
Async XLA Ops:
  2.8 21.7 %copy-start.61 = (bf16[128,256]{1,0:T(8,128)(2,1)S(1)}, bf16[128,256]{1,0:T(8,128)(2,1)}, u32[]{:S(2)}) copy-start(bf16[128,256]{1,0:T(8,128)(2,1)} %param.22) | copy-start | bytes 196612
  4.7 19.8 %copy-start.62 = (bf16[128,256]{1,0:T(8,128)(2,1)S(1)}, bf16[128,256]{1,0:T(8,128)(2,1)}, u32[]{:S(2)}) copy-start(bf16[128,256]{1,0:T(8,128)(2,1)} %param.23) | copy-start | bytes 196612
  4.8 24.8 %collective-permute-start.2 = (f32[7712]{0:T(1024)S(1)}, f32[7712]{0:T(1024)}, u32[]{:S(2)}, u32[]{:S(2)}) collective-permute-start(f32[7712]{0:T(1024)S(1)} %pad_maximum_fusion.10), channel_id=1, source_target_pairs={{0,12},{4,0},{8,4},{12,8},{1,13},{5,1},{9,5},{13,9},{2,14},{6,2},{... | collective-permute-start | bytes 92552 | tf_op jit(solution)/shard_map/ppermute | solution.py:289
  4.8 25.5 %collective-permute-start.1 = (f32[7712]{0:T(1024)S(1)}, f32[7712]{0:T(1024)}, u32[]{:S(2)}, u32[]{:S(2)}) collective-permute-start(f32[7712]{0:T(1024)S(1)} %pad_maximum_fusion.10), channel_id=1, source_target_pairs={{0,8},{4,12},{8,0},{12,4},{1,9},{5,13},{9,1},{13,5},{2,10},{6,14},... | collective-permute-start | bytes 92552 | tf_op jit(solution)/shard_map/ppermute | solution.py:289
  7.6 23.6 %collective-permute-start = (f32[7712]{0:T(1024)S(1)}, f32[7712]{0:T(1024)}, u32[]{:S(2)}, u32[]{:S(2)}) collective-permute-start(f32[7712]{0:T(1024)S(1)} %pad_maximum_fusion.10), channel_id=1, source_target_pairs={{0,4},{4,8},{8,12},{12,0},{1,5},{5,9},{9,13},{13,1},{2,6},{6,10},{... | collective-permute-start | bytes 92552 | tf_op jit(solution)/shard_map/ppermute | solution.py:289
  9.6 14.9 %copy-start.92 = (f32[2,16]{1,0:T(2,128)}, f32[2,16]{1,0:T(2,128)S(1)}, u32[]{:S(2)}) copy-start(f32[2,16]{1,0:T(2,128)S(1)} %mul.862) | copy-start | bytes 388
  15.3 19.0 %copy-start.73 = (f32[1,256]{1,0:T(1,128)}, f32[1,256]{1,0:T(1,128)S(1)}, u32[]{:S(2)}) copy-start(f32[1,256]{1,0:T(1,128)S(1)} %get-tuple-element.112) | copy-start | bytes 3076
  15.3 19.0 %copy-start.76 = (f32[1,256]{1,0:T(1,128)}, f32[1,256]{1,0:T(1,128)S(1)}, u32[]{:S(2)}) copy-start(f32[1,256]{1,0:T(1,128)S(1)} %get-tuple-element.113) | copy-start | bytes 3076
  17.5 7.0 %copy-start.28 = (bf16[128,2048]{1,0:T(8,128)(2,1)S(1)}, bf16[128,2048]{1,0:T(8,128)(2,1)}, u32[]{:S(2)}) copy-start(bf16[128,2048]{1,0:T(8,128)(2,1)} %param.21) | copy-start | bytes 1572868
  18.1 9.9 %copy-start.50 = (f32[1,2,16,128]{3,2,1,0:T(8,128)}, f32[1,2,16,128]{3,2,1,0:T(8,128)S(1)}, u32[]{:S(2)}) copy-start(f32[1,2,16,128]{3,2,1,0:T(8,128)S(1)} %reduce_window_sum.48) | copy-start | bytes 49156
  18.2 52.6 %copy-start.48 = (f32[128,2,16]{0,2,1:T(8,128)}, f32[128,2,16]{0,2,1:T(8,128)S(1)}, u32[]{:S(2)}) copy-start(f32[128,2,16]{0,2,1:T(8,128)S(1)} %exponential_bitcast_fusion.1) | copy-start | bytes 49156
  21.8 3.9 %copy-start.100 = (f32[128]{0:T(128)}, f32[128]{0:T(128)S(1)}, u32[]{:S(2)}) copy-start(f32[128]{0:T(128)S(1)} %fusion.119) | copy-start | bytes 1540
  25.8 3.7 %copy-start.102 = (f32[2,16]{1,0:T(2,128)}, f32[2,16]{1,0:T(2,128)S(1)}, u32[]{:S(2)}) copy-start(f32[2,16]{1,0:T(2,128)S(1)} %mul.865) | copy-start | bytes 388
  35.3 3.3 %copy-start.20 = (f32[128,256]{1,0:T(8,128)}, f32[128,256]{1,0:T(8,128)S(1)}, u32[]{:S(2)}) copy-start(f32[128,256]{1,0:T(8,128)S(1)} %get-tuple-element.127) | copy-start | bytes 393220
  41.2 18.3 %copy-start.17 = (bf16[1,128,2048]{2,1,0:T(8,128)(2,1)S(1)}, bf16[1,128,2048]{2,1,0:T(8,128)(2,1)}, u32[]{:S(2)}) copy-start(bf16[1,128,2048]{2,1,0:T(8,128)(2,1)} %param.30) | copy-start | bytes 1572868
  41.2 18.3 %copy-start.56 = (f32[1,2048]{1,0:T(1,128)S(1)}, f32[1,2048]{1,0:T(1,128)}, u32[]{:S(2)}) copy-start(f32[1,2048]{1,0:T(1,128)} %get-tuple-element.108) | copy-start | bytes 24580
  41.2 18.3 %copy-start.72 = (f32[2048]{0:T(1024)S(1)}, f32[2048]{0:T(1024)}, u32[]{:S(2)}) copy-start(f32[2048]{0:T(1024)} %mul.952) | copy-start | bytes 24580
  41.2 18.3 %copy-start.101 = (f32[128]{0:T(128)S(1)}, f32[128]{0:T(128)}, u32[]{:S(2)}) copy-start(f32[128]{0:T(128)} %copy-done.100) | copy-start | bytes 1540
  75.0 29.8 %collective-permute-start.3 = (f32[3,2,16,64,128]{4,3,2,1,0:T(8,128)}, f32[3,2,16,64,128]{4,3,2,1,0:T(8,128)}, u32[]{:S(2)}, u32[]{:S(2)}) collective-permute-start(f32[3,2,16,64,128]{4,3,2,1,0:T(8,128)} %pad_maximum_fusion), channel_id=1, source_target_pairs={{0,4},{4,0},{8,12},{12,8},{1,5},{5,1},{9,13},{13,9},{2,6},{6,2},{1... | collective-permute-start | bytes 9437192 | tf_op jit(solution)/shard_map/ppermute | solution.py:372
  82.9 25.6 %copy-start.43 = (f32[2,16,128]{2,1,0:T(8,128)}, f32[2,16,128]{2,1,0:T(8,128)S(1)}, u32[]{:S(2)}) copy-start(f32[2,16,128]{2,1,0:T(8,128)S(1)} %reduce_window_sum.47) | copy-start | bytes 49156
  104.8 3.7 %copy-start.96 = (f32[2,16]{1,0:T(2,128)}, f32[2,16]{1,0:T(2,128)S(1)}, u32[]{:S(2)}) copy-start(f32[2,16]{1,0:T(2,128)S(1)} %get-tuple-element.110) | copy-start | bytes 388
  104.8 3.8 %copy-start.98 = (f32[2,16]{1,0:T(2,128)}, f32[2,16]{1,0:T(2,128)S(1)}, u32[]{:S(2)}) copy-start(f32[2,16]{1,0:T(2,128)S(1)} %get-tuple-element.111) | copy-start | bytes 388
  104.8 3.8 %copy-start.107 = (f32[2,16]{1,0:T(2,128)S(1)}, f32[2,16]{1,0:T(2,128)}, u32[]{:S(2)}) copy-start(f32[2,16]{1,0:T(2,128)} %exp.141) | copy-start | bytes 388
  108.5 3.5 %copy-start.31 = (f32[1,128,256]{2,1,0:T(8,128)S(1)}, f32[1,128,256]{2,1,0:T(8,128)}, u32[]{:S(2)}) copy-start(f32[1,128,256]{2,1,0:T(8,128)} %get-tuple-element.125) | copy-start | bytes 393220
  108.6 3.5 %copy-start.37 = (f32[1,128,256]{2,1,0:T(8,128)S(1)}, f32[1,128,256]{2,1,0:T(8,128)}, u32[]{:S(2)}) copy-start(f32[1,128,256]{2,1,0:T(8,128)} %copy.220) | copy-start | bytes 393220
  108.6 3.5 %copy-start.83 = (f32[1,256]{1,0:T(1,128)S(1)}, f32[1,256]{1,0:T(1,128)}, u32[]{:S(2)}) copy-start(f32[1,256]{1,0:T(1,128)} %get-tuple-element.114) | copy-start | bytes 3076
  108.6 6.0 %copy-start.74 = (f32[1,256]{1,0:T(1,128)S(1)}, f32[1,256]{1,0:T(1,128)}, u32[]{:S(2)}) copy-start(f32[1,256]{1,0:T(1,128)} %copy-done.73) | copy-start | bytes 3076
  108.6 6.0 %copy-start.77 = (f32[1,256]{1,0:T(1,128)S(1)}, f32[1,256]{1,0:T(1,128)}, u32[]{:S(2)}) copy-start(f32[1,256]{1,0:T(1,128)} %copy-done.76) | copy-start | bytes 3076
  108.6 6.0 %copy-start.80 = (f32[1,256]{1,0:T(1,128)S(1)}, f32[1,256]{1,0:T(1,128)}, u32[]{:S(2)}) copy-start(f32[1,256]{1,0:T(1,128)} %get-tuple-element.115) | copy-start | bytes 3076
  111.7 31.4 %collective-permute-start.4 = (f32[2,16,64,128]{3,2,1,0:T(8,128)}, f32[2,16,64,128]{3,2,1,0:T(8,128)}, u32[]{:S(2)}, u32[]{:S(2)}) collective-permute-start(f32[2,16,64,128]{3,2,1,0:T(8,128)} %get-tuple-element.65), channel_id=1, source_target_pairs={{0,8},{4,12},{8,0},{12,4},{1,9},{5,13},{9,1},{13,5},{2,10},{6,14},... | collective-permute-start | bytes 3145736 | tf_op jit(solution)/shard_map/ppermute | solution.py:392
  136.0 5.5 %copy-start.51 = (f32[1,2048]{1,0:T(1,128)S(1)}, f32[1,2048]{1,0:T(1,128)}, u32[]{:S(2)}) copy-start(f32[1,2048]{1,0:T(1,128)} %get-tuple-element.106) | copy-start | bytes 24580
  136.0 5.5 %copy-start.53 = (f32[1,2048]{1,0:T(1,128)S(1)}, f32[1,2048]{1,0:T(1,128)}, u32[]{:S(2)}) copy-start(f32[1,2048]{1,0:T(1,128)} %get-tuple-element.107) | copy-start | bytes 24580
  141.5 3.9 %copy-start.30 = (f32[2,128,128]{2,1,0:T(8,128)S(1)}, f32[2,128,128]{2,1,0:T(8,128)}, u32[]{:S(2)}) copy-start(f32[2,128,128]{2,1,0:T(8,128)} %get-tuple-element.31) | copy-start | bytes 393220
  141.5 3.9 %copy-start.36 = (f32[1,128,256]{1,2,0:T(8,128)S(1)}, f32[1,128,256]{1,2,0:T(8,128)}, u32[]{:S(2)}) copy-start(f32[1,128,256]{1,2,0:T(8,128)} %copy.221) | copy-start | bytes 393220
  141.5 6.5 %copy-start.15 = (f32[2,16,64,128]{3,2,1,0:T(8,128)S(1)}, f32[2,16,64,128]{3,2,1,0:T(8,128)}, u32[]{:S(2)}) copy-start(f32[2,16,64,128]{3,2,1,0:T(8,128)} %get-tuple-element.66) | copy-start | bytes 3145732
  143.2 4.8 %collective-permute-start.5 = (f32[2,16,64,128]{3,2,1,0:T(8,128)}, f32[2,16,64,128]{3,2,1,0:T(8,128)S(1)}, u32[]{:S(2)}, u32[]{:S(2)}) collective-permute-start(f32[2,16,64,128]{3,2,1,0:T(8,128)} %collective-permute-done.4), channel_id=1, source_target_pairs={{0,4},{4,0},{8,12},{12,8},{1,5},{5,1},{9,13},{13,9},{2,6},{6,2},{1... | collective-permute-start | bytes 3145736 | tf_op jit(solution)/shard_map/ppermute | solution.py:393
  144.0 4.0 %copy-start.1 = (f32[3,2,16,64,128]{4,3,2,1,0:T(8,128)S(1)}, f32[3,2,16,64,128]{4,3,2,1,0:T(8,128)}, u32[]{:S(2)}) copy-start(f32[3,2,16,64,128]{4,3,2,1,0:T(8,128)} %copy-done) | copy-start | bytes 9437188
  144.0 4.0 %copy-start.3 = (f32[3,2,16,64,128]{4,3,2,1,0:T(8,128)S(1)}, f32[3,2,16,64,128]{4,3,2,1,0:T(8,128)}, u32[]{:S(2)}) copy-start(f32[3,2,16,64,128]{4,3,2,1,0:T(8,128)} %copy-done.2) | copy-start | bytes 9437188
  144.4 3.6 %copy-start.97 = (f32[2,16]{1,0:T(2,128)S(1)}, f32[2,16]{1,0:T(2,128)}, u32[]{:S(2)}) copy-start(f32[2,16]{1,0:T(2,128)} %copy-done.96) | copy-start | bytes 388
  144.4 3.6 %copy-start.99 = (f32[2,16]{1,0:T(2,128)S(1)}, f32[2,16]{1,0:T(2,128)}, u32[]{:S(2)}) copy-start(f32[2,16]{1,0:T(2,128)} %copy-done.98) | copy-start | bytes 388
  144.5 3.6 %copy-start.105 = (f32[2,16]{1,0:T(2,128)S(1)}, f32[2,16]{1,0:T(2,128)}, u32[]{:S(2)}) copy-start(f32[2,16]{1,0:T(2,128)} %mul.920) | copy-start | bytes 388
  144.5 3.6 %copy-start.106 = (f32[2,16]{1,0:T(2,128)S(1)}, f32[2,16]{1,0:T(2,128)}, u32[]{:S(2)}) copy-start(f32[2,16]{1,0:T(2,128)} %mul.898) | copy-start | bytes 388
  148.0 3.9 %copy-start.57 = (f32[128,2,16]{0,2,1:T(8,128)S(1)}, f32[128,2,16]{0,2,1:T(8,128)}, u32[]{:S(2)}) copy-start(f32[128,2,16]{0,2,1:T(8,128)} %get-tuple-element.102) | copy-start | bytes 49156
  151.9 4.2 %copy-start.6 = (f32[2,16,64,128]{3,2,1,0:T(8,128)}, f32[2,16,64,128]{3,2,1,0:T(8,128)S(1)}, u32[]{:S(2)}) copy-start(f32[2,16,64,128]{3,2,1,0:T(8,128)S(1)} %get-tuple-element.71) | copy-start | bytes 3145732
  156.2 4.2 %copy-start.23 = (f32[1,128,256]{2,1,0:T(8,128)S(1)}, f32[1,128,256]{2,1,0:T(8,128)}, u32[]{:S(2)}) copy-start(f32[1,128,256]{2,1,0:T(8,128)} %copy-done.22) | copy-start | bytes 393220
  160.4 9.3 %copy-start.4 = (f32[2,16,64,128]{3,2,1,0:T(8,128)S(1)}, f32[2,16,64,128]{3,2,1,0:T(8,128)}, u32[]{:S(2)}) copy-start(f32[2,16,64,128]{3,2,1,0:T(8,128)} %get-tuple-element.42) | copy-start | bytes 3145732
  162.9 6.8 %copy-start.70 = (f32[3,256]{1,0:T(4,128)}, f32[3,256]{1,0:T(4,128)S(1)}, u32[]{:S(2)}) copy-start(f32[3,256]{1,0:T(4,128)S(1)} %slice_bitcast_fusion.6) | copy-start | bytes 9220
  163.6 37.1 %collective-permute-start.8 = (f32[3,2560]{1,0:T(4,128)}, f32[3,2560]{1,0:T(4,128)}, u32[]{:S(2)}, u32[]{:S(2)}) collective-permute-start(f32[3,2560]{1,0:T(4,128)} %pad_maximum_fusion.9), channel_id=1, source_target_pairs={{4,12},{5,13},{6,14},{7,15},{20,28},{21,29},{22,30},{23,31}} | collective-permute-start | bytes 92168 | tf_op jit(solution)/shard_map/ppermute | solution.py:442
  167.2 33.5 %collective-permute-start.9 = (f32[3,2560]{1,0:T(4,128)}, f32[3,2560]{1,0:T(4,128)}, u32[]{:S(2)}, u32[]{:S(2)}) collective-permute-start(f32[3,2560]{1,0:T(4,128)} %pad_maximum_fusion.9), channel_id=1, source_target_pairs={{8,12},{9,13},{10,14},{11,15},{24,28},{25,29},{26,30},{27,31}} | collective-permute-start | bytes 92168 | tf_op jit(solution)/shard_map/ppermute | solution.py:442
  168.5 32.2 %collective-permute-start.7 = (f32[3,2560]{1,0:T(4,128)}, f32[3,2560]{1,0:T(4,128)}, u32[]{:S(2)}, u32[]{:S(2)}) collective-permute-start(f32[3,2560]{1,0:T(4,128)} %pad_maximum_fusion.9), channel_id=1, source_target_pairs={{0,12},{1,13},{2,14},{3,15},{16,28},{17,29},{18,30},{19,31}} | collective-permute-start | bytes 92168 | tf_op jit(solution)/shard_map/ppermute | solution.py:442
  186.1 4.4 %copy-start.21 = (f32[128,256]{1,0:T(8,128)S(1)}, f32[128,256]{1,0:T(8,128)}, u32[]{:S(2)}) copy-start(f32[128,256]{1,0:T(8,128)} %copy-done.20) | copy-start | bytes 393220
  186.1 5.2 %copy-start.63 = (f32[128,2,16]{0,2,1:T(8,128)S(1)}, f32[128,2,16]{0,2,1:T(8,128)}, u32[]{:S(2)}) copy-start(f32[128,2,16]{0,2,1:T(8,128)} %fusion.3) | copy-start | bytes 49156
  186.1 5.3 %copy-start.86 = (f32[1,256]{1,0:T(1,128)S(1)}, f32[1,256]{1,0:T(1,128)}, u32[]{:S(2)}) copy-start(f32[1,256]{1,0:T(1,128)} %get-tuple-element.116) | copy-start | bytes 3076
  186.1 5.3 %copy-start.88 = (f32[1,256]{1,0:T(1,128)S(1)}, f32[1,256]{1,0:T(1,128)}, u32[]{:S(2)}) copy-start(f32[1,256]{1,0:T(1,128)} %get-tuple-element.117) | copy-start | bytes 3076
  186.1 5.3 %copy-start.90 = (f32[1,256]{1,0:T(1,128)S(1)}, f32[1,256]{1,0:T(1,128)}, u32[]{:S(2)}) copy-start(f32[1,256]{1,0:T(1,128)} %get-tuple-element.119) | copy-start | bytes 3076
  186.2 5.3 %copy-start.33 = (f32[2,16,128]{1,0,2:T(2,128)S(1)}, f32[2,16,128]{1,0,2:T(2,128)}, u32[]{:S(2)}) copy-start(f32[2,16,128]{1,0,2:T(2,128)} %copy.194) | copy-start | bytes 49156
  186.7 5.0 %copy-start.95 = (f32[2,16,1]{1,0,2:T(2,128)S(1)}, f32[2,16,1]{1,0,2:T(2,128)}, u32[]{:S(2)}) copy-start(f32[2,16,1]{1,0,2:T(2,128)} %copy.230) | copy-start | bytes 388
  186.7 5.0 %copy-start.103 = (f32[2,16]{1,0:T(2,128)S(1)}, f32[2,16]{1,0:T(2,128)}, u32[]{:S(2)}) copy-start(f32[2,16]{1,0:T(2,128)} %get-tuple-element.40) | copy-start | bytes 388
  186.7 5.0 %copy-start.104 = (f32[2,16]{1,0:T(2,128)S(1)}, f32[2,16]{1,0:T(2,128)}, u32[]{:S(2)}) copy-start(f32[2,16]{1,0:T(2,128)} %get-tuple-element.38) | copy-start | bytes 388
  195.4 6.0 %copy-start.47 = (f32[3,2048]{1,0:T(4,128)S(1)}, f32[3,2048]{1,0:T(4,128)}, u32[]{:S(2)}) copy-start(f32[3,2048]{1,0:T(4,128)} %slice_bitcast_fusion.4) | copy-start | bytes 73732
  195.4 6.0 %copy-start.69 = (f32[3,256]{1,0:T(4,128)S(1)}, f32[3,256]{1,0:T(4,128)}, u32[]{:S(2)}) copy-start(f32[3,256]{1,0:T(4,128)} %slice_bitcast_fusion.7) | copy-start | bytes 9220
  195.4 5.9 %copy-start.71 = (f32[3,256]{1,0:T(4,128)S(1)}, f32[3,256]{1,0:T(4,128)}, u32[]{:S(2)}) copy-start(f32[3,256]{1,0:T(4,128)} %copy-done.70) | copy-start | bytes 9220
  195.6 8.0 %copy-start.11 = (f32[131,2048]{1,0:T(8,128)S(1)}, f32[131,2048]{1,0:T(8,128)}, u32[]{:S(2)}) copy-start(f32[131,2048]{1,0:T(8,128)} %pad_add_fusion.1) | copy-start | bytes 3219460
  196.0 5.3 %collective-permute-start.6 = (f32[3,2560]{1,0:T(4,128)S(1)}, f32[3,2560]{1,0:T(4,128)S(1)}, u32[]{:S(2)}, u32[]{:S(2)}) collective-permute-start(f32[3,2560]{1,0:T(4,128)S(1)} %pad_maximum_fusion.8), channel_id=1, source_target_pairs={{4,0},{8,4},{12,8},{5,1},{9,5},{13,9},{6,2},{10,6},{14,10},{7,3},{... | collective-permute-start | bytes 92168 | tf_op jit(solution)/shard_map/ppermute | solution.py:21
  (56 other events, 110.6 us)

commit v2 on v1

--- a/solution.py
+++ b/solution.py
@@ -6,10 +6,10 @@
 from jax.experimental import pallas as pl
 from jax.sharding import PartitionSpec as P
 
+
 HD = 64
 N = 128
 KW = 4
-Q = 128
 
 
 EXACT_DOT = lax.Precision.HIGHEST
@@ -19,29 +19,6 @@
     devices = range(lax.axis_size(axis))
     route = [(i - distance, i) for i in devices if i - distance in devices]
     return lax.ppermute(block, axis, route)
-
-
-def prefix(shard, axis, combine, identity, reverse):
-    length, here = (lax.axis_size(axis), lax.axis_index(axis))
-    everything = jax.tree.map(lambda part: lax.all_gather(part, axis), shard)
-    start = jax.tree.map(
-        lambda part, zero: jnp.broadcast_to(jnp.asarray(zero, part.dtype), part.shape),
-        shard,
-        identity,
-    )
-
-    def lap(k, before):
-        at = length - 1 - k if reverse else k
-        reached = at > here if reverse else at < here
-        new = combine(before, jax.tree.map(lambda part: part[at], everything))
-        return jax.tree.map(lambda a, b: jnp.where(reached, a, b), new, before)
-
-    return lax.fori_loop(0, length, lap, start)
-
-
-def spread(block, axis, holder):
-    block = jnp.where(lax.axis_index(axis) == holder, block, jnp.zeros_like(block))
-    return lax.psum(block, axis)
 
 
 def causal_conv(values, context, taps):
@@ -53,61 +30,6 @@
             jnp.float32
         )
     return jax.nn.silu(result)
-
-
-def run_scan(x_act, b_act, c_act, step_dt, decay_rates, skip_gain, start_state):
-    tokens = x_act.shape[0]
-    num_heads = x_act.shape[1]
-    num_groups = b_act.shape[1]
-    per_group = num_heads // num_groups
-    blocks = tokens // Q
-    x_blocks = x_act.reshape(blocks, Q, num_groups, per_group, HD)
-    b_blocks = b_act.reshape(blocks, Q, num_groups, N)
-    c_blocks = c_act.reshape(blocks, Q, num_groups, N)
-    log_decay = (
-        (-step_dt * decay_rates[:, None])
-        .reshape(num_groups, per_group, blocks, Q)
-        .transpose(2, 0, 1, 3)
-    )
-    dt_blocks = step_dt.reshape(num_groups, per_group, blocks, Q).transpose(2, 0, 1, 3)
-    lower_tri = jnp.arange(Q)[:, None] >= jnp.arange(Q)[None, :]
-    skip_shaped = skip_gain.reshape(num_groups, per_group)[:, :, None]
-
-    def advance(current, pieces):
-        x_block, b_block, c_block, log_block, dt_block = pieces
-        cumulative = jnp.cumsum(log_block, axis=-1)
-        log_gaps = cumulative[..., :, None] - cumulative[..., None, :]
-        within = jnp.where(lower_tri, jnp.exp(jnp.where(lower_tri, log_gaps, 0.0)), 0.0)
-        scores = jnp.einsum("tgn,sgn->gts", c_block, b_block, precision=EXACT_DOT)
-        mixing = scores[:, None] * within * dt_block[:, :, None, :]
-        inner_out = jnp.einsum("gkts,sgkp->tgkp", mixing, x_block, precision=EXACT_DOT)
-        carried = jnp.einsum("tgn,gkpn->tgkp", c_block, current, precision=EXACT_DOT)
-        carried = carried * jnp.exp(cumulative).transpose(2, 0, 1)[..., None]
-        output = inner_out + carried + skip_shaped * x_block
-        weights = jnp.exp(cumulative[..., -1:] - cumulative) * dt_block
-        updated = current * jnp.exp(cumulative[..., -1])[..., None, None]
-        updated = updated + jnp.einsum(
-            "gks,sgkp,sgn->gkpn", weights, x_block, b_block, precision=EXACT_DOT
-        )
-        return (updated, output)
-
-    last_state, outputs = lax.scan(
-        jax.checkpoint(advance),
-        start_state.reshape(num_groups, per_group, HD, N),
-        (x_blocks, b_blocks, c_blocks, log_decay, dt_blocks),
-    )
-    return (outputs.reshape(tokens, num_heads * HD), last_state.reshape(num_heads, HD, N))
-
-
-def block_forward(x_feat, b_feat, c_feat, dt_raw, left_x, left_b, left_c, start_state, params):
-    conv_x, conv_b, conv_c, decay_rates, dt_offset, skip_gain = params
-    num_heads = decay_rates.shape[0]
-    num_groups = conv_b.shape[1] // N
-    x_act = causal_conv(x_feat, left_x, conv_x).reshape(-1, num_heads, HD)
-    b_act = causal_conv(b_feat, left_b, conv_b).reshape(-1, num_groups, N)
-    c_act = causal_conv(c_feat, left_c, conv_c).reshape(-1, num_groups, N)
-    step_dt = jax.nn.softplus(dt_raw + dt_offset[:, None])
-    return run_scan(x_act, b_act, c_act, step_dt, decay_rates, skip_gain, start_state)
 
 
 def _dot(a, b, dims):
@@ -339,10 +261,11 @@
         return one_step_pullback, conv_pullback, sx, sb, sc, cot, step_g
 
     def suffix_front(*items):
-        unused_a, unused_b, sx, sb, sc, cot, step_g = suffix_parts(*items)
+        _, _, sx, sb, sc, cot, step_g = suffix_parts(*items)
         grow = jnp.exp(jnp.cumsum(-step_g * rate[:, :, None], axis=-1))
         adjoint = jnp.einsum("gkt,tgkp,tgn->gkpn", grow, cot, sc, precision=EXACT_DOT)
-        return adjoint, block_inner(sx, sb, sc, step_g, rate, cot)
+        inner = block_inner(sx, sb, sc, step_g, rate, cot)
+        return adjoint, inner
 
     def suffix_back(end_state, inner, *items):
         one_step_pullback, conv_pullback, sx, sb, sc, cot, step_g = suffix_parts(*items)
@@ -393,6 +316,7 @@
         shared = lax.ppermute(incoming, "suf", [(j, j ^ 1) for j in range(num_ways)])
         got_state.append(jnp.where(core == 0, incoming, shared))
         got_other.append(jnp.where(core == 0, shared, incoming))
+
     def chip_ordered(got):
         ordered = []
         for c in range(num_chips):

time: 207 us -> 207 us (level)
  no operation moved by 1% of the time
where the time goes in v2:
time: 207 us; the launch traced here: 205 us
  other arithmetic  74.7 us (36%)
  local copies, waits for them, and re-layouts  56.2 us (27%)
  Pallas kernels  36.5 us (18%)
  matrix products  19.2 us (9%)
  starting transfers between devices  13.9 us (7%)
  between operations  3.44 us (2%)
    pallas_call x2, Pallas kernels, block_inner(): pl.pallas_call(functools.partial(_grad_kernel, per_group_pairs), grid=(pa...  36.5 us
    mul x12, other arithmetic, causal_conv(): padded[tap_index:tap_index + num_tokens]  11.7 us
    reshape x3, other arithmetic, block_inner(): pl.pallas_call(functools.partial(_grad_kernel, per_group_pairs), grid=(pa...  6.23 us
    ppermute x3, starting transfers between devices, shards(): lax.ppermute(ctx_grads, 'suf', [(sender, num_ways - 1)])  6.15 us
    unnamed x221, local copies, waits for them, and re-layouts  5.24 us
    dot_general x2, matrix products, block_outer(): dc = dc + jnp.einsum('tgkp,gkpn->tgn', g_grow, S0, precision=EXACT_DOT)  5.13 us
    mul x3, other arithmetic, causal_conv(): result = padded[0:num_tokens] * taps[0].astype(jnp.float32)  4.36 us
  transfers between devices with their start and end apart: 10, of which 1 were waited for; matrix products, arithmetic and copies ran while one was open for 46% of the time, Pallas kernels for 9%

profile of v2, /device:TPU:1, one launch (start us, length us, event | category | flops | bytes accessed | tf_op | source)
XLA Modules:
  0.0 204.5 jit_solution(1017853516453408897)
XLA Ops:
  2.8 1.4 compare_select_fusion.7
  4.8 2.7 %collective-permute-start.1 = (f32[7712]{0:T(1024)S(1)}, f32[7712]{0:T(1024)}, u32[]{:S(2)}, u32[]{:S(2)}) collective-permute-start(f32[7712]{0:T(1024)S(1)} %pad_maximum_fusion.10), channel_id=1, source_target_pairs={{0,8},{4,12},{8,0},{12,4},{1,9},{5,13},{9,1},{13,5},{2,10},{6,14},... | collective-permute-start | bytes 92552 | tf_op jit(solution)/shard_map/ppermute | solution.py:211
  7.6 1.4 collective-permute-start
  11.1 1.4 exponential_multiply_fusion.1
  13.9 1.4 slice_convert_fusion.14
  15.3 1.4 slice_convert_fusion.10
  18.2 1.5 slice_convert_fusion.6
  19.7 1.4 compare_select_fusion.3.srow_ref
  21.8 2.2 %fusion.123.g_ref = f32[128,2048]{1,0:T(8,128)} fusion(bf16[1,128,2048]{2,1,0:T(8,128)(2,1)} %param.30, f32[128]{0:T(128)S(1)} %fusion.119), kind=kLoop, calls=%fused_computation.307 | loop fusion | flops 524288 | bytes 1573376 | tf_op jit(solution)/shard_map/vmap()/squeeze;vmap()/reshape;vmap()/reshape | solution.py:90
  28.1 1.4 copy.184
  36.3 1.6 fusion.126
  38.6 2.5 %multiply_bitcast_fusion = (f32[128,2048]{1,0:T(8,128)}, f32[1,128,2048]{2,1,0:T(8,128)S(1)}) fusion(f32[1,128,2048]{2,1,0:T(8,128)S(1)} %convert_element_type.169, f32[2048]{0:T(1024)} %bitcast.294, f32[2048]{0:T(1024)} %bitcast.290, f32[1,3,2048]{2,1,0:T(4,128)} %slice_bitcast_fusion.5, f32[2048]{0:T(1024)} %bitcast.286, f32[2048]{0:T(1024)} %bitcast.282), kind=kLoop, calls=%fused_computation.74 | loop fusion | flops 3670016 | bytes 3203072 | tf_op jit(solution)/shard_map/vmap()/squeeze;vmap()/reshape;vmap()/reshape | solution.py:90
  41.2 18.3 %vmap__.1 = (f32[128,2048]{1,0:T(8,128)}, f32[16,2,128]{2,1,0:T(2,128)}, f32[16,2,128]{2,1,0:T(2,128)}, f32[2,128,128]{2,1,0:T(8,128)}) custom-call(f32[128,2048]{1,0:T(8,128)} %get-tuple-element.53.x_ref, f32[128,2048]{1,0:T(8,128)} %fusion.123.g_ref, f32[128,256]{1,0:T(8,128)} %get-tuple-element.124.b_ref, f32[128,256]{1,0:T(8,128)} %get-tuple-element.49.c_ref, ...), custom_call_target="tpu_custom_call" | custom-call | tf_op jit(solution)/shard_map/vmap()/pallas_call | solution.py:90
  59.5 3.5 %broadcast_multiply_fusion = (f32[1,128,2048]{2,1,0:T(8,128)}, f32[1,128,2048]{2,1,0:T(8,128)}, f32[1,128,2048]{2,1,0:T(8,128)}) fusion(f32[2048]{0:T(1024)S(1)} %bitcast.297, f32[1,128,2048]{2,1,0:T(8,128)S(1)} %get-tuple-element.54, bf16[1,128,2048]{2,1,0:T(8,128)(2,1)S(1)} %copy-done.17, f32[128]{0:T(128)S(1)} %copy-done.101, f32[2048]{0:T(1024)S(1)} %copy-done.72, ...), kind=kLoop, calls=%fused_computation.89 | loop fusion | flops 3670016 | bytes 5784064 | tf_op jit(solution)/shard_map/vmap(transpose(jvp()))/mul | solution.py:29
  63.0 1.6 copy.174
  64.6 2.8 %fusion.36 = (f32[128,2048]{1,0:T(8,128)}, f32[128,2048]{1,0:T(8,128)}) fusion(f32[128,2048]{1,0:T(8,128)S(1)} %copy-done.12, f32[2048]{0:T(1024)} %bitcast.295, f32[2048]{0:T(1024)} %bitcast.291, f32[3,2048]{1,0:T(4,128)} %slice.288, f32[2048]{0:T(1024)} %bitcast.287, f32[2048]{0:T(1024)} %bitcast.283), kind=kLoop, calls=%fused_computation.85 | loop fusion | flops 3670016 | bytes 3203072 | tf_op jit(solution)/shard_map/jvp(jit(silu))/mul | solution.py:32
  67.5 1.5 copy.171
  69.0 1.8 convolution_bitcast_fusion.4
  73.0 2.0 pad_maximum_fusion
  75.0 2.1 %convert_element_type.163.g_ref = f32[128,2048]{1,0:T(8,128)} convert(bf16[128,2048]{1,0:T(8,128)(2,1)} %param.25) | non-fusion elementwise | flops 262144 | bytes 1572864 | tf_op jit(solution)/shard_map/convert_element_type | solution.py:236
  78.5 1.6 negate_multiply_fusion
  80.1 1.6 copy.162
  81.7 1.3 reduce_window_sum.47
  83.6 1.4 copy.230
  85.0 1.4 exponential_bitcast_fusion
  86.4 1.5 copy.168
  87.8 1.3 copy.163
  89.7 1.3 fusion.141
  90.9 1.3 reduce_sum.91
  92.2 1.3 fusion.144
  94.0 1.3 mul.920
  96.5 1.3 exp.141
  97.8 1.3 mul.898
  99.1 1.4 reshape.535
  100.5 1.9 fusion.97
  102.4 1.7 copy.220
  104.8 3.7 %broadcast_select_fusion.1 = (f32[3,2,16,64,128]{4,3,2,1,0:T(8,128)S(1)}, f32[3,2,16,64,128]{4,3,2,1,0:T(8,128)S(1)}) fusion(f32[3,2,16,64,128]{4,3,2,1,0:T(8,128)} %collective-permute-done.3, pred[]{:T(512)S(6)} %eq.58, f32[1,2,16,64,128]{4,3,2,1,0:T(8,128)} %copy-done.9, f32[1,2,16,64,128]{4,3,2,1,0:T(8,128)} %copy-done.8, f32[1,2,16,64,128]{4,3,2,1,0:T(8,128)} %copy-done.10), kind=kLoop, calls=%fused_computation.9 | loop fusion | flops 3145728 | bytes 12582913 | tf_op jit(solution)/shard_map/jit(_where)/select_n | solution.py:297
  108.6 2.2 %fusion.30 = (f32[2,16,64,128]{3,2,1,0:T(8,128)}, f32[2,16,64,128]{3,2,1,0:T(8,128)}) fusion(f32[3,2,16,64,128]{4,3,2,1,0:T(8,128)S(1)} %get-tuple-element.70, f32[3,2,16,64,128]{4,3,2,1,0:T(8,128)S(1)} %get-tuple-element.69, f32[2,16]{1,0:T(2,128)S(1)} %copy-done.107, f32[2,16]{1,0:T(2,128)S(1)} %get-tuple-element.111, pred[]{:T(512)S(6)} %ge.27, ...), kind=kLoop, calls=%fused_computation.63 | loop fusion | flops 2359296 | bytes 8388994 | tf_op jit(solution)/shard_map/jit(_where)/select_n | solution.py:311
  112.9 1.7 copy.221
  117.8 18.2 %shard_map.242 = (f32[128,2048]{1,0:T(8,128)}, f32[16,2,128]{2,1,0:T(2,128)}, f32[16,2,128]{2,1,0:T(2,128)}, f32[2,128,128]{2,1,0:T(8,128)}) custom-call(f32[128,2048]{1,0:T(8,128)} %get-tuple-element.67.x_ref, f32[128,2048]{1,0:T(8,128)} %convert_element_type.163.g_ref, f32[128,256]{1,0:T(8,128)} %copy-done.25, f32[128,256]{1,0:T(8,128)} %copy-done.26, ...), custom_call_target="tpu_custom_call" | custom-call | tf_op jit(solution)/shard_map/pallas_call | solution.py:90
  136.0 2.5 %copy.164 = f32[128,2048]{0,1:T(8,128)} copy(f32[128,2048]{1,0:T(8,128)} %get-tuple-element.28) | data formatting | bytes 2097152 | tf_op jit(solution)/shard_map/pallas_call | solution.py:90
  138.5 1.5 copy.191
  140.0 1.5 copy.194
  141.5 1.7 broadcast_multiply_fusion.1
  145.8 1.6 slice_bitcast_fusion.7
  148.1 3.9 %multiply_reduce_fusion = (f32[2,16]{1,0:T(2,128)}, f32[2,16,64,128]{3,2,1,0:T(8,128)S(1)}, f32[2,16,64,128]{3,2,1,0:T(8,128)}, f32[2,16,64,128]{3,2,1,0:T(8,128)S(1)}) fusion(f32[3,2,16,64,128]{4,3,2,1,0:T(8,128)S(1)} %copy-done.3, f32[2,16]{1,0:T(2,128)S(1)} %copy-done.99, f32[2,16,64,128]{3,2,1,0:T(8,128)S(1)} %copy-done.15, ...), kind=kLoop, calls=%fused_computation.71 | loop fusion | flops 6553568 | bytes 10486407 | tf_op jit(solution)/shard_map/reduce_sum | solution.py:144
  151.9 1.7 fusion.3
  153.6 2.6 %convolution_bitcast_fusion.9 = f32[2,128,128]{2,1,0:T(8,128)} fusion(f32[2,16,64,128]{3,2,1,0:T(8,128)S(1)} %get-tuple-element.41, f32[128,2,16,64]{0,3,2,1:T(8,128)S(1)} %bitcast.254, f32[128,2,16]{0,2,1:T(8,128)S(1)} %copy-done.57), kind=kOutput, calls=%fused_computation.24 | convolution fusion | flops 402915328 | bytes 2244608 | tf_op jit(solution)/shard_map/tgkp,gkpn->tgn/dot_general | solution.py:133
  156.2 2.6 %fusion.5 = f32[1,128,2,128]{1,3,2,0:T(8,128)} fusion(f32[1,128,2,128]{1,3,2,0:T(8,128)S(1)} %convolution_bitcast_fusion.6, f32[2,16,64,128]{3,2,1,0:T(8,128)S(1)} %get-tuple-element.71, f32[128,2,16,64]{0,3,2,1:T(8,128)S(1)} %bitcast.258, f32[128,2,16]{0,2,1:T(8,128)S(1)} %copy-done.49), kind=kOutput, calls=%fused_computation.27 | convolution fusion | flops 402948096 | bytes 2375680 | tf_op jit(solution)/shard_map/vmap(tgkp,gkpn->tgn)/dot_general | solution.py:133
  158.8 1.7 copy.222
  163.6 3.6 %collective-permute-start.8 = (f32[3,2560]{1,0:T(4,128)}, f32[3,2560]{1,0:T(4,128)}, u32[]{:S(2)}, u32[]{:S(2)}) collective-permute-start(f32[3,2560]{1,0:T(4,128)} %pad_maximum_fusion.9), channel_id=1, source_target_pairs={{4,12},{5,13},{6,14},{7,15},{20,28},{21,29},{22,30},{23,31}} | collective-permute-start | bytes 92168 | tf_op jit(solution)/shard_map/ppermute | solution.py:366
  167.2 1.3 collective-permute-start.9
  168.5 1.3 collective-permute-start.7
  169.7 2.0 multiply_reduce_fusion.1
  171.8 1.7 fusion.110
  174.9 2.7 %multiply_add_fusion = f32[128,2,16,64]{0,3,2,1:T(8,128)} fusion(f32[128,2,16,64]{0,3,2,1:T(8,128)} %get-tuple-element.123, f32[128,2,16,64]{0,3,2,1:T(8,128)} %bitcast.260, f32[128,2,16]{0,2,1:T(8,128)} %copy.170, f32[2,16]{1,0:T(2,128)} %copy-done.102, f32[128,2048]{0,1:T(8,128)S(1)} %copy.165), kind=kLoop, calls=%fused_computation.79 | loop fusion | flops 1048576 | bytes 4210816 | tf_op jit(solution)/shard_map/add | solution.py:139
  177.6 2.6 %copy.177 = f32[128,2048]{1,0:T(8,128)} copy(f32[128,2048]{0,1:T(8,128)} %bitcast.261) | data formatting | bytes 2097152 | tf_op jit(solution)/shard_map/reshape | solution.py:355
  180.3 1.7 broadcast_multiply_fusion.4
  183.0 1.4 pad_add_fusion.1
  184.5 1.7 fusion.2
  189.0 1.5 exponential_multiply_fusion
  192.4 1.8 convolution_bitcast_fusion.10
  196.0 2.4 %collective-permute-start.6 = (f32[3,2560]{1,0:T(4,128)S(1)}, f32[3,2560]{1,0:T(4,128)S(1)}, u32[]{:S(2)}, u32[]{:S(2)}) collective-permute-start(f32[3,2560]{1,0:T(4,128)S(1)} %pad_maximum_fusion.8), channel_id=1, source_target_pairs={{4,0},{8,4},{12,8},{5,1},{9,5},{13,9},{6,2},{10,6},{14,10},{7,3},{... | collective-permute-start | bytes 92168 | tf_op jit(solution)/shard_map/ppermute | solution.py:21
  199.1 1.5 split.68
  (344 shorter events, 50.3 us)
Async XLA Ops:
  2.8 21.7 %copy-start.61 = (bf16[128,256]{1,0:T(8,128)(2,1)S(1)}, bf16[128,256]{1,0:T(8,128)(2,1)}, u32[]{:S(2)}) copy-start(bf16[128,256]{1,0:T(8,128)(2,1)} %param.22) | copy-start | bytes 196612
  4.7 19.8 %copy-start.62 = (bf16[128,256]{1,0:T(8,128)(2,1)S(1)}, bf16[128,256]{1,0:T(8,128)(2,1)}, u32[]{:S(2)}) copy-start(bf16[128,256]{1,0:T(8,128)(2,1)} %param.23) | copy-start | bytes 196612
  4.8 24.8 %collective-permute-start.2 = (f32[7712]{0:T(1024)S(1)}, f32[7712]{0:T(1024)}, u32[]{:S(2)}, u32[]{:S(2)}) collective-permute-start(f32[7712]{0:T(1024)S(1)} %pad_maximum_fusion.10), channel_id=1, source_target_pairs={{0,12},{4,0},{8,4},{12,8},{1,13},{5,1},{9,5},{13,9},{2,14},{6,2},{... | collective-permute-start | bytes 92552 | tf_op jit(solution)/shard_map/ppermute | solution.py:211
  4.8 25.5 %collective-permute-start.1 = (f32[7712]{0:T(1024)S(1)}, f32[7712]{0:T(1024)}, u32[]{:S(2)}, u32[]{:S(2)}) collective-permute-start(f32[7712]{0:T(1024)S(1)} %pad_maximum_fusion.10), channel_id=1, source_target_pairs={{0,8},{4,12},{8,0},{12,4},{1,9},{5,13},{9,1},{13,5},{2,10},{6,14},... | collective-permute-start | bytes 92552 | tf_op jit(solution)/shard_map/ppermute | solution.py:211
  7.6 23.6 %collective-permute-start = (f32[7712]{0:T(1024)S(1)}, f32[7712]{0:T(1024)}, u32[]{:S(2)}, u32[]{:S(2)}) collective-permute-start(f32[7712]{0:T(1024)S(1)} %pad_maximum_fusion.10), channel_id=1, source_target_pairs={{0,4},{4,8},{8,12},{12,0},{1,5},{5,9},{9,13},{13,1},{2,6},{6,10},{... | collective-permute-start | bytes 92552 | tf_op jit(solution)/shard_map/ppermute | solution.py:211
  9.6 14.9 %copy-start.92 = (f32[2,16]{1,0:T(2,128)}, f32[2,16]{1,0:T(2,128)S(1)}, u32[]{:S(2)}) copy-start(f32[2,16]{1,0:T(2,128)S(1)} %mul.862) | copy-start | bytes 388
  15.3 19.0 %copy-start.73 = (f32[1,256]{1,0:T(1,128)}, f32[1,256]{1,0:T(1,128)S(1)}, u32[]{:S(2)}) copy-start(f32[1,256]{1,0:T(1,128)S(1)} %get-tuple-element.112) | copy-start | bytes 3076
  15.3 19.0 %copy-start.76 = (f32[1,256]{1,0:T(1,128)}, f32[1,256]{1,0:T(1,128)S(1)}, u32[]{:S(2)}) copy-start(f32[1,256]{1,0:T(1,128)S(1)} %get-tuple-element.113) | copy-start | bytes 3076
  17.5 7.0 %copy-start.28 = (bf16[128,2048]{1,0:T(8,128)(2,1)S(1)}, bf16[128,2048]{1,0:T(8,128)(2,1)}, u32[]{:S(2)}) copy-start(bf16[128,2048]{1,0:T(8,128)(2,1)} %param.21) | copy-start | bytes 1572868
  18.1 9.9 %copy-start.50 = (f32[1,2,16,128]{3,2,1,0:T(8,128)}, f32[1,2,16,128]{3,2,1,0:T(8,128)S(1)}, u32[]{:S(2)}) copy-start(f32[1,2,16,128]{3,2,1,0:T(8,128)S(1)} %reduce_window_sum.48) | copy-start | bytes 49156
  18.2 52.6 %copy-start.48 = (f32[128,2,16]{0,2,1:T(8,128)}, f32[128,2,16]{0,2,1:T(8,128)S(1)}, u32[]{:S(2)}) copy-start(f32[128,2,16]{0,2,1:T(8,128)S(1)} %exponential_bitcast_fusion.1) | copy-start | bytes 49156
  21.8 3.9 %copy-start.100 = (f32[128]{0:T(128)}, f32[128]{0:T(128)S(1)}, u32[]{:S(2)}) copy-start(f32[128]{0:T(128)S(1)} %fusion.119) | copy-start | bytes 1540
  25.8 3.7 %copy-start.102 = (f32[2,16]{1,0:T(2,128)}, f32[2,16]{1,0:T(2,128)S(1)}, u32[]{:S(2)}) copy-start(f32[2,16]{1,0:T(2,128)S(1)} %mul.865) | copy-start | bytes 388
  35.3 3.3 %copy-start.20 = (f32[128,256]{1,0:T(8,128)}, f32[128,256]{1,0:T(8,128)S(1)}, u32[]{:S(2)}) copy-start(f32[128,256]{1,0:T(8,128)S(1)} %get-tuple-element.127) | copy-start | bytes 393220
  41.2 18.3 %copy-start.17 = (bf16[1,128,2048]{2,1,0:T(8,128)(2,1)S(1)}, bf16[1,128,2048]{2,1,0:T(8,128)(2,1)}, u32[]{:S(2)}) copy-start(bf16[1,128,2048]{2,1,0:T(8,128)(2,1)} %param.30) | copy-start | bytes 1572868
  41.2 18.3 %copy-start.56 = (f32[1,2048]{1,0:T(1,128)S(1)}, f32[1,2048]{1,0:T(1,128)}, u32[]{:S(2)}) copy-start(f32[1,2048]{1,0:T(1,128)} %get-tuple-element.108) | copy-start | bytes 24580
  41.2 18.3 %copy-start.72 = (f32[2048]{0:T(1024)S(1)}, f32[2048]{0:T(1024)}, u32[]{:S(2)}) copy-start(f32[2048]{0:T(1024)} %mul.952) | copy-start | bytes 24580
  41.2 18.3 %copy-start.101 = (f32[128]{0:T(128)S(1)}, f32[128]{0:T(128)}, u32[]{:S(2)}) copy-start(f32[128]{0:T(128)} %copy-done.100) | copy-start | bytes 1540
  75.0 29.8 %collective-permute-start.3 = (f32[3,2,16,64,128]{4,3,2,1,0:T(8,128)}, f32[3,2,16,64,128]{4,3,2,1,0:T(8,128)}, u32[]{:S(2)}, u32[]{:S(2)}) collective-permute-start(f32[3,2,16,64,128]{4,3,2,1,0:T(8,128)} %pad_maximum_fusion), channel_id=1, source_target_pairs={{0,4},{4,0},{8,12},{12,8},{1,5},{5,1},{9,13},{13,9},{2,6},{6,2},{1... | collective-permute-start | bytes 9437192 | tf_op jit(solution)/shard_map/ppermute | solution.py:295
  82.9 25.6 %copy-start.43 = (f32[2,16,128]{2,1,0:T(8,128)}, f32[2,16,128]{2,1,0:T(8,128)S(1)}, u32[]{:S(2)}) copy-start(f32[2,16,128]{2,1,0:T(8,128)S(1)} %reduce_window_sum.47) | copy-start | bytes 49156
  104.8 3.7 %copy-start.96 = (f32[2,16]{1,0:T(2,128)}, f32[2,16]{1,0:T(2,128)S(1)}, u32[]{:S(2)}) copy-start(f32[2,16]{1,0:T(2,128)S(1)} %get-tuple-element.110) | copy-start | bytes 388
  104.8 3.8 %copy-start.98 = (f32[2,16]{1,0:T(2,128)}, f32[2,16]{1,0:T(2,128)S(1)}, u32[]{:S(2)}) copy-start(f32[2,16]{1,0:T(2,128)S(1)} %get-tuple-element.111) | copy-start | bytes 388
  104.8 3.8 %copy-start.107 = (f32[2,16]{1,0:T(2,128)S(1)}, f32[2,16]{1,0:T(2,128)}, u32[]{:S(2)}) copy-start(f32[2,16]{1,0:T(2,128)} %exp.141) | copy-start | bytes 388
  108.5 3.5 %copy-start.31 = (f32[1,128,256]{2,1,0:T(8,128)S(1)}, f32[1,128,256]{2,1,0:T(8,128)}, u32[]{:S(2)}) copy-start(f32[1,128,256]{2,1,0:T(8,128)} %get-tuple-element.125) | copy-start | bytes 393220
  108.6 3.5 %copy-start.37 = (f32[1,128,256]{2,1,0:T(8,128)S(1)}, f32[1,128,256]{2,1,0:T(8,128)}, u32[]{:S(2)}) copy-start(f32[1,128,256]{2,1,0:T(8,128)} %copy.220) | copy-start | bytes 393220
  108.6 3.5 %copy-start.83 = (f32[1,256]{1,0:T(1,128)S(1)}, f32[1,256]{1,0:T(1,128)}, u32[]{:S(2)}) copy-start(f32[1,256]{1,0:T(1,128)} %get-tuple-element.114) | copy-start | bytes 3076
  108.6 6.0 %copy-start.74 = (f32[1,256]{1,0:T(1,128)S(1)}, f32[1,256]{1,0:T(1,128)}, u32[]{:S(2)}) copy-start(f32[1,256]{1,0:T(1,128)} %copy-done.73) | copy-start | bytes 3076
  108.6 6.0 %copy-start.77 = (f32[1,256]{1,0:T(1,128)S(1)}, f32[1,256]{1,0:T(1,128)}, u32[]{:S(2)}) copy-start(f32[1,256]{1,0:T(1,128)} %copy-done.76) | copy-start | bytes 3076
  108.6 6.0 %copy-start.80 = (f32[1,256]{1,0:T(1,128)S(1)}, f32[1,256]{1,0:T(1,128)}, u32[]{:S(2)}) copy-start(f32[1,256]{1,0:T(1,128)} %get-tuple-element.115) | copy-start | bytes 3076
  111.7 31.4 %collective-permute-start.4 = (f32[2,16,64,128]{3,2,1,0:T(8,128)}, f32[2,16,64,128]{3,2,1,0:T(8,128)}, u32[]{:S(2)}, u32[]{:S(2)}) collective-permute-start(f32[2,16,64,128]{3,2,1,0:T(8,128)} %get-tuple-element.65), channel_id=1, source_target_pairs={{0,8},{4,12},{8,0},{12,4},{1,9},{5,13},{9,1},{13,5},{2,10},{6,14},... | collective-permute-start | bytes 3145736 | tf_op jit(solution)/shard_map/ppermute | solution.py:315
  136.0 5.5 %copy-start.51 = (f32[1,2048]{1,0:T(1,128)S(1)}, f32[1,2048]{1,0:T(1,128)}, u32[]{:S(2)}) copy-start(f32[1,2048]{1,0:T(1,128)} %get-tuple-element.106) | copy-start | bytes 24580
  136.0 5.5 %copy-start.53 = (f32[1,2048]{1,0:T(1,128)S(1)}, f32[1,2048]{1,0:T(1,128)}, u32[]{:S(2)}) copy-start(f32[1,2048]{1,0:T(1,128)} %get-tuple-element.107) | copy-start | bytes 24580
  141.5 3.9 %copy-start.30 = (f32[2,128,128]{2,1,0:T(8,128)S(1)}, f32[2,128,128]{2,1,0:T(8,128)}, u32[]{:S(2)}) copy-start(f32[2,128,128]{2,1,0:T(8,128)} %get-tuple-element.31) | copy-start | bytes 393220
  141.5 3.9 %copy-start.36 = (f32[1,128,256]{1,2,0:T(8,128)S(1)}, f32[1,128,256]{1,2,0:T(8,128)}, u32[]{:S(2)}) copy-start(f32[1,128,256]{1,2,0:T(8,128)} %copy.221) | copy-start | bytes 393220
  141.5 6.5 %copy-start.15 = (f32[2,16,64,128]{3,2,1,0:T(8,128)S(1)}, f32[2,16,64,128]{3,2,1,0:T(8,128)}, u32[]{:S(2)}) copy-start(f32[2,16,64,128]{3,2,1,0:T(8,128)} %get-tuple-element.66) | copy-start | bytes 3145732
  143.2 4.8 %collective-permute-start.5 = (f32[2,16,64,128]{3,2,1,0:T(8,128)}, f32[2,16,64,128]{3,2,1,0:T(8,128)S(1)}, u32[]{:S(2)}, u32[]{:S(2)}) collective-permute-start(f32[2,16,64,128]{3,2,1,0:T(8,128)} %collective-permute-done.4), channel_id=1, source_target_pairs={{0,4},{4,0},{8,12},{12,8},{1,5},{5,1},{9,13},{13,9},{2,6},{6,2},{1... | collective-permute-start | bytes 3145736 | tf_op jit(solution)/shard_map/ppermute | solution.py:316
  144.0 4.0 %copy-start.1 = (f32[3,2,16,64,128]{4,3,2,1,0:T(8,128)S(1)}, f32[3,2,16,64,128]{4,3,2,1,0:T(8,128)}, u32[]{:S(2)}) copy-start(f32[3,2,16,64,128]{4,3,2,1,0:T(8,128)} %copy-done) | copy-start | bytes 9437188
  144.0 4.0 %copy-start.3 = (f32[3,2,16,64,128]{4,3,2,1,0:T(8,128)S(1)}, f32[3,2,16,64,128]{4,3,2,1,0:T(8,128)}, u32[]{:S(2)}) copy-start(f32[3,2,16,64,128]{4,3,2,1,0:T(8,128)} %copy-done.2) | copy-start | bytes 9437188
  144.4 3.6 %copy-start.97 = (f32[2,16]{1,0:T(2,128)S(1)}, f32[2,16]{1,0:T(2,128)}, u32[]{:S(2)}) copy-start(f32[2,16]{1,0:T(2,128)} %copy-done.96) | copy-start | bytes 388
  144.4 3.6 %copy-start.99 = (f32[2,16]{1,0:T(2,128)S(1)}, f32[2,16]{1,0:T(2,128)}, u32[]{:S(2)}) copy-start(f32[2,16]{1,0:T(2,128)} %copy-done.98) | copy-start | bytes 388
  144.5 3.6 %copy-start.105 = (f32[2,16]{1,0:T(2,128)S(1)}, f32[2,16]{1,0:T(2,128)}, u32[]{:S(2)}) copy-start(f32[2,16]{1,0:T(2,128)} %mul.920) | copy-start | bytes 388
  144.5 3.6 %copy-start.106 = (f32[2,16]{1,0:T(2,128)S(1)}, f32[2,16]{1,0:T(2,128)}, u32[]{:S(2)}) copy-start(f32[2,16]{1,0:T(2,128)} %mul.898) | copy-start | bytes 388
  148.0 3.9 %copy-start.57 = (f32[128,2,16]{0,2,1:T(8,128)S(1)}, f32[128,2,16]{0,2,1:T(8,128)}, u32[]{:S(2)}) copy-start(f32[128,2,16]{0,2,1:T(8,128)} %get-tuple-element.102) | copy-start | bytes 49156
  151.9 4.2 %copy-start.6 = (f32[2,16,64,128]{3,2,1,0:T(8,128)}, f32[2,16,64,128]{3,2,1,0:T(8,128)S(1)}, u32[]{:S(2)}) copy-start(f32[2,16,64,128]{3,2,1,0:T(8,128)S(1)} %get-tuple-element.71) | copy-start | bytes 3145732
  156.2 4.2 %copy-start.23 = (f32[1,128,256]{2,1,0:T(8,128)S(1)}, f32[1,128,256]{2,1,0:T(8,128)}, u32[]{:S(2)}) copy-start(f32[1,128,256]{2,1,0:T(8,128)} %copy-done.22) | copy-start | bytes 393220
  160.4 9.3 %copy-start.4 = (f32[2,16,64,128]{3,2,1,0:T(8,128)S(1)}, f32[2,16,64,128]{3,2,1,0:T(8,128)}, u32[]{:S(2)}) copy-start(f32[2,16,64,128]{3,2,1,0:T(8,128)} %get-tuple-element.42) | copy-start | bytes 3145732
  162.9 6.8 %copy-start.70 = (f32[3,256]{1,0:T(4,128)}, f32[3,256]{1,0:T(4,128)S(1)}, u32[]{:S(2)}) copy-start(f32[3,256]{1,0:T(4,128)S(1)} %slice_bitcast_fusion.6) | copy-start | bytes 9220
  163.6 37.1 %collective-permute-start.8 = (f32[3,2560]{1,0:T(4,128)}, f32[3,2560]{1,0:T(4,128)}, u32[]{:S(2)}, u32[]{:S(2)}) collective-permute-start(f32[3,2560]{1,0:T(4,128)} %pad_maximum_fusion.9), channel_id=1, source_target_pairs={{4,12},{5,13},{6,14},{7,15},{20,28},{21,29},{22,30},{23,31}} | collective-permute-start | bytes 92168 | tf_op jit(solution)/shard_map/ppermute | solution.py:366
  167.2 33.5 %collective-permute-start.9 = (f32[3,2560]{1,0:T(4,128)}, f32[3,2560]{1,0:T(4,128)}, u32[]{:S(2)}, u32[]{:S(2)}) collective-permute-start(f32[3,2560]{1,0:T(4,128)} %pad_maximum_fusion.9), channel_id=1, source_target_pairs={{8,12},{9,13},{10,14},{11,15},{24,28},{25,29},{26,30},{27,31}} | collective-permute-start | bytes 92168 | tf_op jit(solution)/shard_map/ppermute | solution.py:366
  168.5 32.2 %collective-permute-start.7 = (f32[3,2560]{1,0:T(4,128)}, f32[3,2560]{1,0:T(4,128)}, u32[]{:S(2)}, u32[]{:S(2)}) collective-permute-start(f32[3,2560]{1,0:T(4,128)} %pad_maximum_fusion.9), channel_id=1, source_target_pairs={{0,12},{1,13},{2,14},{3,15},{16,28},{17,29},{18,30},{19,31}} | collective-permute-start | bytes 92168 | tf_op jit(solution)/shard_map/ppermute | solution.py:366
  186.1 4.4 %copy-start.21 = (f32[128,256]{1,0:T(8,128)S(1)}, f32[128,256]{1,0:T(8,128)}, u32[]{:S(2)}) copy-start(f32[128,256]{1,0:T(8,128)} %copy-done.20) | copy-start | bytes 393220
  186.1 5.2 %copy-start.63 = (f32[128,2,16]{0,2,1:T(8,128)S(1)}, f32[128,2,16]{0,2,1:T(8,128)}, u32[]{:S(2)}) copy-start(f32[128,2,16]{0,2,1:T(8,128)} %fusion.3) | copy-start | bytes 49156
  186.1 5.3 %copy-start.86 = (f32[1,256]{1,0:T(1,128)S(1)}, f32[1,256]{1,0:T(1,128)}, u32[]{:S(2)}) copy-start(f32[1,256]{1,0:T(1,128)} %get-tuple-element.116) | copy-start | bytes 3076
  186.1 5.3 %copy-start.88 = (f32[1,256]{1,0:T(1,128)S(1)}, f32[1,256]{1,0:T(1,128)}, u32[]{:S(2)}) copy-start(f32[1,256]{1,0:T(1,128)} %get-tuple-element.117) | copy-start | bytes 3076
  186.1 5.3 %copy-start.90 = (f32[1,256]{1,0:T(1,128)S(1)}, f32[1,256]{1,0:T(1,128)}, u32[]{:S(2)}) copy-start(f32[1,256]{1,0:T(1,128)} %get-tuple-element.119) | copy-start | bytes 3076
  186.2 5.3 %copy-start.33 = (f32[2,16,128]{1,0,2:T(2,128)S(1)}, f32[2,16,128]{1,0,2:T(2,128)}, u32[]{:S(2)}) copy-start(f32[2,16,128]{1,0,2:T(2,128)} %copy.194) | copy-start | bytes 49156
  186.7 5.0 %copy-start.95 = (f32[2,16,1]{1,0,2:T(2,128)S(1)}, f32[2,16,1]{1,0,2:T(2,128)}, u32[]{:S(2)}) copy-start(f32[2,16,1]{1,0,2:T(2,128)} %copy.230) | copy-start | bytes 388
  186.7 5.0 %copy-start.103 = (f32[2,16]{1,0:T(2,128)S(1)}, f32[2,16]{1,0:T(2,128)}, u32[]{:S(2)}) copy-start(f32[2,16]{1,0:T(2,128)} %get-tuple-element.40) | copy-start | bytes 388
  186.7 5.0 %copy-start.104 = (f32[2,16]{1,0:T(2,128)S(1)}, f32[2,16]{1,0:T(2,128)}, u32[]{:S(2)}) copy-start(f32[2,16]{1,0:T(2,128)} %get-tuple-element.38) | copy-start | bytes 388
  195.4 6.0 %copy-start.47 = (f32[3,2048]{1,0:T(4,128)S(1)}, f32[3,2048]{1,0:T(4,128)}, u32[]{:S(2)}) copy-start(f32[3,2048]{1,0:T(4,128)} %slice_bitcast_fusion.4) | copy-start | bytes 73732
  195.4 6.0 %copy-start.69 = (f32[3,256]{1,0:T(4,128)S(1)}, f32[3,256]{1,0:T(4,128)}, u32[]{:S(2)}) copy-start(f32[3,256]{1,0:T(4,128)} %slice_bitcast_fusion.7) | copy-start | bytes 9220
  195.4 5.9 %copy-start.71 = (f32[3,256]{1,0:T(4,128)S(1)}, f32[3,256]{1,0:T(4,128)}, u32[]{:S(2)}) copy-start(f32[3,256]{1,0:T(4,128)} %copy-done.70) | copy-start | bytes 9220
  195.6 8.0 %copy-start.11 = (f32[131,2048]{1,0:T(8,128)S(1)}, f32[131,2048]{1,0:T(8,128)}, u32[]{:S(2)}) copy-start(f32[131,2048]{1,0:T(8,128)} %pad_add_fusion.1) | copy-start | bytes 3219460
  196.0 5.3 %collective-permute-start.6 = (f32[3,2560]{1,0:T(4,128)S(1)}, f32[3,2560]{1,0:T(4,128)S(1)}, u32[]{:S(2)}, u32[]{:S(2)}) collective-permute-start(f32[3,2560]{1,0:T(4,128)S(1)} %pad_maximum_fusion.8), channel_id=1, source_target_pairs={{4,0},{8,4},{12,8},{5,1},{9,5},{13,9},{6,2},{10,6},{14,10},{7,3},{... | collective-permute-start | bytes 92168 | tf_op jit(solution)/shard_map/ppermute | solution.py:21
  (56 other events, 110.6 us)

commit v3 on v2

--- a/solution.py
+++ b/solution.py
@@ -4,6 +4,7 @@
 import jax.numpy as jnp
 from jax import lax
 from jax.experimental import pallas as pl
+from jax.experimental.pallas import tpu as pltpu
 from jax.sharding import PartitionSpec as P
 
 
@@ -36,97 +37,105 @@
     return lax.dot_general(a, b, (dims, ((), ())), precision=EXACT_DOT, preferred_element_type=jnp.float32)
 
 
-def _grad_kernel(per_group_pairs, x_ref, g_ref, b_ref, c_ref, crow_ref, ccol_ref, srow_ref,
-                 dx_ref, dstep_ref, dcum_ref, dsc_ref):
+def _grad_kernel(steps_per_group, x_ref, g_ref, b_ref, c_ref, crow_ref, srow_ref, skip_ref,
+                 dx_ref, dstep_ref, dcum_ref, dc_ref, db_ref, dsc_ref):
     step_id = pl.program_id(0)
-    x = x_ref[...]
-    g = g_ref[...]
-    t_len = x.shape[0]
+    bb = b_ref[...]
+    cc = c_ref[...]
+    t_len = bb.shape[0]
+    lanes = 2 * HD
     tri = lax.broadcasted_iota(jnp.int32, (t_len, t_len), 0) >= lax.broadcasted_iota(jnp.int32, (t_len, t_len), 1)
-    lane = lax.broadcasted_iota(jnp.int32, (1, 2 * HD), 1)
+    lane = lax.broadcasted_iota(jnp.int32, (1, lanes), 1)
     ones = jnp.ones((8, t_len), jnp.float32)
-    scores = _dot(c_ref[...], b_ref[...], ((1,), (1,)))
-    dx = jnp.zeros_like(x)
+    scores = _dot(cc, bb, ((1,), (1,)))
     dsc = jnp.zeros((t_len, t_len), jnp.float32)
-    for h in range(2):
-        mask = ((lane >= h * HD) & (lane < (h + 1) * HD)).astype(jnp.float32)
-        gm = g * mask
-        crow = crow_ref[0, h : h + 1, :]
-        ccol = ccol_ref[0, :, h : h + 1]
-        srow = srow_ref[0, h : h + 1, :]
-        within = jnp.where(tri, jnp.exp(jnp.where(tri, ccol - crow, 0.0)), 0.0)
-        score_w = scores * within
-        d_mix = _dot(gm, x, ((1,), (1,)))
-        dx = dx + _dot(score_w * srow, gm, ((0,), (0,)))
-        dsc = dsc + d_mix * within * srow
-        q_mat = d_mix * score_w
-        p_mat = q_mat * srow
-        dstep_ref[0, h : h + 1, :] = jnp.sum(q_mat, axis=0, keepdims=True)
-        dcum_ref[0, h : h + 1, :] = _dot(ones, p_mat, ((1,), (1,)))[0:1] - jnp.sum(
-            p_mat, axis=0, keepdims=True
-        )
-    dx_ref[...] = dx
-    first = step_id % per_group_pairs == 0
-
-    @pl.when(first)
+    for pair in range(dx_ref.shape[1] // lanes):
+        cols = slice(pair * lanes, (pair + 1) * lanes)
+        x = x_ref[:, cols]
+        g = g_ref[:, cols]
+        dx = skip_ref[:, cols] * g
+        for h in range(2):
+            head = 2 * pair + h
+            mask = ((lane >= h * HD) & (lane < (h + 1) * HD)).astype(jnp.float32)
+            gm = g * mask
+            crow = crow_ref[head : head + 1, :]
+            srow = srow_ref[head : head + 1, :]
+            ccol = jnp.transpose(jnp.broadcast_to(crow, (t_len, t_len)))
+            within = jnp.where(tri, jnp.exp(jnp.where(tri, ccol - crow, 0.0)), 0.0)
+            score_w = scores * within
+            d_mix = _dot(gm, x, ((1,), (1,)))
+            dx = dx + _dot(score_w * srow, gm, ((0,), (0,)))
+            dsc = dsc + d_mix * within * srow
+            q_mat = d_mix * score_w
+            p_mat = q_mat * srow
+            dstep_ref[head : head + 1, :] = jnp.sum(q_mat, axis=0, keepdims=True)
+            dcum_ref[head : head + 1, :] = _dot(ones, p_mat, ((1,), (1,)))[0:1] - jnp.sum(
+                p_mat, axis=0, keepdims=True
+            )
+        dx_ref[:, cols] = dx
+    within_group = step_id % steps_per_group
+
+    @pl.when(within_group == 0)
     def _():
-        dsc_ref[0] = dsc
-
-    @pl.when(jnp.logical_not(first))
+        dsc_ref[...] = dsc
+
+    @pl.when(within_group != 0)
     def _():
-        dsc_ref[0] += dsc
-
-
-def block_inner(xa, ba, ca, step, rate, G):
+        dsc_ref[...] += dsc
+
+    @pl.when(within_group == steps_per_group - 1)
+    def _():
+        total = dsc_ref[...]
+        dc_ref[...] = _dot(total, bb, ((1,), (0,)))
+        db_ref[...] = _dot(total, cc, ((0,), (0,)))
+
+
+def block_inner(xa, ba, ca, step, rate, skip, G):
     T, ng, nk, P = xa.shape
     nh = ng * nk
-    pairs = nh // 2
-    per_group_pairs = nk // 2
+    heads_per_step = 8
+    steps_per_group = nk // heads_per_step
     cum = jnp.cumsum(-step * rate[:, :, None], axis=-1)
-    cum_pairs = cum.reshape(pairs, 2, T)
-    row_spec = pl.BlockSpec((1, 2, T), lambda j: (j, 0, 0))
-    lane_spec = pl.BlockSpec((T, 2 * P), lambda j: (0, j))
-    grp_spec = pl.BlockSpec((T, N), lambda j: (0, j // per_group_pairs))
-    dx2, d_direct, d_cum, d_scores = pl.pallas_call(
-        functools.partial(_grad_kernel, per_group_pairs),
-        grid=(pairs,),
+    row_spec = pl.BlockSpec((heads_per_step, T), lambda j: (j, 0))
+    lane_spec = pl.BlockSpec((T, heads_per_step * P), lambda j: (0, j))
+    grp_spec = pl.BlockSpec((T, N), lambda j: (0, j // steps_per_group))
+    dx2, d_direct, d_cum, dc, db = pl.pallas_call(
+        functools.partial(_grad_kernel, steps_per_group),
+        grid=(nh // heads_per_step,),
         in_specs=[
-            lane_spec, lane_spec, grp_spec, grp_spec, row_spec,
-            pl.BlockSpec((1, T, 2), lambda j: (j, 0, 0)), row_spec,
+            lane_spec, lane_spec, grp_spec, grp_spec, row_spec, row_spec,
+            pl.BlockSpec((1, heads_per_step * P), lambda j: (0, j)),
         ],
-        out_specs=[
-            lane_spec, row_spec, row_spec,
-            pl.BlockSpec((1, T, T), lambda j: (j // per_group_pairs, 0, 0)),
-        ],
+        out_specs=[lane_spec, row_spec, row_spec, grp_spec, grp_spec],
         out_shape=[
             jax.ShapeDtypeStruct((T, nh * P), jnp.float32),
-            jax.ShapeDtypeStruct((pairs, 2, T), jnp.float32),
-            jax.ShapeDtypeStruct((pairs, 2, T), jnp.float32),
-            jax.ShapeDtypeStruct((ng, T, T), jnp.float32),
+            jax.ShapeDtypeStruct((nh, T), jnp.float32),
+            jax.ShapeDtypeStruct((nh, T), jnp.float32),
+            jax.ShapeDtypeStruct((T, ng * N), jnp.float32),
+            jax.ShapeDtypeStruct((T, ng * N), jnp.float32),
         ],
+        scratch_shapes=[pltpu.VMEM((T, T), jnp.float32)],
     )(
         xa.reshape(T, nh * P),
         G.reshape(T, nh * P),
         ba.reshape(T, ng * N),
         ca.reshape(T, ng * N),
-        cum_pairs,
-        jnp.swapaxes(cum_pairs, 1, 2),
-        step.reshape(pairs, 2, T),
+        cum.reshape(nh, T),
+        step.reshape(nh, T),
+        jnp.repeat(skip.reshape(1, nh), P, axis=1),
     )
     return (
         dx2.reshape(T, ng, nk, P),
         d_direct.reshape(ng, nk, T),
         d_cum.reshape(ng, nk, T),
-        d_scores,
+        dc.reshape(T, ng, N),
+        db.reshape(T, ng, N),
         cum,
     )
 
 
-def block_outer(inner, xa, ba, ca, step, rate, skip, S0, G, lam):
-    dx, d_step, d_cum, d_scores, cum = inner
-    dx = dx + skip[None, :, :, None] * G
-    dc = jnp.einsum("gts,sgn->tgn", d_scores, ba, precision=EXACT_DOT)
-    db = jnp.einsum("gts,tgn->sgn", d_scores, ca, precision=EXACT_DOT)
+def block_outer(inner, xa, ba, ca, step, rate, S0, G, lam):
+    dx, d_step, d_cum, dc, db, cum = inner
     grow = jnp.exp(cum)
     g_grow = G * grow.transpose(2, 0, 1)[..., None]
     carried = jnp.einsum("tgn,gkpn->tgkp", ca, S0, precision=EXACT_DOT)
@@ -264,13 +273,13 @@
         _, _, sx, sb, sc, cot, step_g = suffix_parts(*items)
         grow = jnp.exp(jnp.cumsum(-step_g * rate[:, :, None], axis=-1))
         adjoint = jnp.einsum("gkt,tgkp,tgn->gkpn", grow, cot, sc, precision=EXACT_DOT)
-        inner = block_inner(sx, sb, sc, step_g, rate, cot)
+        inner = block_inner(sx, sb, sc, step_g, rate, gain, cot)
         return adjoint, inner
 
     def suffix_back(end_state, inner, *items):
         one_step_pullback, conv_pullback, sx, sb, sc, cot, step_g = suffix_parts(*items)
         suffix_len = sx.shape[0]
-        dx, db, dc, d_step = block_outer(inner, sx, sb, sc, step_g, rate, gain, end_state, cot, None)
+        dx, db, dc, d_step = block_outer(inner, sx, sb, sc, step_g, rate, end_state, cot, None)
         conv_grads = conv_pullback(
             (dx.reshape(suffix_len, -1), db.reshape(suffix_len, -1), dc.reshape(suffix_len, -1))
         )
@@ -287,7 +296,7 @@
     )
     adjoints, suffix_inner = jax.vmap(suffix_front, in_axes=(0, 0, 0, 1, 0, 0))(*suffix_items)
     step_g = prompt_step.reshape(num_groups, per_group, prompt_len)
-    prompt_inner = block_inner(x_act, b_act, c_act, step_g, rate, prompt_cot)
+    prompt_inner = block_inner(x_act, b_act, c_act, step_g, rate, gain, prompt_cot)
     core = my_index % 2
     chip = my_index // 2
     num_chips = num_ways // 2
@@ -349,7 +358,7 @@
         suffix_back, in_axes=(None, 0, 0, 0, 0, 1, 0, 0), out_axes=(0, 1)
     )(prompt_end_late, suffix_inner, *suffix_items)
     dx, db, dc, d_step = block_outer(
-        prompt_inner, x_act, b_act, c_act, step_g, rate, gain, start_state, prompt_cot, end_grad
+        prompt_inner, x_act, b_act, c_act, step_g, rate, start_state, prompt_cot, end_grad
     )
     prompt_grads = prompt_conv_pullback(
         (dx.reshape(prompt_len, -1), db.reshape(prompt_len, -1), dc.reshape(prompt_len, -1))

time: 207 us -> 208 us (level)
  waiting for transfers between devices: 0.68 us -> 28.1 us
  other arithmetic: 74.7 us -> 65 us
  Pallas kernels: 36.5 us -> 28.2 us
  local copies, waits for them, and re-layouts: 56.2 us -> 52.3 us
  matrix products: 19.2 us -> 16.2 us
    ppermute x1, waiting for transfers between devices: 0.01 us -> 24.4 us  [shards(): incoming = lax.ppermute(outgoing, 'suf', route)]
    pallas_call x2, Pallas kernels: 36.5 us -> 28.2 us  [block_inner(): pl.pallas_call(functools.partial(_grad_kernel, steps_per_group), grid=(nh...]
    mul x12, other arithmetic: 11.7 us -> 7.82 us  [causal_conv(): padded[tap_index:tap_index + num_tokens]]
    ppermute x1, waiting for transfers between devices: 0.01 us -> 3.59 us  [shards(): lax.ppermute(own_triple, 'suf', [(j, j ^ 1) for j in range(num_ways)])]
    broadcast_in_dim x0 -> x3, local copies, waits for them, and re-layouts: none -> 3.47 us  [the longest x2 2.72 us: block_inner(): jnp.repeat(skip.reshape(1, nh), P, axis=1)]
    dot_general x4 -> x0, matrix products: 3.11 us -> none  [the longest x2 2.33 us: block_outer(): db = jnp.einsum('gts,tgn->sgn', d_scores, ca, precision=EXACT_DOT)]
    select_n x2 -> x0, other arithmetic: 2.87 us -> none  [softplus_of(): return jax.nn.softplus(raw + dt_bias[:, None])]
    another operation x4, local copies, waits for them, and re-layouts: 2.37 us -> 0.09 us  [shards(): jnp.stack(received)]
  transfers between devices with their start and end apart: 10 -> 10, of which waited for: 1 -> 2; matrix products, arithmetic and copies ran while one was open for 46% -> 34% of each run, Pallas kernels for 9% -> 7%
where the time goes in v3:
time: 208 us; the launch traced here: 206 us
  other arithmetic  65 us (31%)
  local copies, waits for them, and re-layouts  52.3 us (25%)
  Pallas kernels  28.2 us (14%)
  waiting for transfers between devices  28.1 us (14%)
  matrix products  16.2 us (8%)
  starting transfers between devices  13.1 us (6%)
  between operations  3.29 us (2%)
    pallas_call x2, Pallas kernels, block_inner(): pl.pallas_call(functools.partial(_grad_kernel, steps_per_group), grid=(nh...  28.2 us
    ppermute x1, waiting for transfers between devices, shards(): incoming = lax.ppermute(outgoing, 'suf', route)  24.4 us
    mul x12, other arithmetic, causal_conv(): padded[tap_index:tap_index + num_tokens]  7.82 us
    reshape x2, other arithmetic, block_inner(): pl.pallas_call(functools.partial(_grad_kernel, steps_per_group), grid=(nh...  7.21 us
    unnamed x185, local copies, waits for them, and re-layouts  6.58 us
    dot_general x2, matrix products, block_outer(): dc = dc + jnp.einsum('tgkp,gkpn->tgn', g_grow, S0, precision=EXACT_DOT)  5.55 us
    reduce_sum x1, other arithmetic, block_outer(): jnp.sum(lam * S0, axis=(-2, -1))  5.48 us
    split x3, local copies, waits for them, and re-layouts, causal_conv(): padded = jnp.concatenate([context, values], axis=0)  5.33 us
  transfers between devices with their start and end apart: 10, of which 2 were waited for; matrix products, arithmetic and copies ran while one was open for 34% of the time, Pallas kernels for 7%

profile of v3, /device:TPU:1, one launch (start us, length us, event | category | flops | bytes accessed | tf_op | source)
XLA Modules:
  0.0 206.1 jit_solution(17505515079669886426)
XLA Ops:
  4.2 2.7 %collective-permute-start = (f32[7712]{0:T(1024)S(1)}, f32[7712]{0:T(1024)S(1)}, u32[]{:S(2)}, u32[]{:S(2)}) collective-permute-start(f32[7712]{0:T(1024)S(1)} %pad_maximum_fusion.10), channel_id=1, source_target_pairs={{0,4},{4,8},{8,12},{12,0},{1,5},{5,9},{9,13},{13,1},{2,6},{6,10},{... | collective-permute-start | bytes 92552 | tf_op jit(solution)/shard_map/ppermute | solution.py:220
  7.3 1.4 exponential_multiply_fusion.1
  12.0 1.5 slice_convert_fusion.6
  16.2 1.2 fusion.113
  19.3 1.1 convert_element_type.162
  20.4 1.1 convert_element_type.169
  26.3 2.5 %fusion.37 = (f32[128,2048]{1,0:T(8,128)S(1)}, f32[128,2048]{1,0:T(8,128)}) fusion(f32[128,2048]{1,0:T(8,128)S(1)} %copy-done.17, f32[2048]{0:T(1024)} %bitcast.272, f32[2048]{0:T(1024)} %bitcast.268, f32[3,2048]{1,0:T(4,128)} %slice.288, f32[2048]{0:T(1024)} %bitcast.264, f32[2048]{0:T(1024)} %bitcast.260), kind=kLoop, calls=%fused_computation.84 | loop fusion | flops 3670016 | bytes 3203072 | tf_op jit(solution)/shard_map/jvp(jit(silu))/mul | solution.py:33
  29.1 1.7 multiply_bitcast_fusion.1
  31.6 5.5 %multiply_bitcast_fusion = (f32[128,2048]{1,0:T(8,128)}, f32[1,128,2048]{2,1,0:T(8,128)}, f32[1,128,2048]{2,1,0:T(8,128)}, f32[128,2048]{1,0:T(8,128)}) fusion(f32[1,128,2048]{2,1,0:T(8,128)} %convert_element_type.169, f32[2048]{0:T(1024)} %bitcast.273, f32[2048]{0:T(1024)} %bitcast.269, f32[1,3,2048]{2,1,0:T(4,128)} %slice_bitcast_fusion.5, ...), kind=kLoop, calls=%fused_computation.73 | loop fusion | flops 4194304 | bytes 5825024 | tf_op jit(solution)/shard_map/vmap()/squeeze;vmap()/reshape;vmap()/reshape | solution.py:102
  37.1 1.5 copy.123
  38.7 1.1 reshape.510
  39.8 1.8 convolution_bitcast_fusion.5
  41.6 1.0 convolution_bitcast_fusion.3
  42.7 1.0 convolution_bitcast_fusion.4
  43.8 2.0 pad_maximum_fusion
  45.7 1.4 collective-permute-start.3
  49.2 3.6 %collective-permute-done.3 = f32[3,2,16,64,128]{4,3,2,1,0:T(8,128)} collective-permute-done((f32[3,2,16,64,128]{4,3,2,1,0:T(8,128)}, f32[3,2,16,64,128]{4,3,2,1,0:T(8,128)}, u32[]{:S(2)}, u32[]{:S(2)}) %collective-permute-start.3) | collective-permute-done | bytes 3145760 | tf_op jit(solution)/shard_map/ppermute | solution.py:304
  52.7 3.5 %broadcast_select_fusion.1 = (f32[3,2,16,64,128]{4,3,2,1,0:T(8,128)S(1)}, f32[3,2,16,64,128]{4,3,2,1,0:T(8,128)S(1)}) fusion(f32[3,2,16,64,128]{4,3,2,1,0:T(8,128)} %collective-permute-done.3, pred[]{:T(512)S(6)} %eq.58, f32[1,2,16,64,128]{4,3,2,1,0:T(8,128)} %copy-done.14, f32[1,2,16,64,128]{4,3,2,1,0:T(8,128)} %copy-done.15, ...), kind=kLoop, calls=%fused_computation.9 | loop fusion | flops 3145728 | bytes 12582913 | tf_op jit(solution)/shard_map/jit(_where)/select_n | solution.py:306
  56.3 1.9 fusion.31
  58.2 24.4 %collective-permute-done.4 = f32[2,16,64,128]{3,2,1,0:T(8,128)} collective-permute-done((f32[2,16,64,128]{3,2,1,0:T(8,128)S(1)}, f32[2,16,64,128]{3,2,1,0:T(8,128)}, u32[]{:S(2)}, u32[]{:S(2)}) %collective-permute-start.4) | collective-permute-done | bytes 1048608 | tf_op jit(solution)/shard_map/ppermute | solution.py:324
  82.6 1.2 collective-permute-start.5
  83.9 2.1 %convert_element_type.163.g_ref = f32[128,2048]{1,0:T(8,128)} convert(bf16[128,2048]{1,0:T(8,128)(2,1)} %param.25) | non-fusion elementwise | flops 262144 | bytes 1572864 | tf_op jit(solution)/shard_map/convert_element_type | solution.py:245
  86.0 1.5 copy.111
  88.1 1.6 negate_multiply_fusion
  89.7 1.6 copy.112
  91.3 1.9 reduce_window_sum.47
  93.2 1.4 slice.303
  94.6 1.3 copy.177
  95.9 1.4 exponential_bitcast_fusion
  97.3 1.5 copy.116
  98.8 1.3 broadcast_in_dim.54
  100.1 1.4 broadcast_in_dim.59.skip_ref
  101.5 1.3 multiply_reduce_fusion.2
  102.8 1.3 mul.870
  104.1 1.3 mul.892
  105.3 14.1 %shard_map.242 = (f32[128,2048]{1,0:T(8,128)}, f32[32,128]{1,0:T(8,128)}, f32[32,128]{1,0:T(8,128)}, f32[128,256]{1,0:T(8,128)}, f32[128,256]{1,0:T(8,128)}) custom-call(f32[128,2048]{1,0:T(8,128)} %copy-done.9, f32[128,2048]{1,0:T(8,128)} %convert_element_type.163.g_ref, f32[128,256]{1,0:T(8,128)} %copy-done.21, f32[128,256]{1,0:T(8,128)} %get-tuple-element.67.c_ref, ...), custom_call_target="tpu_custom_call" | custom-call | tf_op jit(solution)/shard_map/pallas_call | solution.py:102
  119.4 1.5 copy.140
  120.9 1.5 copy.137
  122.4 2.6 %copy.113 = f32[128,2048]{0,1:T(8,128)} copy(f32[128,2048]{1,0:T(8,128)} %get-tuple-element.30) | data formatting | bytes 2097152 | tf_op jit(solution)/shard_map/pallas_call | solution.py:102
  125.0 1.7 copy.164
  126.6 1.7 copy.166
  128.3 5.5 %multiply_reduce_fusion = (f32[2,16]{1,0:T(2,128)}, f32[2,16,64,128]{3,2,1,0:T(8,128)S(1)}, f32[2,16,64,128]{3,2,1,0:T(8,128)}, f32[2,16,64,128]{3,2,1,0:T(8,128)}) fusion(f32[3,2,16,64,128]{4,3,2,1,0:T(8,128)} %copy-done, f32[2,16]{1,0:T(2,128)} %copy-done.87, f32[2,16,64,128]{3,2,1,0:T(8,128)} %get-tuple-element.66, ...), kind=kLoop, calls=%fused_computation.70 | loop fusion | flops 6553568 | bytes 10486407 | tf_op jit(solution)/shard_map/reduce_sum | solution.py:153
  133.8 1.0 copy-done.10
  134.8 1.1 fusion.3
  136.3 2.0 multiply_reduce_fusion.1
  140.8 14.1 %vmap__.1 = (f32[128,2048]{1,0:T(8,128)}, f32[32,128]{1,0:T(8,128)}, f32[32,128]{1,0:T(8,128)}, f32[128,256]{1,0:T(8,128)}, f32[128,256]{1,0:T(8,128)}) custom-call(f32[128,2048]{1,0:T(8,128)} %get-tuple-element.57.x_ref, f32[128,2048]{1,0:T(8,128)} %get-tuple-element.134.g_ref, f32[128,256]{1,0:T(8,128)} %get-tuple-element.55.b_ref, ...), custom_call_target="tpu_custom_call" | custom-call | tf_op jit(solution)/shard_map/vmap()/pallas_call | solution.py:102
  155.0 1.7 broadcast_multiply_fusion
  157.6 1.0 copy-done.19
  161.4 3.7 %fusion.4 = f32[1,128,2,128]{1,3,2,0:T(8,128)} fusion(f32[1,128,2,128]{1,3,2,0:T(8,128)} %bitcast.256, f32[2,16,64,128]{3,2,1,0:T(8,128)} %get-tuple-element.75, f32[128,2,16,64]{0,3,2,1:T(8,128)S(1)} %bitcast.240, f32[128,2,16]{0,2,1:T(8,128)S(1)} %exponential_bitcast_fusion.1), kind=kOutput, calls=%fused_computation.23 | convolution fusion | flops 402948096 | bytes 2375680 | tf_op jit(solution)/shard_map/vmap(tgkp,gkpn->tgn)/dot_general | solution.py:142
  165.1 1.7 copy.169
  169.9 1.3 collective-permute-start.7
  171.1 2.5 %collective-permute-start.8 = (f32[3,2560]{1,0:T(4,128)}, f32[3,2560]{1,0:T(4,128)}, u32[]{:S(2)}, u32[]{:S(2)}) collective-permute-start(f32[3,2560]{1,0:T(4,128)} %pad_maximum_fusion.9), channel_id=1, source_target_pairs={{4,12},{5,13},{6,14},{7,15},{20,28},{21,29},{22,30},{23,31}} | collective-permute-start | bytes 92168 | tf_op jit(solution)/shard_map/ppermute | solution.py:375
  173.7 1.3 collective-permute-start.9
  175.7 2.8 %multiply_add_fusion = f32[128,2,16,64]{0,3,2,1:T(8,128)} fusion(f32[128,2,16,64]{0,3,2,1:T(8,128)} %bitcast.242, f32[128,2,16,64]{0,3,2,1:T(8,128)} %get-tuple-element.128, f32[128,2,16]{0,2,1:T(8,128)S(1)} %copy.118), kind=kLoop, calls=%fused_computation.78 | loop fusion | flops 524288 | bytes 3162112 | tf_op jit(solution)/shard_map/add | solution.py:148
  178.5 2.5 %copy.126 = f32[128,2048]{1,0:T(8,128)} copy(f32[128,2048]{0,1:T(8,128)} %bitcast.243) | data formatting | bytes 2097152 | tf_op jit(solution)/shard_map/reshape | solution.py:364
  181.0 2.0 broadcast_multiply_fusion.4
  184.1 1.4 pad_add_fusion.1
  185.5 1.1 fusion.2
  187.3 2.6 %fusion.5 = f32[128,2,128]{0,2,1:T(8,128)S(1)} fusion(f32[128,2,128]{0,2,1:T(8,128)S(1)} %bitcast.253, f32[2,16,64,128]{3,2,1,0:T(8,128)S(1)} %copy-done.8, f32[2,16,128,64]{2,3,1,0:T(8,128)S(1)} %bitcast.235, f32[2,16,128]{2,1,0:T(8,128)} %copy.128), kind=kOutput, calls=%fused_computation.24 | convolution fusion | flops 402948096 | bytes 2375680 | tf_op jit(solution)/shard_map/gkpn,sgkp,gks->sgn/dot_general | solution.py:149
  191.7 1.8 fusion.6
  194.4 2.3 %collective-permute-start.6 = (f32[3,2560]{1,0:T(4,128)S(1)}, f32[3,2560]{1,0:T(4,128)S(1)}, u32[]{:S(2)}, u32[]{:S(2)}) collective-permute-start(f32[3,2560]{1,0:T(4,128)S(1)} %pad_maximum_fusion.8), channel_id=1, source_target_pairs={{4,0},{8,4},{12,8},{5,1},{9,5},{13,9},{6,2},{10,6},{14,10},{7,3},{... | collective-permute-start | bytes 92168 | tf_op jit(solution)/shard_map/ppermute | solution.py:22
  197.6 2.1 %split.67 = bf16[1,128,2048]{2,1,0:T(8,128)(2,1)} slice(f32[1,131,2048]{2,1,0:T(8,128)} %copy-done.19), slice={[0:1], [3:131], [0:2048]} | slice | bytes 1048576 | tf_op jit(solution)/shard_map/vmap(transpose(jvp()))/split | solution.py:26
  199.7 1.6 split.69
  201.4 1.5 split.68
  (297 shorter events, 37.3 us)
Async XLA Ops:
  0.6 18.6 %copy-start.27 = (bf16[128,2048]{1,0:T(8,128)(2,1)S(1)}, bf16[128,2048]{1,0:T(8,128)(2,1)}, u32[]{:S(2)}) copy-start(bf16[128,2048]{1,0:T(8,128)(2,1)} %param.21) | copy-start | bytes 1572868
  4.2 17.5 %collective-permute-start = (f32[7712]{0:T(1024)S(1)}, f32[7712]{0:T(1024)S(1)}, u32[]{:S(2)}, u32[]{:S(2)}) collective-permute-start(f32[7712]{0:T(1024)S(1)} %pad_maximum_fusion.10), channel_id=1, source_target_pairs={{0,4},{4,8},{8,12},{12,0},{1,5},{5,9},{9,13},{13,1},{2,6},{6,10},{... | collective-permute-start | bytes 92552 | tf_op jit(solution)/shard_map/ppermute | solution.py:220
  6.9 14.9 %collective-permute-start.1 = (f32[7712]{0:T(1024)S(1)}, f32[7712]{0:T(1024)S(1)}, u32[]{:S(2)}, u32[]{:S(2)}) collective-permute-start(f32[7712]{0:T(1024)S(1)} %pad_maximum_fusion.10), channel_id=1, source_target_pairs={{0,8},{4,12},{8,0},{12,4},{1,9},{5,13},{9,1},{13,5},{2,10},{6,14},... | collective-permute-start | bytes 92552 | tf_op jit(solution)/shard_map/ppermute | solution.py:220
  6.9 14.9 %collective-permute-start.2 = (f32[7712]{0:T(1024)S(1)}, f32[7712]{0:T(1024)S(1)}, u32[]{:S(2)}, u32[]{:S(2)}) collective-permute-start(f32[7712]{0:T(1024)S(1)} %pad_maximum_fusion.10), channel_id=1, source_target_pairs={{0,12},{4,0},{8,4},{12,8},{1,13},{5,1},{9,5},{13,9},{2,14},{6,2},{... | collective-permute-start | bytes 92552 | tf_op jit(solution)/shard_map/ppermute | solution.py:220
  9.5 5.3 %copy-start.80 = (f32[2,16]{1,0:T(2,128)}, f32[2,16]{1,0:T(2,128)S(1)}, u32[]{:S(2)}) copy-start(f32[2,16]{1,0:T(2,128)S(1)} %mul.837) | copy-start | bytes 388
  11.1 13.7 %copy-start.72 = (f32[1,256]{1,0:T(1,128)}, f32[1,256]{1,0:T(1,128)S(1)}, u32[]{:S(2)}) copy-start(f32[1,256]{1,0:T(1,128)S(1)} %get-tuple-element.119) | copy-start | bytes 3076
  11.1 13.7 %copy-start.74 = (f32[1,256]{1,0:T(1,128)}, f32[1,256]{1,0:T(1,128)S(1)}, u32[]{:S(2)}) copy-start(f32[1,256]{1,0:T(1,128)S(1)} %get-tuple-element.120) | copy-start | bytes 3076
  11.1 13.7 %copy-start.76 = (f32[1,256]{1,0:T(1,128)}, f32[1,256]{1,0:T(1,128)S(1)}, u32[]{:S(2)}) copy-start(f32[1,256]{1,0:T(1,128)S(1)} %get-tuple-element.122) | copy-start | bytes 3076
  11.1 13.7 %copy-start.78 = (f32[1,256]{1,0:T(1,128)}, f32[1,256]{1,0:T(1,128)S(1)}, u32[]{:S(2)}) copy-start(f32[1,256]{1,0:T(1,128)S(1)} %get-tuple-element.121) | copy-start | bytes 3076
  11.1 9.2 %copy-start.58 = (bf16[1,128,256]{2,1,0:T(8,128)(2,1)S(1)}, bf16[1,128,256]{2,1,0:T(8,128)(2,1)}, u32[]{:S(2)}) copy-start(bf16[1,128,256]{2,1,0:T(8,128)(2,1)} %param.28) | copy-start | bytes 196612
  12.0 12.8 %copy-start.64 = (f32[1,256]{1,0:T(1,128)}, f32[1,256]{1,0:T(1,128)S(1)}, u32[]{:S(2)}) copy-start(f32[1,256]{1,0:T(1,128)S(1)} %get-tuple-element.115) | copy-start | bytes 3076
  12.0 12.8 %copy-start.66 = (f32[1,256]{1,0:T(1,128)}, f32[1,256]{1,0:T(1,128)S(1)}, u32[]{:S(2)}) copy-start(f32[1,256]{1,0:T(1,128)S(1)} %get-tuple-element.116) | copy-start | bytes 3076
  12.0 12.8 %copy-start.68 = (f32[1,256]{1,0:T(1,128)}, f32[1,256]{1,0:T(1,128)S(1)}, u32[]{:S(2)}) copy-start(f32[1,256]{1,0:T(1,128)S(1)} %get-tuple-element.118) | copy-start | bytes 3076
  12.0 12.8 %copy-start.70 = (f32[1,256]{1,0:T(1,128)}, f32[1,256]{1,0:T(1,128)S(1)}, u32[]{:S(2)}) copy-start(f32[1,256]{1,0:T(1,128)S(1)} %get-tuple-element.117) | copy-start | bytes 3076
  17.4 2.9 %copy-start.59 = (bf16[1,128,256]{2,1,0:T(8,128)(2,1)S(1)}, bf16[1,128,256]{2,1,0:T(8,128)(2,1)}, u32[]{:S(2)}) copy-start(bf16[1,128,256]{2,1,0:T(8,128)(2,1)} %param.27) | copy-start | bytes 196612
  18.3 2.1 copy-start.28
  21.7 20.9 %copy-start.3 = (f32[128,2048]{0,1:T(8,128)}, f32[128,2048]{0,1:T(8,128)S(1)}, u32[]{:S(2)}) copy-start(f32[128,2048]{0,1:T(8,128)S(1)} %copy.121) | copy-start | bytes 3145732
  22.6 3.7 %copy-start.17 = (f32[128,2048]{1,0:T(8,128)S(1)}, f32[128,2048]{1,0:T(8,128)}, u32[]{:S(2)}) copy-start(f32[128,2048]{1,0:T(8,128)} %convert_element_type.162) | copy-start | bytes 3145732
  29.1 10.7 %copy-start.1 = (f32[128,2048]{0,1:T(8,128)}, f32[128,2048]{0,1:T(8,128)S(1)}, u32[]{:S(2)}) copy-start(f32[128,2048]{0,1:T(8,128)S(1)} %copy.119) | copy-start | bytes 3145732
  38.7 2.9 %copy-start.6 = (f32[1,128,2048]{1,2,0:T(8,128)}, f32[1,128,2048]{1,2,0:T(8,128)S(1)}, u32[]{:S(2)}) copy-start(f32[1,128,2048]{1,2,0:T(8,128)S(1)} %copy.123) | copy-start | bytes 3145732
  41.6 2.2 %copy-start.13 = (f32[1,2,16,64,128]{4,3,2,1,0:T(8,128)}, f32[1,2,16,64,128]{4,3,2,1,0:T(8,128)S(1)}, u32[]{:S(2)}) copy-start(f32[1,2,16,64,128]{4,3,2,1,0:T(8,128)S(1)} %convolution_bitcast_fusion.5) | copy-start | bytes 3145732
  45.7 7.0 %collective-permute-start.3 = (f32[3,2,16,64,128]{4,3,2,1,0:T(8,128)}, f32[3,2,16,64,128]{4,3,2,1,0:T(8,128)}, u32[]{:S(2)}, u32[]{:S(2)}) collective-permute-start(f32[3,2,16,64,128]{4,3,2,1,0:T(8,128)} %pad_maximum_fusion), channel_id=1, source_target_pairs={{0,4},{4,0},{8,12},{12,8},{1,5},{5,1},{9,13},{13,9},{2,6},{6,2},{1... | collective-permute-start | bytes 9437192 | tf_op jit(solution)/shard_map/ppermute | solution.py:304
  49.1 7.1 %copy-start.86 = (f32[2,16]{1,0:T(2,128)}, f32[2,16]{1,0:T(2,128)S(1)}, u32[]{:S(2)}) copy-start(f32[2,16]{1,0:T(2,128)S(1)} %get-tuple-element.113) | copy-start | bytes 388
  49.1 7.1 %copy-start.87 = (f32[2,16]{1,0:T(2,128)}, f32[2,16]{1,0:T(2,128)S(1)}, u32[]{:S(2)}) copy-start(f32[2,16]{1,0:T(2,128)S(1)} %get-tuple-element.114) | copy-start | bytes 388
  49.1 7.1 %copy-start.91 = (f32[2,16]{1,0:T(2,128)S(1)}, f32[2,16]{1,0:T(2,128)}, u32[]{:S(2)}) copy-start(f32[2,16]{1,0:T(2,128)} %exp.142) | copy-start | bytes 388
  58.2 24.5 %collective-permute-start.4 = (f32[2,16,64,128]{3,2,1,0:T(8,128)S(1)}, f32[2,16,64,128]{3,2,1,0:T(8,128)}, u32[]{:S(2)}, u32[]{:S(2)}) collective-permute-start(f32[2,16,64,128]{3,2,1,0:T(8,128)S(1)} %get-tuple-element.65), channel_id=1, source_target_pairs={{0,8},{4,12},{8,0},{12,4},{1,9},{5,13},{9,1},{13,5},{2,10},{6,14},... | collective-permute-start | bytes 3145736 | tf_op jit(solution)/shard_map/ppermute | solution.py:324
  82.6 45.7 %collective-permute-start.5 = (f32[2,16,64,128]{3,2,1,0:T(8,128)}, f32[2,16,64,128]{3,2,1,0:T(8,128)}, u32[]{:S(2)}, u32[]{:S(2)}) collective-permute-start(f32[2,16,64,128]{3,2,1,0:T(8,128)} %collective-permute-done.4), channel_id=1, source_target_pairs={{0,4},{4,0},{8,12},{12,8},{1,5},{5,1},{9,13},{13,9},{2,6},{6,2},{1... | collective-permute-start | bytes 3145736 | tf_op jit(solution)/shard_map/ppermute | solution.py:325
  128.3 6.5 %copy-start.4 = (f32[128,2048]{0,1:T(8,128)S(1)}, f32[128,2048]{0,1:T(8,128)}, u32[]{:S(2)}) copy-start(f32[128,2048]{0,1:T(8,128)} %copy-done.3) | copy-start | bytes 3145732
  128.3 6.5 %copy-start.48 = (f32[128,2,16]{0,2,1:T(8,128)S(1)}, f32[128,2,16]{0,2,1:T(8,128)}, u32[]{:S(2)}) copy-start(f32[128,2,16]{0,2,1:T(8,128)} %get-tuple-element.106) | copy-start | bytes 49156
  136.3 2.1 %copy-start.24 = (f32[2,16,128]{1,0,2:T(2,128)S(1)}, f32[2,16,128]{1,0,2:T(2,128)}, u32[]{:S(2)}) copy-start(f32[2,16,128]{1,0,2:T(2,128)} %copy.116) | copy-start | bytes 49156
  136.3 2.1 %copy-start.25 = (f32[2,16,128]{1,0,2:T(2,128)S(1)}, f32[2,16,128]{1,0,2:T(2,128)}, u32[]{:S(2)}) copy-start(f32[2,16,128]{1,0,2:T(2,128)} %copy.111) | copy-start | bytes 49156
  136.3 2.3 %copy-start.32 = (f32[2,16,128]{1,0,2:T(2,128)S(1)}, f32[2,16,128]{1,0,2:T(2,128)}, u32[]{:S(2)}) copy-start(f32[2,16,128]{1,0,2:T(2,128)} %copy.140) | copy-start | bytes 49156
  140.8 14.1 %copy-start.18 = (f32[1,128,2048]{2,1,0:T(8,128)S(1)}, f32[1,128,2048]{2,1,0:T(8,128)}, u32[]{:S(2)}) copy-start(f32[1,128,2048]{2,1,0:T(8,128)} %get-tuple-element.58) | copy-start | bytes 3145732
  140.8 14.1 %copy-start.46 = (f32[1,2048]{1,0:T(1,128)S(1)}, f32[1,2048]{1,0:T(1,128)}, u32[]{:S(2)}) copy-start(f32[1,2048]{1,0:T(1,128)} %get-tuple-element.111) | copy-start | bytes 24580
  157.0 2.2 %copy-start.35 = (f32[1,128,256]{2,1,0:T(8,128)S(1)}, f32[1,128,256]{2,1,0:T(8,128)}, u32[]{:S(2)}) copy-start(f32[1,128,256]{2,1,0:T(8,128)} %get-tuple-element.56) | copy-start | bytes 393220
  157.0 2.1 %copy-start.56 = (f32[128,256]{1,0:T(8,128)S(1)}, f32[128,256]{1,0:T(8,128)}, u32[]{:S(2)}) copy-start(f32[128,256]{1,0:T(8,128)} %get-tuple-element.34) | copy-start | bytes 393220
  157.1 2.1 %copy-start.79 = (f32[1,256]{1,0:T(1,128)S(1)}, f32[1,256]{1,0:T(1,128)}, u32[]{:S(2)}) copy-start(f32[1,256]{1,0:T(1,128)} %copy-done.78) | copy-start | bytes 3076
  157.1 2.2 %copy-start.73 = (f32[1,256]{1,0:T(1,128)S(1)}, f32[1,256]{1,0:T(1,128)}, u32[]{:S(2)}) copy-start(f32[1,256]{1,0:T(1,128)} %copy-done.72) | copy-start | bytes 3076
  157.1 2.2 %copy-start.75 = (f32[1,256]{1,0:T(1,128)S(1)}, f32[1,256]{1,0:T(1,128)}, u32[]{:S(2)}) copy-start(f32[1,256]{1,0:T(1,128)} %copy-done.74) | copy-start | bytes 3076
  157.1 2.2 %copy-start.77 = (f32[1,256]{1,0:T(1,128)S(1)}, f32[1,256]{1,0:T(1,128)}, u32[]{:S(2)}) copy-start(f32[1,256]{1,0:T(1,128)} %copy-done.76) | copy-start | bytes 3076
  158.6 2.1 %copy-start.55 = (f32[128,256]{1,0:T(8,128)S(1)}, f32[128,256]{1,0:T(8,128)}, u32[]{:S(2)}) copy-start(f32[128,256]{1,0:T(8,128)} %get-tuple-element.35) | copy-start | bytes 393220
  158.6 2.8 %copy-start.7 = (f32[1,128,2048]{1,2,0:T(8,128)S(1)}, f32[1,128,2048]{1,2,0:T(8,128)}, u32[]{:S(2)}) copy-start(f32[1,128,2048]{1,2,0:T(8,128)} %copy-done.6) | copy-start | bytes 3145732
  161.4 5.4 %copy-start.23 = (f32[1,128,256]{2,1,0:T(8,128)S(1)}, f32[1,128,256]{2,1,0:T(8,128)}, u32[]{:S(2)}) copy-start(f32[1,128,256]{2,1,0:T(8,128)} %copy-done.22) | copy-start | bytes 393220
  166.8 2.4 %copy-start.38 = (f32[3,2048]{1,0:T(4,128)S(1)}, f32[3,2048]{1,0:T(4,128)}, u32[]{:S(2)}) copy-start(f32[3,2048]{1,0:T(4,128)} %slice_bitcast_fusion.4) | copy-start | bytes 73732
  166.8 2.4 %copy-start.60 = (f32[3,256]{1,0:T(4,128)S(1)}, f32[3,256]{1,0:T(4,128)}, u32[]{:S(2)}) copy-start(f32[3,256]{1,0:T(4,128)} %slice_bitcast_fusion.7) | copy-start | bytes 9220
  169.2 6.4 %copy-start.62 = (f32[3,256]{1,0:T(4,128)}, f32[3,256]{1,0:T(4,128)S(1)}, u32[]{:S(2)}) copy-start(f32[3,256]{1,0:T(4,128)S(1)} %slice_bitcast_fusion.6) | copy-start | bytes 9220
  169.9 33.1 %collective-permute-start.7 = (f32[3,2560]{1,0:T(4,128)}, f32[3,2560]{1,0:T(4,128)}, u32[]{:S(2)}, u32[]{:S(2)}) collective-permute-start(f32[3,2560]{1,0:T(4,128)} %pad_maximum_fusion.9), channel_id=1, source_target_pairs={{0,12},{1,13},{2,14},{3,15},{16,28},{17,29},{18,30},{19,31}} | collective-permute-start | bytes 92168 | tf_op jit(solution)/shard_map/ppermute | solution.py:375
  171.1 31.8 %collective-permute-start.8 = (f32[3,2560]{1,0:T(4,128)}, f32[3,2560]{1,0:T(4,128)}, u32[]{:S(2)}, u32[]{:S(2)}) collective-permute-start(f32[3,2560]{1,0:T(4,128)} %pad_maximum_fusion.9), channel_id=1, source_target_pairs={{4,12},{5,13},{6,14},{7,15},{20,28},{21,29},{22,30},{23,31}} | collective-permute-start | bytes 92168 | tf_op jit(solution)/shard_map/ppermute | solution.py:375
  173.7 29.3 %collective-permute-start.9 = (f32[3,2560]{1,0:T(4,128)}, f32[3,2560]{1,0:T(4,128)}, u32[]{:S(2)}, u32[]{:S(2)}) collective-permute-start(f32[3,2560]{1,0:T(4,128)} %pad_maximum_fusion.9), channel_id=1, source_target_pairs={{8,12},{9,13},{10,14},{11,15},{24,28},{25,29},{26,30},{27,31}} | collective-permute-start | bytes 92168 | tf_op jit(solution)/shard_map/ppermute | solution.py:375
  178.5 2.5 %copy-start.47 = (f32[1,2048]{1,0:T(1,128)S(1)}, f32[1,2048]{1,0:T(1,128)}, u32[]{:S(2)}) copy-start(f32[1,2048]{1,0:T(1,128)} %get-tuple-element.111) | copy-start | bytes 24580
  187.3 2.8 %copy-start.34 = (f32[128,256]{1,0:T(8,128)S(1)}, f32[128,256]{1,0:T(8,128)}, u32[]{:S(2)}) copy-start(f32[128,256]{1,0:T(8,128)} %get-tuple-element.130) | copy-start | bytes 393220
  187.3 4.3 %copy-start.11 = (f32[2,16,64,128]{3,2,1,0:T(8,128)S(1)}, f32[2,16,64,128]{3,2,1,0:T(8,128)}, u32[]{:S(2)}) copy-start(f32[2,16,64,128]{3,2,1,0:T(8,128)} %copy-done.10) | copy-start | bytes 3145732
  191.7 2.1 %copy-start.65 = (f32[1,256]{1,0:T(1,128)S(1)}, f32[1,256]{1,0:T(1,128)}, u32[]{:S(2)}) copy-start(f32[1,256]{1,0:T(1,128)} %copy-done.64) | copy-start | bytes 3076
  191.7 2.1 %copy-start.67 = (f32[1,256]{1,0:T(1,128)S(1)}, f32[1,256]{1,0:T(1,128)}, u32[]{:S(2)}) copy-start(f32[1,256]{1,0:T(1,128)} %copy-done.66) | copy-start | bytes 3076
  191.7 2.1 %copy-start.69 = (f32[1,256]{1,0:T(1,128)S(1)}, f32[1,256]{1,0:T(1,128)}, u32[]{:S(2)}) copy-start(f32[1,256]{1,0:T(1,128)} %copy-done.68) | copy-start | bytes 3076
  193.7 3.0 %copy-start.82 = (f32[2,16]{1,0:T(2,128)S(1)}, f32[2,16]{1,0:T(2,128)}, u32[]{:S(2)}) copy-start(f32[2,16]{1,0:T(2,128)} %copy-done.80) | copy-start | bytes 388
  193.7 3.0 %copy-start.83 = (f32[32,128]{1,0:T(8,128)S(1)}, f32[32,128]{1,0:T(8,128)}, u32[]{:S(2)}) copy-start(f32[32,128]{1,0:T(8,128)} %get-tuple-element.38) | copy-start | bytes 49156
  193.7 3.1 %copy-start.52 = (f32[32,1,128]{2,1,0:T(1,128)S(1)}, f32[32,1,128]{2,1,0:T(1,128)}, u32[]{:S(2)}) copy-start(f32[32,1,128]{2,1,0:T(1,128)} %param.29) | copy-start | bytes 49156
  193.7 3.1 %copy-start.89 = (f32[32]{0:T(128)S(1)}, f32[32]{0:T(128)}, u32[]{:S(2)}) copy-start(f32[32]{0:T(128)} %param.38) | copy-start | bytes 388
  193.9 9.1 %copy-start.39 = (f32[3,2048]{1,0:T(4,128)S(1)}, f32[3,2048]{1,0:T(4,128)}, u32[]{:S(2)}) copy-start(f32[3,2048]{1,0:T(4,128)} %slice_bitcast_fusion.4) | copy-start | bytes 73732
  193.9 9.1 %copy-start.61 = (f32[3,256]{1,0:T(4,128)S(1)}, f32[3,256]{1,0:T(4,128)}, u32[]{:S(2)}) copy-start(f32[3,256]{1,0:T(4,128)} %slice_bitcast_fusion.7) | copy-start | bytes 9220
  193.9 9.1 %copy-start.63 = (f32[3,256]{1,0:T(4,128)S(1)}, f32[3,256]{1,0:T(4,128)}, u32[]{:S(2)}) copy-start(f32[3,256]{1,0:T(4,128)} %copy-done.62) | copy-start | bytes 9220
  194.4 8.5 %collective-permute-start.6 = (f32[3,2560]{1,0:T(4,128)S(1)}, f32[3,2560]{1,0:T(4,128)S(1)}, u32[]{:S(2)}, u32[]{:S(2)}) collective-permute-start(f32[3,2560]{1,0:T(4,128)S(1)} %pad_maximum_fusion.8), channel_id=1, source_target_pairs={{4,0},{8,4},{12,8},{5,1},{9,5},{13,9},{6,2},{10,6},{14,10},{7,3},{... | collective-permute-start | bytes 92168 | tf_op jit(solution)/shard_map/ppermute | solution.py:22
  199.7 5.5 %copy-start.16 = (f32[131,2048]{1,0:T(8,128)S(1)}, f32[131,2048]{1,0:T(8,128)}, u32[]{:S(2)}) copy-start(f32[131,2048]{1,0:T(8,128)} %pad_add_fusion.1) | copy-start | bytes 3219460
  (38 other events, 52.6 us)

commit v4 on v3

--- a/solution.py
+++ b/solution.py
@@ -22,7 +22,7 @@
     return lax.ppermute(block, axis, route)
 
 
-def causal_conv(values, context, taps):
+def conv_pre(values, context, taps):
     padded = jnp.concatenate([context, values], axis=0)
     num_tokens = values.shape[0]
     result = padded[0:num_tokens] * taps[0].astype(jnp.float32)
@@ -30,7 +30,39 @@
         result = result + padded[tap_index : tap_index + num_tokens] * taps[tap_index].astype(
             jnp.float32
         )
-    return jax.nn.silu(result)
+    return result
+
+
+@jax.custom_vjp
+def causal_conv(values, context, taps):
+    return jax.nn.silu(conv_pre(values, context, taps))
+
+
+def _conv_forward(values, context, taps):
+    pre = conv_pre(values, context, taps)
+    return jax.nn.silu(pre), (pre, taps)
+
+
+def _conv_backward(saved, d_act):
+    pre, taps = saved
+    gate = jax.nn.sigmoid(pre)
+    d_pre = d_act * (gate + pre * (gate * (1.0 - gate)))
+    weights = taps.astype(jnp.float32)
+    margin = taps.shape[0] - 1
+    d_values = d_pre * weights[margin]
+    for tap_index in range(margin):
+        shift = margin - tap_index
+        d_values = d_values + jnp.pad(d_pre[shift:], ((0, shift), (0, 0))) * weights[tap_index]
+    d_context = jnp.stack(
+        [
+            sum(weights[tap_index] * d_pre[row - tap_index] for tap_index in range(row + 1))
+            for row in range(margin)
+        ]
+    )
+    return d_values, d_context, jnp.zeros_like(taps)
+
+
+causal_conv.defvjp(_conv_forward, _conv_backward)
 
 
 def _dot(a, b, dims):

time: 208 us -> 221 us (1.062)
  other arithmetic: 65 us -> 80.3 us
  waiting for transfers between devices: 28.1 us -> 20.4 us
  matrix products: 16.2 us -> 20 us
    slice x1 -> x21, local copies, waits for them, and re-layouts: 0.68 us -> 11 us  [the longest x7 4.15 us: convs(): causal_conv(ux, cx, conv_x)]
    convert_element_type x0 -> x6, other arithmetic: none -> 9.36 us  [the longest x1 2.76 us: shards(): conv_grads[0].astype(jnp.bfloat16)]
    ppermute x1, waiting for transfers between devices: 24.4 us -> 16.3 us  [shards(): incoming = lax.ppermute(outgoing, 'suf', route)]
    split x3 -> x0, local copies, waits for them, and re-layouts: 5.33 us -> none  [causal_conv(): padded = jnp.concatenate([context, values], axis=0)]
    unnamed x185 -> x167, local copies, waits for them, and re-layouts: 6.58 us -> 3.33 us
    mul x19 -> x15, other arithmetic: 15.6 us -> 17.3 us  [the longest x3 5.95 us: _conv_forward(): return (jax.nn.silu(pre), (pre, taps))]
  transfers between devices with their start and end apart: 10 -> 10, of which waited for: 2 -> 2; matrix products, arithmetic and copies ran while one was open for 34% -> 39% of each run, Pallas kernels for 7% -> 6%
where the time goes in v4:
time: 221 us; the launch traced here: 218 us
  other arithmetic  80.3 us (36%)
  local copies, waits for them, and re-layouts  53 us (24%)
  Pallas kernels  28.2 us (13%)
  waiting for transfers between devices  20.4 us (9%)
  matrix products  20 us (9%)
  starting transfers between devices  13.2 us (6%)
  between operations  3.23 us (1%)
    pallas_call x2, Pallas kernels, block_inner(): pl.pallas_call(functools.partial(_grad_kernel, steps_per_group), grid=(nh...  28.2 us
    ppermute x1, waiting for transfers between devices, shards(): incoming = lax.ppermute(outgoing, 'suf', route)  16.3 us
    reshape x2, other arithmetic, block_inner(): pl.pallas_call(functools.partial(_grad_kernel, steps_per_group), grid=(nh...  8.08 us
    mul x3, other arithmetic, _conv_forward(): return (jax.nn.silu(pre), (pre, taps))  5.95 us
    dot_general x2, matrix products, block_outer(): dc = dc + jnp.einsum('tgkp,gkpn->tgn', g_grow, S0, precision=EXACT_DOT)  5.84 us
    reduce_sum x1, other arithmetic, block_outer(): jnp.sum(lam * S0, axis=(-2, -1))  5.49 us
    ppermute x3, starting transfers between devices, shards(): lax.ppermute(ctx_grads, 'suf', [(sender, num_ways - 1)])  5.08 us
    mul x3, other arithmetic, convs(): causal_conv(ux, cx, conv_x)  4.49 us
  transfers between devices with their start and end apart: 10, of which 2 were waited for; matrix products, arithmetic and copies ran while one was open for 39% of the time, Pallas kernels for 6%

profile of v4, /device:TPU:1, one launch (start us, length us, event | category | flops | bytes accessed | tf_op | source)
XLA Modules:
  0.0 218.4 jit_solution(14547878800450135378)
XLA Ops:
  4.2 2.7 %collective-permute-start = (f32[7712]{0:T(1024)S(1)}, f32[7712]{0:T(1024)S(1)}, u32[]{:S(2)}, u32[]{:S(2)}) collective-permute-start(f32[7712]{0:T(1024)S(1)} %pad_maximum_fusion.9), channel_id=1, source_target_pairs={{0,4},{4,8},{8,12},{12,0},{1,5},{5,9},{9,13},{13,1},{2,6},{6,10},{... | collective-permute-start | bytes 92552 | tf_op jit(solution)/shard_map/ppermute | solution.py:252
  7.4 1.4 exponential_multiply_fusion.1
  15.7 1.2 fusion.132
  18.7 2.2 %convert_element_type.210 = f32[128,2048]{1,0:T(8,128)} convert(bf16[128,2048]{1,0:T(8,128)(2,1)} %param.21) | non-fusion elementwise | flops 262144 | bytes 1572864 | tf_op jit(solution)/shard_map/convert_element_type | solution.py:267
  21.8 1.5 convert_element_type.221
  23.3 1.1 convert_element_type.220
  28.5 4.4 %fusion.38 = (f32[128,2048]{1,0:T(8,128)S(1)}, f32[128,2048]{1,0:T(8,128)}) fusion(f32[128,2048]{1,0:T(8,128)} %convert_element_type.210, f32[2048]{0:T(1024)S(1)} %bitcast.369, f32[2048]{0:T(1024)S(1)} %bitcast.365, f32[3,2048]{1,0:T(4,128)S(1)} %slice.546, f32[2048]{0:T(1024)S(1)} %bitcast.367, f32[2048]{0:T(1024)S(1)} %bitcast.363), kind=kLoop, calls=%fused_computation.81 | loop fusion | flops 3670016 | bytes 3203072 | tf_op jit(solution)/shard_map/jvp(jit(silu))/mul | solution.py:43
  33.3 2.4 %multiply_bitcast_fusion.1 = (f32[128,256]{1,0:T(8,128)}, f32[1,128,256]{2,1,0:T(8,128)}, f32[128,256]{1,0:T(8,128)}, f32[1,128,256]{2,1,0:T(8,128)S(1)}) fusion(f32[1,128,256]{2,1,0:T(8,128)} %convert_element_type.221, f32[256]{0:T(256)} %bitcast.402, f32[256]{0:T(256)} %bitcast.398, f32[1,3,256]{2,1,0:T(4,128)} %get-tuple-element.88, f32[256]{0:T(256)} %bitcast.400, ...), kind=kLoop, calls=%fused_computation.170 | loop fusion | flops 917504 | bytes 800768 | tf_op jit(solution)/shard_map/vmap()/squeeze;vmap()/reshape;vmap()/reshape | solution.py:134
  37.4 5.7 %multiply_bitcast_fusion = (f32[128,2048]{1,0:T(8,128)}, f32[1,128,2048]{2,1,0:T(8,128)}, f32[1,128,2048]{2,1,0:T(8,128)}, f32[128,2048]{1,0:T(8,128)}) fusion(f32[1,128,2048]{2,1,0:T(8,128)} %convert_element_type.220, f32[2048]{0:T(1024)} %bitcast.370, f32[2048]{0:T(1024)} %bitcast.366, f32[1,3,2048]{2,1,0:T(4,128)} %slice_bitcast_fusion.4, ...), kind=kLoop, calls=%fused_computation.70 | loop fusion | flops 4194304 | bytes 5825024 | tf_op jit(solution)/shard_map/vmap()/squeeze;vmap()/reshape;vmap()/reshape | solution.py:134
  43.1 1.5 copy.121
  44.6 1.8 reshape.549
  46.4 1.8 convolution_bitcast_fusion.5
  50.4 2.0 pad_maximum_fusion
  52.4 1.4 collective-permute-start.3
  55.3 4.2 %collective-permute-done.3 = f32[3,2,16,64,128]{4,3,2,1,0:T(8,128)} collective-permute-done((f32[3,2,16,64,128]{4,3,2,1,0:T(8,128)}, f32[3,2,16,64,128]{4,3,2,1,0:T(8,128)}, u32[]{:S(2)}, u32[]{:S(2)}) %collective-permute-start.3) | collective-permute-done | bytes 3145760 | tf_op jit(solution)/shard_map/ppermute | solution.py:336
  59.5 3.5 %broadcast_select_fusion = (f32[3,2,16,64,128]{4,3,2,1,0:T(8,128)S(1)}, f32[3,2,16,64,128]{4,3,2,1,0:T(8,128)S(1)}) fusion(f32[3,2,16,64,128]{4,3,2,1,0:T(8,128)} %collective-permute-done.3, pred[]{:T(512)S(6)} %eq.58, f32[1,2,16,64,128]{4,3,2,1,0:T(8,128)} %copy-done.11, f32[1,2,16,64,128]{4,3,2,1,0:T(8,128)} %copy-done.12, f32[1,2,16,64,128]{4,3,2,1,0:T(8,128)} %copy-done.10), kind=kLoop, calls=%fused_computation.8 | loop fusion | flops 3145728 | bytes 12582913 | tf_op jit(solution)/shard_map/jit(_where)/select_n | solution.py:337
  63.0 2.3 %fusion.32 = (f32[2,16,64,128]{3,2,1,0:T(8,128)}, f32[2,16,64,128]{3,2,1,0:T(8,128)}) fusion(f32[3,2,16,64,128]{4,3,2,1,0:T(8,128)S(1)} %get-tuple-element.61, f32[3,2,16,64,128]{4,3,2,1,0:T(8,128)S(1)} %get-tuple-element.62, f32[2,16]{1,0:T(2,128)S(1)} %exp.143, f32[2,16]{1,0:T(2,128)S(1)} %get-tuple-element.106, pred[]{:T(512)S(6)} %ge.27, pred[]{:T(512)S(6)} %eq.58, ...), kind=kLoop, calls=%fused_computation.58 | loop fusion | flops 2359296 | bytes 8388994 | tf_op jit(solution)/shard_map/jit(_where)/select_n | solution.py:352
  67.5 1.6 copy.110
  69.0 1.9 reduce_window_sum.47
  70.9 1.4 slice.561
  72.3 1.4 copy.174
  73.7 16.3 %collective-permute-done.4 = f32[2,16,64,128]{3,2,1,0:T(8,128)} collective-permute-done((f32[2,16,64,128]{3,2,1,0:T(8,128)}, f32[2,16,64,128]{3,2,1,0:T(8,128)}, u32[]{:S(2)}, u32[]{:S(2)}) %collective-permute-start.4) | collective-permute-done | bytes 1048608 | tf_op jit(solution)/shard_map/ppermute | solution.py:356
  90.0 1.2 collective-permute-start.5
  91.2 1.4 subtract_exponential_fusion
  92.6 2.1 convert_element_type.211.g_ref
  95.3 1.3 convert_element_type.218
  96.6 1.3 convert_element_type.219
  97.9 1.5 copy.114
  99.4 1.3 broadcast_in_dim.54
  100.7 1.4 broadcast_in_dim.59.skip_ref
  102.1 1.4 fusion.148
  103.5 1.4 fusion.149
  105.6 1.3 slice_reduce_fusion.2
  107.7 14.1 %shard_map.242 = (f32[128,2048]{1,0:T(8,128)}, f32[32,128]{1,0:T(8,128)}, f32[32,128]{1,0:T(8,128)}, f32[128,256]{1,0:T(8,128)}, f32[128,256]{1,0:T(8,128)}) custom-call(f32[128,2048]{1,0:T(8,128)} %copy-done.7, f32[128,2048]{1,0:T(8,128)} %convert_element_type.211.g_ref, f32[128,256]{1,0:T(8,128)} %copy-done.16, f32[128,256]{1,0:T(8,128)} %get-tuple-element.55.c_ref, ...), custom_call_target="tpu_custom_call" | custom-call | tf_op jit(solution)/shard_map/pallas_call | solution.py:134
  121.7 1.5 copy.137
  123.2 1.5 copy.134
  124.6 2.6 %copy.111 = f32[128,2048]{0,1:T(8,128)} copy(f32[128,2048]{1,0:T(8,128)} %get-tuple-element.30) | data formatting | bytes 2097152 | tf_op jit(solution)/shard_map/pallas_call | solution.py:134
  127.2 1.7 copy.161
  128.9 1.7 copy.163
  130.6 5.5 %multiply_reduce_fusion = (f32[2,16]{1,0:T(2,128)}, f32[2,16,64,128]{3,2,1,0:T(8,128)}, f32[2,16,64,128]{3,2,1,0:T(8,128)S(1)}, f32[2,16,64,128]{3,2,1,0:T(8,128)}) fusion(pred[]{:T(512)S(6)} %ge.31, pred[]{:T(512)S(6)} %eq.61, pred[]{:T(512)S(6)} %ge.30, f32[2,16]{1,0:T(2,128)S(1)} %mul.1032, f32[3,2,16,64,128]{4,3,2,1,0:T(8,128)} %copy-done, ...), kind=kLoop, calls=%fused_computation.66 | loop fusion | flops 6553568 | bytes 10486407 | tf_op jit(solution)/shard_map/reduce_sum | solution.py:185
  137.1 1.1 fusion.3
  138.4 3.6 %multiply_reduce_fusion.1 = (f32[128,2,16]{0,2,1:T(8,128)S(1)}, f32[128,2,16,64]{0,3,2,1:T(8,128)}) fusion(f32[128,2048]{0,1:T(8,128)} %copy-done.1, f32[2,16,64,128]{3,2,1,0:T(8,128)} %get-tuple-element.45, f32[128,2,128,1]{2,1,0,3:T(2,128)S(1)} %bitcast.338), kind=kOutput, calls=%fused_computation.67 | convolution fusion | flops 403173376 | bytes 3293184 | tf_op jit(solution)/shard_map/gkpn,sgn->sgkp/dot_general | solution.py:179
  144.1 14.1 %vmap__.1 = (f32[128,2048]{1,0:T(8,128)}, f32[32,128]{1,0:T(8,128)}, f32[32,128]{1,0:T(8,128)}, f32[128,256]{1,0:T(8,128)}, f32[128,256]{1,0:T(8,128)}) custom-call(f32[128,2048]{1,0:T(8,128)} %get-tuple-element.51.x_ref, f32[128,2048]{1,0:T(8,128)} %get-tuple-element.134.g_ref, f32[128,256]{1,0:T(8,128)} %get-tuple-element.49.b_ref, ...), custom_call_target="tpu_custom_call" | custom-call | tf_op jit(solution)/shard_map/vmap()/pallas_call | solution.py:134
  159.4 1.8 fusion.4
  165.4 1.9 fusion.26
  167.3 1.1 slice.628
  169.5 1.1 slice.630
  172.0 1.3 collective-permute-start.7
  173.2 2.5 %collective-permute-start.8 = (f32[3,2560]{1,0:T(4,128)}, f32[3,2560]{1,0:T(4,128)}, u32[]{:S(2)}, u32[]{:S(2)}) collective-permute-start(f32[3,2560]{1,0:T(4,128)} %pad_maximum_fusion.8), channel_id=1, source_target_pairs={{4,12},{5,13},{6,14},{7,15},{20,28},{21,29},{22,30},{23,31}} | collective-permute-start | bytes 92168 | tf_op jit(solution)/shard_map/ppermute | solution.py:407
  175.8 1.3 collective-permute-start.9
  177.7 2.0 fusion.2
  182.0 1.8 multiply_add_fusion
  183.8 1.3 copy.124
  185.1 1.9 fusion.23
  187.7 3.7 %fusion.5 = f32[128,2,128]{0,2,1:T(8,128)} fusion(f32[128,2,128]{0,2,1:T(8,128)S(1)} %bitcast.343, f32[2,16,64,128]{3,2,1,0:T(8,128)} %get-tuple-element.45, f32[2,16,128,64]{2,3,1,0:T(8,128)S(1)} %bitcast.325, f32[2,16,128]{2,1,0:T(8,128)} %copy.125), kind=kOutput, calls=%fused_computation.24 | convolution fusion | flops 402948096 | bytes 2375680 | tf_op jit(solution)/shard_map/gkpn,sgkp,gks->sgn/dot_general | solution.py:181
  191.4 1.7 copy.162
  194.2 1.4 slice_multiply_fusion.5
  195.6 4.0 %fusion.6 = f32[128,2,128]{0,2,1:T(8,128)} fusion(f32[128,2,128]{0,2,1:T(8,128)} %bitcast.342, f32[2,16,64,128]{3,2,1,0:T(8,128)} %copy-done.8, f32[128,2,16,64]{0,3,2,1:T(8,128)} %bitcast.327, f32[128,2,16]{0,2,1:T(8,128)S(1)} %copy-done.36), kind=kOutput, calls=%fused_computation.25 | convolution fusion | flops 402948096 | bytes 2375680 | tf_op jit(solution)/shard_map/tgkp,gkpn->tgn/dot_general | solution.py:174
  199.6 1.7 copy.164
  203.8 2.3 %collective-permute-start.6 = (f32[3,2560]{1,0:T(4,128)S(1)}, f32[3,2560]{1,0:T(4,128)S(1)}, u32[]{:S(2)}, u32[]{:S(2)}) collective-permute-start(f32[3,2560]{1,0:T(4,128)S(1)} %maximum_maximum_fusion), channel_id=1, source_target_pairs={{4,0},{8,4},{12,8},{5,1},{9,5},{13,9},{6,2},{10,6},{14,10},{7,3},{... | collective-permute-start | bytes 92168 | tf_op jit(solution)/shard_map/ppermute | solution.py:22
  206.9 1.7 add_convert_fusion.2
  208.6 1.7 add_convert_fusion.3
  210.4 2.8 %add_convert_fusion = bf16[1,128,2048]{2,1,0:T(8,128)(2,1)} fusion(f32[1,127,2048]{2,1,0:T(8,128)} %slice.630, f32[1,126,2048]{2,1,0:T(8,128)} %slice.629, f32[1,125,2048]{2,1,0:T(8,128)S(1)} %copy-done.13, f32[1,128,2048]{2,1,0:T(8,128)S(1)} %fusion.26, f32[2048]{0:T(1024)} %bitcast.361, f32[2048]{0:T(1024)} %bitcast.359, f32[2048]{0:T(1024)} %bitcast.357, ...), kind=kLoop, calls=%fused_computation.65 | loop fusion | flops 2097152 | bytes 4702208 | tf_op jit(solution)/shard_map/convert_element_type | solution.py:420
  217.1 1.2 add_convert_fusion.1
  (296 shorter events, 48.6 us)
Async XLA Ops:
  0.6 22.7 %copy-start.23 = (bf16[1,128,2048]{2,1,0:T(8,128)(2,1)S(1)}, bf16[1,128,2048]{2,1,0:T(8,128)(2,1)}, u32[]{:S(2)}) copy-start(bf16[1,128,2048]{2,1,0:T(8,128)(2,1)} %param.26) | copy-start | bytes 1572868
  0.6 23.7 %copy-start.14 = (bf16[128,2048]{1,0:T(8,128)(2,1)S(1)}, bf16[128,2048]{1,0:T(8,128)(2,1)}, u32[]{:S(2)}) copy-start(bf16[128,2048]{1,0:T(8,128)(2,1)} %param.25) | copy-start | bytes 1572868
  4.2 20.3 %collective-permute-start = (f32[7712]{0:T(1024)S(1)}, f32[7712]{0:T(1024)S(1)}, u32[]{:S(2)}, u32[]{:S(2)}) collective-permute-start(f32[7712]{0:T(1024)S(1)} %pad_maximum_fusion.9), channel_id=1, source_target_pairs={{0,4},{4,8},{8,12},{12,0},{1,5},{5,9},{9,13},{13,1},{2,6},{6,10},{... | collective-permute-start | bytes 92552 | tf_op jit(solution)/shard_map/ppermute | solution.py:252
  6.9 17.7 %collective-permute-start.1 = (f32[7712]{0:T(1024)S(1)}, f32[7712]{0:T(1024)S(1)}, u32[]{:S(2)}, u32[]{:S(2)}) collective-permute-start(f32[7712]{0:T(1024)S(1)} %pad_maximum_fusion.9), channel_id=1, source_target_pairs={{0,8},{4,12},{8,0},{12,4},{1,9},{5,13},{9,1},{13,5},{2,10},{6,14},... | collective-permute-start | bytes 92552 | tf_op jit(solution)/shard_map/ppermute | solution.py:252
  6.9 17.8 %collective-permute-start.2 = (f32[7712]{0:T(1024)S(1)}, f32[7712]{0:T(1024)S(1)}, u32[]{:S(2)}, u32[]{:S(2)}) collective-permute-start(f32[7712]{0:T(1024)S(1)} %pad_maximum_fusion.9), channel_id=1, source_target_pairs={{0,12},{4,0},{8,4},{12,8},{1,13},{5,1},{9,5},{13,9},{2,14},{6,2},{... | collective-permute-start | bytes 92552 | tf_op jit(solution)/shard_map/ppermute | solution.py:252
  9.6 7.4 %copy-start.57 = (f32[2,16]{1,0:T(2,128)}, f32[2,16]{1,0:T(2,128)S(1)}, u32[]{:S(2)}) copy-start(f32[2,16]{1,0:T(2,128)S(1)} %mul.999) | copy-start | bytes 388
  11.2 16.4 %copy-start.67 = (f32[1,256]{1,0:T(1,128)}, f32[1,256]{1,0:T(1,128)S(1)}, u32[]{:S(2)}) copy-start(f32[1,256]{1,0:T(1,128)S(1)} %get-tuple-element.119) | copy-start | bytes 3076
  11.2 16.4 %copy-start.68 = (f32[1,256]{1,0:T(1,128)}, f32[1,256]{1,0:T(1,128)S(1)}, u32[]{:S(2)}) copy-start(f32[1,256]{1,0:T(1,128)S(1)} %get-tuple-element.120) | copy-start | bytes 3076
  11.2 16.4 %copy-start.69 = (f32[1,256]{1,0:T(1,128)}, f32[1,256]{1,0:T(1,128)S(1)}, u32[]{:S(2)}) copy-start(f32[1,256]{1,0:T(1,128)S(1)} %get-tuple-element.121) | copy-start | bytes 3076
  11.2 16.4 %copy-start.70 = (f32[1,256]{1,0:T(1,128)}, f32[1,256]{1,0:T(1,128)S(1)}, u32[]{:S(2)}) copy-start(f32[1,256]{1,0:T(1,128)S(1)} %get-tuple-element.122) | copy-start | bytes 3076
  12.0 15.5 %copy-start.71 = (f32[1,256]{1,0:T(1,128)}, f32[1,256]{1,0:T(1,128)S(1)}, u32[]{:S(2)}) copy-start(f32[1,256]{1,0:T(1,128)S(1)} %get-tuple-element.115) | copy-start | bytes 3076
  12.0 15.5 %copy-start.72 = (f32[1,256]{1,0:T(1,128)}, f32[1,256]{1,0:T(1,128)S(1)}, u32[]{:S(2)}) copy-start(f32[1,256]{1,0:T(1,128)S(1)} %get-tuple-element.116) | copy-start | bytes 3076
  12.0 15.5 %copy-start.73 = (f32[1,256]{1,0:T(1,128)}, f32[1,256]{1,0:T(1,128)S(1)}, u32[]{:S(2)}) copy-start(f32[1,256]{1,0:T(1,128)S(1)} %get-tuple-element.117) | copy-start | bytes 3076
  12.0 15.5 %copy-start.74 = (f32[1,256]{1,0:T(1,128)}, f32[1,256]{1,0:T(1,128)S(1)}, u32[]{:S(2)}) copy-start(f32[1,256]{1,0:T(1,128)S(1)} %get-tuple-element.118) | copy-start | bytes 3076
  12.9 15.5 %copy-start.46 = (f32[1,2048]{1,0:T(1,128)}, f32[1,2048]{1,0:T(1,128)S(1)}, u32[]{:S(2)}) copy-start(f32[1,2048]{1,0:T(1,128)S(1)} %get-tuple-element.101) | copy-start | bytes 24580
  13.0 15.5 %copy-start.47 = (f32[1,2048]{1,0:T(1,128)}, f32[1,2048]{1,0:T(1,128)S(1)}, u32[]{:S(2)}) copy-start(f32[1,2048]{1,0:T(1,128)S(1)} %get-tuple-element.102) | copy-start | bytes 24580
  13.0 15.5 %copy-start.48 = (f32[1,2048]{1,0:T(1,128)}, f32[1,2048]{1,0:T(1,128)S(1)}, u32[]{:S(2)}) copy-start(f32[1,2048]{1,0:T(1,128)S(1)} %get-tuple-element.103) | copy-start | bytes 24580
  13.0 15.5 %copy-start.49 = (f32[1,2048]{1,0:T(1,128)}, f32[1,2048]{1,0:T(1,128)S(1)}, u32[]{:S(2)}) copy-start(f32[1,2048]{1,0:T(1,128)S(1)} %get-tuple-element.104) | copy-start | bytes 24580
  15.7 7.6 %copy-start.37 = (f32[1,2,16,128]{3,2,1,0:T(8,128)}, f32[1,2,16,128]{3,2,1,0:T(8,128)S(1)}, u32[]{:S(2)}) copy-start(f32[1,2,16,128]{3,2,1,0:T(8,128)S(1)} %reduce_window_sum.48) | copy-start | bytes 49156
  15.7 32.5 %copy-start.31 = (f32[128,2,16]{0,2,1:T(8,128)}, f32[128,2,16]{0,2,1:T(8,128)S(1)}, u32[]{:S(2)}) copy-start(f32[128,2,16]{0,2,1:T(8,128)S(1)} %exponential_bitcast_fusion.1) | copy-start | bytes 49156
  24.6 24.7 %copy-start.3 = (f32[128,2048]{0,1:T(8,128)}, f32[128,2048]{0,1:T(8,128)S(1)}, u32[]{:S(2)}) copy-start(f32[128,2048]{0,1:T(8,128)S(1)} %copy.119) | copy-start | bytes 3145732
  28.4 4.5 %copy-start.16 = (f32[128,256]{1,0:T(8,128)}, f32[128,256]{1,0:T(8,128)S(1)}, u32[]{:S(2)}) copy-start(f32[128,256]{1,0:T(8,128)S(1)} %get-tuple-element.129.b_ref) | copy-start | bytes 393220
  33.0 10.1 %copy-start.7 = (f32[128,2048]{1,0:T(8,128)}, f32[128,2048]{1,0:T(8,128)S(1)}, u32[]{:S(2)}) copy-start(f32[128,2048]{1,0:T(8,128)S(1)} %get-tuple-element.59.x_ref) | copy-start | bytes 3145732
  33.3 13.1 %copy-start.1 = (f32[128,2048]{0,1:T(8,128)}, f32[128,2048]{0,1:T(8,128)S(1)}, u32[]{:S(2)}) copy-start(f32[128,2048]{0,1:T(8,128)S(1)} %copy.117) | copy-start | bytes 3145732
  37.3 10.9 %copy-start.15 = (f32[128,2,128]{2,1,0:T(2,128)}, f32[128,2,128]{2,1,0:T(2,128)S(1)}, u32[]{:S(2)}) copy-start(f32[128,2,128]{2,1,0:T(2,128)S(1)} %reshape.551) | copy-start | bytes 393220
  44.6 5.8 %copy-start.5 = (f32[1,128,2048]{1,2,0:T(8,128)}, f32[1,128,2048]{1,2,0:T(8,128)S(1)}, u32[]{:S(2)}) copy-start(f32[1,128,2048]{1,2,0:T(8,128)S(1)} %copy.121) | copy-start | bytes 3145732
  48.2 4.2 %copy-start.10 = (f32[1,2,16,64,128]{4,3,2,1,0:T(8,128)}, f32[1,2,16,64,128]{4,3,2,1,0:T(8,128)S(1)}, u32[]{:S(2)}) copy-start(f32[1,2,16,64,128]{4,3,2,1,0:T(8,128)S(1)} %convolution_bitcast_fusion.5) | copy-start | bytes 3145732
  52.4 7.1 %collective-permute-start.3 = (f32[3,2,16,64,128]{4,3,2,1,0:T(8,128)}, f32[3,2,16,64,128]{4,3,2,1,0:T(8,128)}, u32[]{:S(2)}, u32[]{:S(2)}) collective-permute-start(f32[3,2,16,64,128]{4,3,2,1,0:T(8,128)} %pad_maximum_fusion), channel_id=1, source_target_pairs={{0,4},{4,0},{8,12},{12,8},{1,5},{5,1},{9,13},{13,9},{2,6},{6,2},{1... | collective-permute-start | bytes 9437192 | tf_op jit(solution)/shard_map/ppermute | solution.py:336
  55.3 7.7 %copy-start.76 = (f32[2,16]{1,0:T(2,128)}, f32[2,16]{1,0:T(2,128)S(1)}, u32[]{:S(2)}) copy-start(f32[2,16]{1,0:T(2,128)S(1)} %get-tuple-element.105) | copy-start | bytes 388
  55.3 7.7 %copy-start.78 = (f32[2,16]{1,0:T(2,128)}, f32[2,16]{1,0:T(2,128)S(1)}, u32[]{:S(2)}) copy-start(f32[2,16]{1,0:T(2,128)S(1)} %get-tuple-element.106) | copy-start | bytes 388
  63.0 31.7 %copy-start.28 = (bf16[4,2048]{1,0:T(4,128)(2,1)S(1)}, bf16[4,2048]{1,0:T(4,128)(2,1)}, u32[]{:S(2)}) copy-start(bf16[4,2048]{1,0:T(4,128)(2,1)} %param.34) | copy-start | bytes 49156
  65.3 24.7 %collective-permute-start.4 = (f32[2,16,64,128]{3,2,1,0:T(8,128)}, f32[2,16,64,128]{3,2,1,0:T(8,128)}, u32[]{:S(2)}, u32[]{:S(2)}) collective-permute-start(f32[2,16,64,128]{3,2,1,0:T(8,128)} %get-tuple-element.53), channel_id=1, source_target_pairs={{0,8},{4,12},{8,0},{12,4},{1,9},{5,13},{9,1},{13,5},{2,10},{6,14},... | collective-permute-start | bytes 3145736 | tf_op jit(solution)/shard_map/ppermute | solution.py:356
  66.1 61.1 %copy-start.20 = (f32[2,16,128]{1,0,2:T(2,128)}, f32[2,16,128]{1,0,2:T(2,128)S(1)}, u32[]{:S(2)}) copy-start(f32[2,16,128]{1,0,2:T(2,128)S(1)} %copy.109) | copy-start | bytes 49156
  90.0 40.6 %collective-permute-start.5 = (f32[2,16,64,128]{3,2,1,0:T(8,128)}, f32[2,16,64,128]{3,2,1,0:T(8,128)}, u32[]{:S(2)}, u32[]{:S(2)}) collective-permute-start(f32[2,16,64,128]{3,2,1,0:T(8,128)} %collective-permute-done.4), channel_id=1, source_target_pairs={{0,4},{4,0},{8,12},{12,8},{1,5},{5,1},{9,13},{13,9},{2,6},{6,2},{1... | collective-permute-start | bytes 3145736 | tf_op jit(solution)/shard_map/ppermute | solution.py:357
  105.5 25.0 %copy-start.77 = (f32[2,16]{1,0:T(2,128)S(1)}, f32[2,16]{1,0:T(2,128)}, u32[]{:S(2)}) copy-start(f32[2,16]{1,0:T(2,128)} %copy-done.76) | copy-start | bytes 388
  105.6 25.0 %copy-start.79 = (f32[2,16]{1,0:T(2,128)S(1)}, f32[2,16]{1,0:T(2,128)}, u32[]{:S(2)}) copy-start(f32[2,16]{1,0:T(2,128)} %copy-done.78) | copy-start | bytes 388
  130.5 6.5 %copy-start.4 = (f32[128,2048]{0,1:T(8,128)S(1)}, f32[128,2048]{0,1:T(8,128)}, u32[]{:S(2)}) copy-start(f32[128,2048]{0,1:T(8,128)} %copy-done.3) | copy-start | bytes 3145732
  130.5 6.5 %copy-start.18 = (f32[128,2,128]{2,1,0:T(2,128)S(1)}, f32[128,2,128]{2,1,0:T(2,128)}, u32[]{:S(2)}) copy-start(f32[128,2,128]{2,1,0:T(2,128)} %reshape.549) | copy-start | bytes 393220
  130.5 6.5 %copy-start.35 = (f32[128,2,16]{0,2,1:T(8,128)S(1)}, f32[128,2,16]{0,2,1:T(8,128)}, u32[]{:S(2)}) copy-start(f32[128,2,16]{0,2,1:T(8,128)} %get-tuple-element.99) | copy-start | bytes 49156
  136.0 6.0 %copy-start.19 = (f32[2,16,128]{1,0,2:T(2,128)S(1)}, f32[2,16,128]{1,0,2:T(2,128)}, u32[]{:S(2)}) copy-start(f32[2,16,128]{1,0,2:T(2,128)} %copy.114) | copy-start | bytes 49156
  136.1 6.0 %copy-start.21 = (f32[2,16,128]{1,0,2:T(2,128)S(1)}, f32[2,16,128]{1,0,2:T(2,128)}, u32[]{:S(2)}) copy-start(f32[2,16,128]{1,0,2:T(2,128)} %copy-done.20) | copy-start | bytes 49156
  137.1 5.2 %copy-start.27 = (f32[2,16,128]{1,0,2:T(2,128)S(1)}, f32[2,16,128]{1,0,2:T(2,128)}, u32[]{:S(2)}) copy-start(f32[2,16,128]{1,0,2:T(2,128)} %copy.137) | copy-start | bytes 49156
  137.1 5.3 %copy-start.75 = (f32[2,16,1]{1,0,2:T(2,128)S(1)}, f32[2,16,1]{1,0,2:T(2,128)}, u32[]{:S(2)}) copy-start(f32[2,16,1]{1,0,2:T(2,128)} %copy.174) | copy-start | bytes 388
  137.1 5.3 %copy-start.82 = (f32[2,16]{1,0:T(2,128)S(1)}, f32[2,16]{1,0:T(2,128)}, u32[]{:S(2)}) copy-start(f32[2,16]{1,0:T(2,128)} %get-tuple-element.44) | copy-start | bytes 388
  138.2 5.0 %copy-start.26 = (f32[2,16,128]{1,0,2:T(2,128)S(1)}, f32[2,16,128]{1,0,2:T(2,128)}, u32[]{:S(2)}) copy-start(f32[2,16,128]{1,0,2:T(2,128)} %copy.134) | copy-start | bytes 49156
  138.2 5.0 %copy-start.58 = (f32[2,16]{1,0:T(2,128)S(1)}, f32[2,16]{1,0:T(2,128)}, u32[]{:S(2)}) copy-start(f32[2,16]{1,0:T(2,128)} %copy-done.57) | copy-start | bytes 388
  138.2 5.2 %copy-start.38 = (f32[32,1,128]{2,1,0:T(1,128)S(1)}, f32[32,1,128]{2,1,0:T(1,128)}, u32[]{:S(2)}) copy-start(f32[32,1,128]{2,1,0:T(1,128)} %param.29) | copy-start | bytes 49156
  138.2 5.2 %copy-start.40 = (f32[32,128]{1,0:T(8,128)S(1)}, f32[32,128]{1,0:T(8,128)}, u32[]{:S(2)}) copy-start(f32[32,128]{1,0:T(8,128)} %param.24) | copy-start | bytes 49156
  138.2 5.2 %copy-start.80 = (f32[32]{0:T(128)S(1)}, f32[32]{0:T(128)}, u32[]{:S(2)}) copy-start(f32[32]{0:T(128)} %param.38) | copy-start | bytes 388
  141.9 17.4 %copy-start.6 = (f32[1,128,2048]{1,2,0:T(8,128)S(1)}, f32[1,128,2048]{1,2,0:T(8,128)}, u32[]{:S(2)}) copy-start(f32[1,128,2048]{1,2,0:T(8,128)} %copy-done.5) | copy-start | bytes 3145732
  141.9 17.4 %copy-start.9 = (f32[2,16,64,128]{3,2,1,0:T(8,128)S(1)}, f32[2,16,64,128]{3,2,1,0:T(8,128)}, u32[]{:S(2)}) copy-start(f32[2,16,64,128]{3,2,1,0:T(8,128)} %get-tuple-element.63) | copy-start | bytes 3145732
  141.9 17.4 %copy-start.32 = (f32[128,2,16]{0,2,1:T(8,128)S(1)}, f32[128,2,16]{0,2,1:T(8,128)}, u32[]{:S(2)}) copy-start(f32[128,2,16]{0,2,1:T(8,128)} %copy-done.31) | copy-start | bytes 49156
  144.1 19.2 %copy-start.24 = (f32[1,128,256]{2,1,0:T(8,128)S(1)}, f32[1,128,256]{2,1,0:T(8,128)}, u32[]{:S(2)}) copy-start(f32[1,128,256]{2,1,0:T(8,128)} %get-tuple-element.50) | copy-start | bytes 393220
  158.3 5.1 %copy-start.41 = (f32[128,256]{1,0:T(8,128)S(1)}, f32[128,256]{1,0:T(8,128)}, u32[]{:S(2)}) copy-start(f32[128,256]{1,0:T(8,128)} %get-tuple-element.34) | copy-start | bytes 393220
  172.0 42.6 %collective-permute-start.7 = (f32[3,2560]{1,0:T(4,128)}, f32[3,2560]{1,0:T(4,128)}, u32[]{:S(2)}, u32[]{:S(2)}) collective-permute-start(f32[3,2560]{1,0:T(4,128)} %pad_maximum_fusion.8), channel_id=1, source_target_pairs={{0,12},{1,13},{2,14},{3,15},{16,28},{17,29},{18,30},{19,31}} | collective-permute-start | bytes 92168 | tf_op jit(solution)/shard_map/ppermute | solution.py:407
  173.2 41.3 %collective-permute-start.8 = (f32[3,2560]{1,0:T(4,128)}, f32[3,2560]{1,0:T(4,128)}, u32[]{:S(2)}, u32[]{:S(2)}) collective-permute-start(f32[3,2560]{1,0:T(4,128)} %pad_maximum_fusion.8), channel_id=1, source_target_pairs={{4,12},{5,13},{6,14},{7,15},{20,28},{21,29},{22,30},{23,31}} | collective-permute-start | bytes 92168 | tf_op jit(solution)/shard_map/ppermute | solution.py:407
  175.8 38.8 %collective-permute-start.9 = (f32[3,2560]{1,0:T(4,128)}, f32[3,2560]{1,0:T(4,128)}, u32[]{:S(2)}, u32[]{:S(2)}) collective-permute-start(f32[3,2560]{1,0:T(4,128)} %pad_maximum_fusion.8), channel_id=1, source_target_pairs={{8,12},{9,13},{10,14},{11,15},{24,28},{25,29},{26,30},{27,31}} | collective-permute-start | bytes 92168 | tf_op jit(solution)/shard_map/ppermute | solution.py:407
  183.7 4.0 %copy-start.2 = (f32[128,2048]{0,1:T(8,128)S(1)}, f32[128,2048]{0,1:T(8,128)}, u32[]{:S(2)}) copy-start(f32[128,2048]{0,1:T(8,128)} %copy-done.1) | copy-start | bytes 3145732
  183.8 4.0 %copy-start.25 = (f32[128,256]{0,1:T(8,128)S(1)}, f32[128,256]{0,1:T(8,128)}, u32[]{:S(2)}) copy-start(f32[128,256]{0,1:T(8,128)} %copy.161) | copy-start | bytes 393220
  185.1 10.5 %copy-start.36 = (f32[128,2,16]{0,2,1:T(8,128)S(1)}, f32[128,2,16]{0,2,1:T(8,128)}, u32[]{:S(2)}) copy-start(f32[128,2,16]{0,2,1:T(8,128)} %get-tuple-element.99) | copy-start | bytes 49156
  191.4 18.9 %copy-start.13 = (f32[1,125,2048]{2,1,0:T(8,128)S(1)}, f32[1,125,2048]{2,1,0:T(8,128)}, u32[]{:S(2)}) copy-start(f32[1,125,2048]{2,1,0:T(8,128)} %slice.628) | copy-start | bytes 3072004
  202.3 10.9 %copy-start.39 = (f32[32,1,128]{2,1,0:T(1,128)S(1)}, f32[32,1,128]{2,1,0:T(1,128)}, u32[]{:S(2)}) copy-start(f32[32,1,128]{2,1,0:T(1,128)} %param.29) | copy-start | bytes 49156
  202.3 10.8 %copy-start.81 = (f32[32]{0:T(128)S(1)}, f32[32]{0:T(128)}, u32[]{:S(2)}) copy-start(f32[32]{0:T(128)} %param.38) | copy-start | bytes 388
  203.8 10.7 %collective-permute-start.6 = (f32[3,2560]{1,0:T(4,128)S(1)}, f32[3,2560]{1,0:T(4,128)S(1)}, u32[]{:S(2)}, u32[]{:S(2)}) collective-permute-start(f32[3,2560]{1,0:T(4,128)S(1)} %maximum_maximum_fusion), channel_id=1, source_target_pairs={{4,0},{8,4},{12,8},{5,1},{9,5},{13,9},{6,2},{10,6},{14,10},{7,3},{... | collective-permute-start | bytes 92168 | tf_op jit(solution)/shard_map/ppermute | solution.py:22
  (29 other events, 59.7 us)

commit v5 on v3

--- a/solution.py
+++ b/solution.py
@@ -14,12 +14,6 @@
 
 
 EXACT_DOT = lax.Precision.HIGHEST
-
-
-def from_behind(block, axis, distance):
-    devices = range(lax.axis_size(axis))
-    route = [(i - distance, i) for i in devices if i - distance in devices]
-    return lax.ppermute(block, axis, route)
 
 
 def causal_conv(values, context, taps):
@@ -365,13 +359,17 @@
     )
     prefix_ddt = step_pullback(d_step.reshape(num_heads, prompt_len))[0]
     left_grads = jnp.concatenate([prompt_grads[3], prompt_grads[4], prompt_grads[5]], axis=1)
-    from_right = from_behind(left_grads, "suf", -1)
     ctx_grads = jnp.concatenate(
         [jnp.sum(conv_grads[3], axis=0), jnp.sum(conv_grads[4], axis=0), jnp.sum(conv_grads[5], axis=0)],
         axis=1,
     )
+    from_right = lax.ppermute(
+        jnp.where(my_index == 0, ctx_grads, left_grads),
+        "suf",
+        [(j, (j - 1) % num_ways) for j in range(num_ways)],
+    )
     from_suffix = ctx_grads
-    for sender in range(num_ways - 1):
+    for sender in range(1, num_ways - 1):
         from_suffix = from_suffix + lax.ppermute(ctx_grads, "suf", [(sender, num_ways - 1)])
     last_device = my_index == num_ways - 1
     tail_add = split_tokens(from_right + jnp.where(last_device, from_suffix, 0.0))

time: 208 us -> 219 us (1.053)
  other arithmetic: 65 us -> 77.3 us
  local copies, waits for them, and re-layouts: 52.3 us -> 56.8 us
  starting transfers between devices: 13.1 us -> 9.54 us
  matrix products: 16.2 us -> 13.1 us
    mul x12, other arithmetic: 7.82 us -> 12.4 us  [causal_conv(): padded[tap_index:tap_index + num_tokens]]
    rev x4, local copies, waits for them, and re-layouts: 0.26 us -> 3.32 us  [block_outer(): d_log = jnp.flip(jnp.cumsum(jnp.flip(d_cum, -1), axis=-1), -1)]
    ppermute x1, starting transfers between devices: 2.27 us -> 0.01 us  [shards(): lax.ppermute(jnp.where(my_index == 0, ctx_grads, left_grads), 'suf', [(j,...]
    unnamed x185 -> x209, local copies, waits for them, and re-layouts: 6.58 us -> 5.01 us
    ppermute x3 -> x2, starting transfers between devices: 5.07 us -> 3.77 us  [shards(): lax.ppermute(ctx_grads, 'suf', [(sender, num_ways - 1)])]
  transfers between devices with their start and end apart: 10 -> 9, of which waited for: 2 -> 2; matrix products, arithmetic and copies ran while one was open for 34% -> 25% of each run, Pallas kernels for 7% -> 6%
where the time goes in v5:
time: 219 us; the launch traced here: 217 us
  other arithmetic  77.3 us (35%)
  local copies, waits for them, and re-layouts  56.8 us (26%)
  Pallas kernels  28.4 us (13%)
  waiting for transfers between devices  28.1 us (13%)
  matrix products  13.1 us (6%)
  starting transfers between devices  9.54 us (4%)
  between operations  3.37 us (2%)
    pallas_call x2, Pallas kernels, block_inner(): pl.pallas_call(functools.partial(_grad_kernel, steps_per_group), grid=(nh...  28.4 us
    ppermute x1, waiting for transfers between devices, shards(): incoming = lax.ppermute(outgoing, 'suf', route)  24.4 us
    mul x12, other arithmetic, causal_conv(): padded[tap_index:tap_index + num_tokens]  12.4 us
    reshape x2, other arithmetic, block_inner(): pl.pallas_call(functools.partial(_grad_kernel, steps_per_group), grid=(nh...  7.26 us
    reduce_sum x1, other arithmetic, block_outer(): jnp.sum(lam * S0, axis=(-2, -1))  5.49 us
    split x3, local copies, waits for them, and re-layouts, causal_conv(): padded = jnp.concatenate([context, values], axis=0)  5.33 us
    unnamed x209, local copies, waits for them, and re-layouts  5.01 us
  transfers between devices with their start and end apart: 9, of which 2 were waited for; matrix products, arithmetic and copies ran while one was open for 25% of the time, Pallas kernels for 6%

profile of v5, /device:TPU:1, one launch (start us, length us, event | category | flops | bytes accessed | tf_op | source)
XLA Modules:
  0.0 216.6 jit_solution(12641198313519664167)
XLA Ops:
  4.2 2.7 %collective-permute-start = (f32[7712]{0:T(1024)S(1)}, f32[7712]{0:T(1024)S(1)}, u32[]{:S(2)}, u32[]{:S(2)}) collective-permute-start(f32[7712]{0:T(1024)S(1)} %pad_maximum_fusion.9), channel_id=1, source_target_pairs={{0,4},{4,8},{8,12},{12,0},{1,5},{5,9},{9,13},{13,1},{2,6},{6,10},{... | collective-permute-start | bytes 92552 | tf_op jit(solution)/shard_map/ppermute | solution.py:214
  7.3 1.4 exponential_multiply_fusion.1
  12.0 1.5 slice_convert_fusion.6
  16.2 1.2 fusion.113
  19.3 1.2 convert_element_type.162
  26.5 2.6 %fusion.37 = (f32[128,2048]{1,0:T(8,128)S(1)}, f32[128,2048]{1,0:T(8,128)}) fusion(f32[128,2048]{1,0:T(8,128)S(1)} %copy-done.21, f32[2048]{0:T(1024)} %bitcast.272, f32[2048]{0:T(1024)} %bitcast.268, f32[3,2048]{1,0:T(4,128)} %slice.288, f32[2048]{0:T(1024)} %bitcast.264, f32[2048]{0:T(1024)} %bitcast.260), kind=kLoop, calls=%fused_computation.84 | loop fusion | flops 3670016 | bytes 3203072 | tf_op jit(solution)/shard_map/jvp(jit(silu))/mul | solution.py:27
  29.4 1.7 multiply_bitcast_fusion.1
  31.9 5.6 %multiply_bitcast_fusion = (f32[128,2048]{1,0:T(8,128)}, f32[1,128,2048]{2,1,0:T(8,128)}, f32[1,128,2048]{2,1,0:T(8,128)}, f32[128,2048]{1,0:T(8,128)}) fusion(f32[1,128,2048]{2,1,0:T(8,128)} %convert_element_type.169, f32[2048]{0:T(1024)} %bitcast.273, f32[2048]{0:T(1024)} %bitcast.269, f32[1,3,2048]{2,1,0:T(4,128)} %slice_bitcast_fusion.5, ...), kind=kLoop, calls=%fused_computation.76 | loop fusion | flops 4194304 | bytes 5825024 | tf_op jit(solution)/shard_map/vmap()/squeeze;vmap()/reshape;vmap()/reshape | solution.py:96
  37.4 1.5 copy.123
  40.1 1.8 convolution_bitcast_fusion.5
  44.1 1.9 pad_maximum_fusion
  46.0 1.4 collective-permute-start.3
  49.4 3.6 %collective-permute-done.3 = f32[3,2,16,64,128]{4,3,2,1,0:T(8,128)} collective-permute-done((f32[3,2,16,64,128]{4,3,2,1,0:T(8,128)}, f32[3,2,16,64,128]{4,3,2,1,0:T(8,128)}, u32[]{:S(2)}, u32[]{:S(2)}) %collective-permute-start.3) | collective-permute-done | bytes 3145760 | tf_op jit(solution)/shard_map/ppermute | solution.py:298
  53.0 3.5 %broadcast_select_fusion.1 = (f32[3,2,16,64,128]{4,3,2,1,0:T(8,128)S(1)}, f32[3,2,16,64,128]{4,3,2,1,0:T(8,128)S(1)}) fusion(f32[3,2,16,64,128]{4,3,2,1,0:T(8,128)} %collective-permute-done.3, pred[]{:T(512)S(6)} %eq.61, f32[1,2,16,64,128]{4,3,2,1,0:T(8,128)} %copy-done.14, f32[1,2,16,64,128]{4,3,2,1,0:T(8,128)} %copy-done.15, ...), kind=kLoop, calls=%fused_computation.9 | loop fusion | flops 3145728 | bytes 12582913 | tf_op jit(solution)/shard_map/jit(_where)/select_n | solution.py:300
  56.6 2.0 fusion.31
  58.6 24.4 %collective-permute-done.4 = f32[2,16,64,128]{3,2,1,0:T(8,128)} collective-permute-done((f32[2,16,64,128]{3,2,1,0:T(8,128)S(1)}, f32[2,16,64,128]{3,2,1,0:T(8,128)}, u32[]{:S(2)}, u32[]{:S(2)}) %collective-permute-start.4) | collective-permute-done | bytes 1048608 | tf_op jit(solution)/shard_map/ppermute | solution.py:318
  83.0 1.2 collective-permute-start.5
  84.2 2.1 convert_element_type.163.g_ref
  86.3 1.5 copy.111
  88.5 1.6 negate_multiply_fusion
  90.0 1.6 copy.112
  91.6 1.9 reduce_window_sum.47
  93.5 1.4 slice.303
  94.9 1.3 copy.177
  96.2 1.4 exponential_bitcast_fusion
  97.6 1.5 copy.116
  99.1 1.3 broadcast_in_dim.54
  100.4 1.4 broadcast_in_dim.59.skip_ref
  101.8 1.3 multiply_reduce_fusion.2
  103.1 1.3 mul.870
  104.3 1.3 mul.918
  105.6 14.1 %shard_map.242 = (f32[128,2048]{1,0:T(8,128)}, f32[32,128]{1,0:T(8,128)}, f32[32,128]{1,0:T(8,128)}, f32[128,256]{1,0:T(8,128)}, f32[128,256]{1,0:T(8,128)}) custom-call(f32[128,2048]{1,0:T(8,128)} %copy-done.9, f32[128,2048]{1,0:T(8,128)} %convert_element_type.163.g_ref, f32[128,256]{1,0:T(8,128)} %copy-done.26, f32[128,256]{1,0:T(8,128)} %get-tuple-element.67.c_ref, ...), custom_call_target="tpu_custom_call" | custom-call | tf_op jit(solution)/shard_map/pallas_call | solution.py:96
  119.7 1.5 copy.140
  121.2 1.5 copy.137
  122.6 2.5 %copy.113 = f32[128,2048]{0,1:T(8,128)} copy(f32[128,2048]{1,0:T(8,128)} %get-tuple-element.30) | data formatting | bytes 2097152 | tf_op jit(solution)/shard_map/pallas_call | solution.py:96
  125.1 1.6 copy.166
  126.8 1.7 copy.168
  128.5 5.5 %multiply_reduce_fusion = (f32[2,16]{1,0:T(2,128)}, f32[2,16,64,128]{3,2,1,0:T(8,128)S(1)}, f32[2,16,64,128]{3,2,1,0:T(8,128)}, f32[2,16,64,128]{3,2,1,0:T(8,128)}) fusion(f32[3,2,16,64,128]{4,3,2,1,0:T(8,128)} %copy-done, f32[2,16]{1,0:T(2,128)} %copy-done.100, f32[2,16,64,128]{3,2,1,0:T(8,128)} %get-tuple-element.66, ...), kind=kLoop, calls=%fused_computation.70 | loop fusion | flops 6553568 | bytes 10486407 | tf_op jit(solution)/shard_map/reduce_sum | solution.py:147
  138.0 1.7 fusion.104
  140.3 1.7 fusion.91
  142.0 1.3 fusion.111
  143.3 1.6 rev.14
  144.9 1.6 copy.141
  146.5 1.9 reduce_window_sum.49
  148.4 1.5 copy.142
  149.8 1.8 fusion.93
  151.6 1.6 copy.143
  153.3 2.5 %multiply_add_fusion = f32[128,2,16,64]{0,3,2,1:T(8,128)} fusion(f32[128,2,16,64]{0,3,2,1:T(8,128)} %bitcast.242, f32[128,2,16,64]{0,3,2,1:T(8,128)S(1)} %get-tuple-element.130, f32[128,2,16]{0,2,1:T(8,128)S(1)} %copy.118), kind=kLoop, calls=%fused_computation.78 | loop fusion | flops 524288 | bytes 3162112 | tf_op jit(solution)/shard_map/add | solution.py:142
  155.8 2.6 %copy.126 = f32[128,2048]{1,0:T(8,128)} copy(f32[128,2048]{0,1:T(8,128)} %bitcast.243) | data formatting | bytes 2097152 | tf_op jit(solution)/shard_map/reshape | solution.py:358
  158.4 2.6 %broadcast_multiply_fusion.4 = (f32[128,2048]{1,0:T(8,128)}, f32[128,2048]{1,0:T(8,128)S(1)}) fusion(f32[2048]{0:T(1024)S(1)} %bitcast.274, f32[128,2048]{1,0:T(8,128)S(1)} %copy-done.22, f32[128,2048]{1,0:T(8,128)} %copy.126), kind=kLoop, calls=%fused_computation.98 | loop fusion | flops 2621440 | bytes 4202496 | tf_op jit(solution)/shard_map/transpose(jvp())/mul | solution.py:24
  161.1 1.8 broadcast_multiply_fusion.5
  163.0 1.8 fusion.5
  166.0 1.5 broadcast_multiply_fusion.21
  167.5 1.8 fusion.6
  171.8 14.4 %vmap__.1 = (f32[128,2048]{1,0:T(8,128)}, f32[32,128]{1,0:T(8,128)}, f32[32,128]{1,0:T(8,128)}, f32[128,256]{1,0:T(8,128)}, f32[128,256]{1,0:T(8,128)}) custom-call(f32[128,2048]{1,0:T(8,128)} %get-tuple-element.57.x_ref, f32[128,2048]{1,0:T(8,128)} %get-tuple-element.136.g_ref, f32[128,256]{1,0:T(8,128)} %get-tuple-element.55.b_ref, ...), custom_call_target="tpu_custom_call" | custom-call | tf_op jit(solution)/shard_map/vmap()/pallas_call | solution.py:96
  186.2 1.7 broadcast_multiply_fusion
  191.4 2.5 %fusion.4 = f32[1,128,2,128]{1,3,2,0:T(8,128)} fusion(f32[1,128,2,128]{1,3,2,0:T(8,128)S(1)} %bitcast.256, f32[2,16,64,128]{3,2,1,0:T(8,128)S(1)} %copy-done.10, f32[128,2,16,64]{0,3,2,1:T(8,128)S(1)} %bitcast.237, f32[128,2,16]{0,2,1:T(8,128)S(1)} %exponential_bitcast_fusion.1), kind=kOutput, calls=%fused_computation.23 | convolution fusion | flops 402948096 | bytes 2375680 | tf_op jit(solution)/shard_map/vmap(tgkp,gkpn->tgn)/dot_general | solution.py:136
  193.9 1.8 copy.165
  200.1 2.5 %collective-permute-start.7 = (f32[3,2560]{1,0:T(4,128)}, f32[3,2560]{1,0:T(4,128)}, u32[]{:S(2)}, u32[]{:S(2)}) collective-permute-start(f32[3,2560]{1,0:T(4,128)} %get-tuple-element.100), channel_id=1, source_target_pairs={{4,12},{5,13},{6,14},{7,15},{20,28},{21,29},{22,30},{23,31}} | collective-permute-start | bytes 92168 | tf_op jit(solution)/shard_map/ppermute | solution.py:373
  202.6 1.3 collective-permute-start.8
  203.9 1.4 pad_add_fusion.1
  208.1 2.1 split.67
  210.2 1.6 split.69
  211.9 1.5 split.68
  (318 shorter events, 45.0 us)
Async XLA Ops:
  0.6 18.7 %copy-start.43 = (bf16[128,2048]{1,0:T(8,128)(2,1)S(1)}, bf16[128,2048]{1,0:T(8,128)(2,1)}, u32[]{:S(2)}) copy-start(bf16[128,2048]{1,0:T(8,128)(2,1)} %param.21) | copy-start | bytes 1572868
  4.2 17.7 %collective-permute-start = (f32[7712]{0:T(1024)S(1)}, f32[7712]{0:T(1024)S(1)}, u32[]{:S(2)}, u32[]{:S(2)}) collective-permute-start(f32[7712]{0:T(1024)S(1)} %pad_maximum_fusion.9), channel_id=1, source_target_pairs={{0,4},{4,8},{8,12},{12,0},{1,5},{5,9},{9,13},{13,1},{2,6},{6,10},{... | collective-permute-start | bytes 92552 | tf_op jit(solution)/shard_map/ppermute | solution.py:214
  6.9 15.1 %collective-permute-start.1 = (f32[7712]{0:T(1024)S(1)}, f32[7712]{0:T(1024)S(1)}, u32[]{:S(2)}, u32[]{:S(2)}) collective-permute-start(f32[7712]{0:T(1024)S(1)} %pad_maximum_fusion.9), channel_id=1, source_target_pairs={{0,8},{4,12},{8,0},{12,4},{1,9},{5,13},{9,1},{13,5},{2,10},{6,14},... | collective-permute-start | bytes 92552 | tf_op jit(solution)/shard_map/ppermute | solution.py:214
  6.9 15.1 %collective-permute-start.2 = (f32[7712]{0:T(1024)S(1)}, f32[7712]{0:T(1024)S(1)}, u32[]{:S(2)}, u32[]{:S(2)}) collective-permute-start(f32[7712]{0:T(1024)S(1)} %pad_maximum_fusion.9), channel_id=1, source_target_pairs={{0,12},{4,0},{8,4},{12,8},{1,13},{5,1},{9,5},{13,9},{2,14},{6,2},{... | collective-permute-start | bytes 92552 | tf_op jit(solution)/shard_map/ppermute | solution.py:214
  9.5 5.3 %copy-start.95 = (f32[2,16]{1,0:T(2,128)}, f32[2,16]{1,0:T(2,128)S(1)}, u32[]{:S(2)}) copy-start(f32[2,16]{1,0:T(2,128)S(1)} %mul.837) | copy-start | bytes 388
  11.1 13.8 %copy-start.87 = (f32[1,256]{1,0:T(1,128)}, f32[1,256]{1,0:T(1,128)S(1)}, u32[]{:S(2)}) copy-start(f32[1,256]{1,0:T(1,128)S(1)} %get-tuple-element.121) | copy-start | bytes 3076
  11.1 13.8 %copy-start.89 = (f32[1,256]{1,0:T(1,128)}, f32[1,256]{1,0:T(1,128)S(1)}, u32[]{:S(2)}) copy-start(f32[1,256]{1,0:T(1,128)S(1)} %get-tuple-element.122) | copy-start | bytes 3076
  11.1 13.8 %copy-start.91 = (f32[1,256]{1,0:T(1,128)}, f32[1,256]{1,0:T(1,128)S(1)}, u32[]{:S(2)}) copy-start(f32[1,256]{1,0:T(1,128)S(1)} %get-tuple-element.124) | copy-start | bytes 3076
  11.1 13.8 %copy-start.93 = (f32[1,256]{1,0:T(1,128)}, f32[1,256]{1,0:T(1,128)S(1)}, u32[]{:S(2)}) copy-start(f32[1,256]{1,0:T(1,128)S(1)} %get-tuple-element.123) | copy-start | bytes 3076
  11.1 9.4 %copy-start.71 = (bf16[1,128,256]{2,1,0:T(8,128)(2,1)S(1)}, bf16[1,128,256]{2,1,0:T(8,128)(2,1)}, u32[]{:S(2)}) copy-start(bf16[1,128,256]{2,1,0:T(8,128)(2,1)} %param.28) | copy-start | bytes 196612
  12.0 12.9 %copy-start.79 = (f32[1,256]{1,0:T(1,128)}, f32[1,256]{1,0:T(1,128)S(1)}, u32[]{:S(2)}) copy-start(f32[1,256]{1,0:T(1,128)S(1)} %get-tuple-element.117) | copy-start | bytes 3076
  12.0 13.0 %copy-start.81 = (f32[1,256]{1,0:T(1,128)}, f32[1,256]{1,0:T(1,128)S(1)}, u32[]{:S(2)}) copy-start(f32[1,256]{1,0:T(1,128)S(1)} %get-tuple-element.118) | copy-start | bytes 3076
  12.0 13.0 %copy-start.83 = (f32[1,256]{1,0:T(1,128)}, f32[1,256]{1,0:T(1,128)S(1)}, u32[]{:S(2)}) copy-start(f32[1,256]{1,0:T(1,128)S(1)} %get-tuple-element.120) | copy-start | bytes 3076
  12.0 13.0 %copy-start.85 = (f32[1,256]{1,0:T(1,128)}, f32[1,256]{1,0:T(1,128)S(1)}, u32[]{:S(2)}) copy-start(f32[1,256]{1,0:T(1,128)S(1)} %get-tuple-element.119) | copy-start | bytes 3076
  17.5 3.0 %copy-start.72 = (bf16[1,128,256]{2,1,0:T(8,128)(2,1)S(1)}, bf16[1,128,256]{2,1,0:T(8,128)(2,1)}, u32[]{:S(2)}) copy-start(bf16[1,128,256]{2,1,0:T(8,128)(2,1)} %param.27) | copy-start | bytes 196612
  18.4 2.2 copy-start.44
  21.9 21.1 %copy-start.5 = (f32[128,2048]{0,1:T(8,128)}, f32[128,2048]{0,1:T(8,128)S(1)}, u32[]{:S(2)}) copy-start(f32[128,2048]{0,1:T(8,128)S(1)} %copy.121) | copy-start | bytes 3145732
  22.8 3.7 %copy-start.21 = (f32[128,2048]{1,0:T(8,128)S(1)}, f32[128,2048]{1,0:T(8,128)}, u32[]{:S(2)}) copy-start(f32[128,2048]{1,0:T(8,128)} %convert_element_type.162) | copy-start | bytes 3145732
  29.4 10.7 %copy-start.1 = (f32[128,2048]{0,1:T(8,128)}, f32[128,2048]{0,1:T(8,128)S(1)}, u32[]{:S(2)}) copy-start(f32[128,2048]{0,1:T(8,128)S(1)} %copy.119) | copy-start | bytes 3145732
  39.0 2.9 %copy-start.3 = (f32[1,128,2048]{1,2,0:T(8,128)}, f32[1,128,2048]{1,2,0:T(8,128)S(1)}, u32[]{:S(2)}) copy-start(f32[1,128,2048]{1,2,0:T(8,128)S(1)} %copy.123) | copy-start | bytes 3145732
  46.0 7.0 %collective-permute-start.3 = (f32[3,2,16,64,128]{4,3,2,1,0:T(8,128)}, f32[3,2,16,64,128]{4,3,2,1,0:T(8,128)}, u32[]{:S(2)}, u32[]{:S(2)}) collective-permute-start(f32[3,2,16,64,128]{4,3,2,1,0:T(8,128)} %pad_maximum_fusion), channel_id=1, source_target_pairs={{0,4},{4,0},{8,12},{12,8},{1,5},{5,1},{9,13},{13,9},{2,6},{6,2},{1... | collective-permute-start | bytes 9437192 | tf_op jit(solution)/shard_map/ppermute | solution.py:298
  49.4 7.1 %copy-start.99 = (f32[2,16]{1,0:T(2,128)}, f32[2,16]{1,0:T(2,128)S(1)}, u32[]{:S(2)}) copy-start(f32[2,16]{1,0:T(2,128)S(1)} %get-tuple-element.115) | copy-start | bytes 388
  49.4 7.1 %copy-start.100 = (f32[2,16]{1,0:T(2,128)}, f32[2,16]{1,0:T(2,128)S(1)}, u32[]{:S(2)}) copy-start(f32[2,16]{1,0:T(2,128)S(1)} %get-tuple-element.116) | copy-start | bytes 388
  49.4 7.1 %copy-start.103 = (f32[2,16]{1,0:T(2,128)S(1)}, f32[2,16]{1,0:T(2,128)}, u32[]{:S(2)}) copy-start(f32[2,16]{1,0:T(2,128)} %exp.142) | copy-start | bytes 388
  58.6 24.5 %collective-permute-start.4 = (f32[2,16,64,128]{3,2,1,0:T(8,128)S(1)}, f32[2,16,64,128]{3,2,1,0:T(8,128)}, u32[]{:S(2)}, u32[]{:S(2)}) collective-permute-start(f32[2,16,64,128]{3,2,1,0:T(8,128)S(1)} %get-tuple-element.65), channel_id=1, source_target_pairs={{0,8},{4,12},{8,0},{12,4},{1,9},{5,13},{9,1},{13,5},{2,10},{6,14},... | collective-permute-start | bytes 3145736 | tf_op jit(solution)/shard_map/ppermute | solution.py:318
  83.0 45.4 %collective-permute-start.5 = (f32[2,16,64,128]{3,2,1,0:T(8,128)}, f32[2,16,64,128]{3,2,1,0:T(8,128)}, u32[]{:S(2)}, u32[]{:S(2)}) collective-permute-start(f32[2,16,64,128]{3,2,1,0:T(8,128)} %collective-permute-done.4), channel_id=1, source_target_pairs={{0,4},{4,0},{8,12},{12,8},{1,5},{5,1},{9,13},{13,9},{2,6},{6,2},{1... | collective-permute-start | bytes 3145736 | tf_op jit(solution)/shard_map/ppermute | solution.py:319
  128.5 6.5 %copy-start.6 = (f32[128,2048]{0,1:T(8,128)S(1)}, f32[128,2048]{0,1:T(8,128)}, u32[]{:S(2)}) copy-start(f32[128,2048]{0,1:T(8,128)} %copy-done.5) | copy-start | bytes 3145732
  128.5 6.5 %copy-start.61 = (f32[128,2,16]{0,2,1:T(8,128)S(1)}, f32[128,2,16]{0,2,1:T(8,128)}, u32[]{:S(2)}) copy-start(f32[128,2,16]{0,2,1:T(8,128)} %get-tuple-element.108) | copy-start | bytes 49156
  155.8 2.6 %copy-start.22 = (f32[128,2048]{1,0:T(8,128)S(1)}, f32[128,2048]{1,0:T(8,128)}, u32[]{:S(2)}) copy-start(f32[128,2048]{1,0:T(8,128)} %get-tuple-element.72) | copy-start | bytes 3145732
  155.8 2.6 %copy-start.59 = (f32[1,2048]{1,0:T(1,128)S(1)}, f32[1,2048]{1,0:T(1,128)}, u32[]{:S(2)}) copy-start(f32[1,2048]{1,0:T(1,128)} %get-tuple-element.113) | copy-start | bytes 24580
  158.4 2.7 %copy-start.53 = (f32[1,2048]{1,0:T(1,128)S(1)}, f32[1,2048]{1,0:T(1,128)}, u32[]{:S(2)}) copy-start(f32[1,2048]{1,0:T(1,128)} %get-tuple-element.111) | copy-start | bytes 24580
  158.4 2.7 %copy-start.55 = (f32[1,2048]{1,0:T(1,128)S(1)}, f32[1,2048]{1,0:T(1,128)}, u32[]{:S(2)}) copy-start(f32[1,2048]{1,0:T(1,128)} %get-tuple-element.112) | copy-start | bytes 24580
  158.4 2.7 %copy-start.57 = (f32[1,2048]{1,0:T(1,128)S(1)}, f32[1,2048]{1,0:T(1,128)}, u32[]{:S(2)}) copy-start(f32[1,2048]{1,0:T(1,128)} %get-tuple-element.114) | copy-start | bytes 24580
  163.0 4.5 %copy-start.12 = (f32[2,16,64,128]{3,2,1,0:T(8,128)S(1)}, f32[2,16,64,128]{3,2,1,0:T(8,128)}, u32[]{:S(2)}) copy-start(f32[2,16,64,128]{3,2,1,0:T(8,128)} %copy-done.11) | copy-start | bytes 3145732
  164.8 2.7 %copy-start.7 = (f32[128,2048]{0,1:T(8,128)S(1)}, f32[128,2048]{0,1:T(8,128)}, u32[]{:S(2)}) copy-start(f32[128,2048]{0,1:T(8,128)} %copy-done.5) | copy-start | bytes 3145732
  164.8 2.6 %copy-start.45 = (f32[128,256]{0,1:T(8,128)S(1)}, f32[128,256]{0,1:T(8,128)}, u32[]{:S(2)}) copy-start(f32[128,256]{0,1:T(8,128)} %copy.168) | copy-start | bytes 393220
  164.8 2.6 %copy-start.62 = (f32[128,2,16]{0,2,1:T(8,128)S(1)}, f32[128,2,16]{0,2,1:T(8,128)}, u32[]{:S(2)}) copy-start(f32[128,2,16]{0,2,1:T(8,128)} %get-tuple-element.108) | copy-start | bytes 49156
  167.5 2.8 %copy-start.80 = (f32[1,256]{1,0:T(1,128)S(1)}, f32[1,256]{1,0:T(1,128)}, u32[]{:S(2)}) copy-start(f32[1,256]{1,0:T(1,128)} %copy-done.79) | copy-start | bytes 3076
  167.5 2.7 %copy-start.82 = (f32[1,256]{1,0:T(1,128)S(1)}, f32[1,256]{1,0:T(1,128)}, u32[]{:S(2)}) copy-start(f32[1,256]{1,0:T(1,128)} %copy-done.81) | copy-start | bytes 3076
  167.5 2.7 %copy-start.84 = (f32[1,256]{1,0:T(1,128)S(1)}, f32[1,256]{1,0:T(1,128)}, u32[]{:S(2)}) copy-start(f32[1,256]{1,0:T(1,128)} %copy-done.83) | copy-start | bytes 3076
  171.8 14.4 %copy-start.23 = (f32[1,128,2048]{2,1,0:T(8,128)S(1)}, f32[1,128,2048]{2,1,0:T(8,128)}, u32[]{:S(2)}) copy-start(f32[1,128,2048]{2,1,0:T(8,128)} %get-tuple-element.58) | copy-start | bytes 3145732
  171.8 14.4 %copy-start.60 = (f32[1,2048]{1,0:T(1,128)S(1)}, f32[1,2048]{1,0:T(1,128)}, u32[]{:S(2)}) copy-start(f32[1,2048]{1,0:T(1,128)} %get-tuple-element.113) | copy-start | bytes 24580
  188.3 2.2 %copy-start.88 = (f32[1,256]{1,0:T(1,128)S(1)}, f32[1,256]{1,0:T(1,128)}, u32[]{:S(2)}) copy-start(f32[1,256]{1,0:T(1,128)} %copy-done.87) | copy-start | bytes 3076
  188.3 2.2 %copy-start.90 = (f32[1,256]{1,0:T(1,128)S(1)}, f32[1,256]{1,0:T(1,128)}, u32[]{:S(2)}) copy-start(f32[1,256]{1,0:T(1,128)} %copy-done.89) | copy-start | bytes 3076
  188.3 2.2 %copy-start.92 = (f32[1,256]{1,0:T(1,128)S(1)}, f32[1,256]{1,0:T(1,128)}, u32[]{:S(2)}) copy-start(f32[1,256]{1,0:T(1,128)} %copy-done.91) | copy-start | bytes 3076
  188.3 3.1 %copy-start.10 = (f32[2,16,64,128]{3,2,1,0:T(8,128)S(1)}, f32[2,16,64,128]{3,2,1,0:T(8,128)}, u32[]{:S(2)}) copy-start(f32[2,16,64,128]{3,2,1,0:T(8,128)} %get-tuple-element.75) | copy-start | bytes 3145732
  191.4 4.2 %copy-start.28 = (f32[1,128,256]{2,1,0:T(8,128)S(1)}, f32[1,128,256]{2,1,0:T(8,128)}, u32[]{:S(2)}) copy-start(f32[1,128,256]{2,1,0:T(8,128)} %copy-done.27) | copy-start | bytes 393220
  193.9 4.2 %copy-start.16 = (f32[128,2048]{1,0:T(8,128)S(1)}, f32[128,2048]{1,0:T(8,128)}, u32[]{:S(2)}) copy-start(f32[128,2048]{1,0:T(8,128)} %get-tuple-element.63) | copy-start | bytes 3145732
  198.1 5.7 %copy-start.18 = (f32[128,2048]{1,0:T(8,128)S(1)}, f32[128,2048]{1,0:T(8,128)}, u32[]{:S(2)}) copy-start(f32[128,2048]{1,0:T(8,128)} %get-tuple-element.80) | copy-start | bytes 3145732
  198.1 5.7 %copy-start.19 = (f32[128,2048]{1,0:T(8,128)S(1)}, f32[128,2048]{1,0:T(8,128)}, u32[]{:S(2)}) copy-start(f32[128,2048]{1,0:T(8,128)} %get-tuple-element.81) | copy-start | bytes 3145732
  199.2 4.6 %copy-start.17 = (f32[128,2048]{1,0:T(8,128)S(1)}, f32[128,2048]{1,0:T(8,128)}, u32[]{:S(2)}) copy-start(f32[128,2048]{1,0:T(8,128)} %get-tuple-element.79) | copy-start | bytes 3145732
  200.1 13.3 %collective-permute-start.7 = (f32[3,2560]{1,0:T(4,128)}, f32[3,2560]{1,0:T(4,128)}, u32[]{:S(2)}, u32[]{:S(2)}) collective-permute-start(f32[3,2560]{1,0:T(4,128)} %get-tuple-element.100), channel_id=1, source_target_pairs={{4,12},{5,13},{6,14},{7,15},{20,28},{21,29},{22,30},{23,31}} | collective-permute-start | bytes 92168 | tf_op jit(solution)/shard_map/ppermute | solution.py:373
  202.6 10.8 %collective-permute-start.8 = (f32[3,2560]{1,0:T(4,128)}, f32[3,2560]{1,0:T(4,128)}, u32[]{:S(2)}, u32[]{:S(2)}) collective-permute-start(f32[3,2560]{1,0:T(4,128)} %get-tuple-element.100), channel_id=1, source_target_pairs={{8,12},{9,13},{10,14},{11,15},{24,28},{25,29},{26,30},{27,31}} | collective-permute-start | bytes 92168 | tf_op jit(solution)/shard_map/ppermute | solution.py:373
  206.3 7.1 %copy-start.52 = (f32[3,2048]{1,0:T(4,128)S(1)}, f32[3,2048]{1,0:T(4,128)}, u32[]{:S(2)}) copy-start(f32[3,2048]{1,0:T(4,128)} %slice_bitcast_fusion.4) | copy-start | bytes 73732
  206.4 7.1 %copy-start.76 = (f32[3,256]{1,0:T(4,128)S(1)}, f32[3,256]{1,0:T(4,128)}, u32[]{:S(2)}) copy-start(f32[3,256]{1,0:T(4,128)} %slice_bitcast_fusion.7) | copy-start | bytes 9220
  206.4 7.1 %copy-start.78 = (f32[3,256]{1,0:T(4,128)S(1)}, f32[3,256]{1,0:T(4,128)}, u32[]{:S(2)}) copy-start(f32[3,256]{1,0:T(4,128)} %copy-done.77) | copy-start | bytes 9220
  206.4 7.9 %copy-start.35 = (f32[128,256]{1,0:T(8,128)S(1)}, f32[128,256]{1,0:T(8,128)}, u32[]{:S(2)}) copy-start(f32[128,256]{1,0:T(8,128)} %get-tuple-element.61) | copy-start | bytes 393220
  206.4 7.9 %copy-start.37 = (f32[128,256]{1,0:T(8,128)S(1)}, f32[128,256]{1,0:T(8,128)}, u32[]{:S(2)}) copy-start(f32[128,256]{1,0:T(8,128)} %get-tuple-element.93) | copy-start | bytes 393220
  206.4 7.9 %copy-start.39 = (f32[128,256]{1,0:T(8,128)S(1)}, f32[128,256]{1,0:T(8,128)}, u32[]{:S(2)}) copy-start(f32[128,256]{1,0:T(8,128)} %get-tuple-element.94) | copy-start | bytes 393220
  206.4 7.9 %copy-start.41 = (f32[128,256]{1,0:T(8,128)S(1)}, f32[128,256]{1,0:T(8,128)}, u32[]{:S(2)}) copy-start(f32[128,256]{1,0:T(8,128)} %get-tuple-element.95) | copy-start | bytes 393220
  207.2 6.3 %collective-permute-start.6 = (f32[3,2560]{1,0:T(4,128)S(1)}, f32[3,2560]{1,0:T(4,128)S(1)}, u32[]{:S(2)}, u32[]{:S(2)}) collective-permute-start(f32[3,2560]{1,0:T(4,128)S(1)} %copy-done.74), channel_id=1, source_target_pairs={{0,12},{4,0},{8,4},{12,8},{1,13},{5,1},{9,5},{13,9},{2,14},{6,2},{... | collective-permute-start | bytes 92168 | tf_op jit(solution)/shard_map/ppermute | solution.py:366
  207.3 7.8 %copy-start.31 = (f32[128,256]{1,0:T(8,128)S(1)}, f32[128,256]{1,0:T(8,128)}, u32[]{:S(2)}) copy-start(f32[128,256]{1,0:T(8,128)} %get-tuple-element.91) | copy-start | bytes 393220
  207.3 7.8 %copy-start.33 = (f32[128,256]{1,0:T(8,128)S(1)}, f32[128,256]{1,0:T(8,128)}, u32[]{:S(2)}) copy-start(f32[128,256]{1,0:T(8,128)} %get-tuple-element.92) | copy-start | bytes 393220
  210.2 5.5 %copy-start.20 = (f32[131,2048]{1,0:T(8,128)S(1)}, f32[131,2048]{1,0:T(8,128)}, u32[]{:S(2)}) copy-start(f32[131,2048]{1,0:T(8,128)} %pad_add_fusion.1) | copy-start | bytes 3219460
  (49 other events, 75.3 us)

commit v6 on v3

--- a/solution.py
+++ b/solution.py
@@ -302,16 +302,19 @@
     num_chips = num_ways // 2
     own_triple = jnp.stack([own_state, own_adjoint, jnp.sum(adjoints, axis=0)])
     partner_triple = lax.ppermute(own_triple, "suf", [(j, j ^ 1) for j in range(num_ways)])
-    even = jnp.where(core == 0, own_triple, partner_triple)
-    odd = jnp.where(core == 0, partner_triple, own_triple)
+    on_even = core == 0
     block_decay = jnp.exp(every_log).reshape(num_ways, num_groups, per_group, 1, 1)
     decay_even = lax.dynamic_index_in_dim(block_decay, 2 * chip, 0, False)
     decay_odd = lax.dynamic_index_in_dim(block_decay, 2 * chip + 1, 0, False)
     chip_log = every_log.reshape(num_chips, 2, num_heads).sum(axis=1)
     later_log = jnp.sum(jnp.where((jnp.arange(num_chips) >= chip)[:, None], chip_log, 0.0), axis=0)
-    chip_state = decay_odd * even[0] + odd[0]
-    chip_adjoint = even[1] + decay_even * odd[1]
-    chip_suffix = even[2] + odd[2]
+    chip_state = decay_odd * jnp.where(on_even, own_state, partner_triple[0]) + jnp.where(
+        on_even, partner_triple[0], own_state
+    )
+    chip_adjoint = jnp.where(on_even, own_adjoint, partner_triple[1]) + decay_even * jnp.where(
+        on_even, partner_triple[1], own_adjoint
+    )
+    chip_suffix = own_triple[2] + partner_triple[2]
     chip_later = chip_adjoint + jnp.exp(later_log).reshape(num_groups, per_group, 1, 1) * chip_suffix
     got_state = [chip_state]
     got_other = [chip_suffix]
@@ -352,8 +355,8 @@
     for c in reversed(range(num_chips)):
         chip_end_grad = jnp.where(chip == c, running, chip_end_grad)
         running = chip_others[c] + chip_decay[c] * running
-    start_state = jnp.where(core == 0, chip_start, decay_even * chip_start + even[0])
-    end_grad = jnp.where(core == 0, odd[1] + decay_odd * chip_end_grad, chip_end_grad)
+    start_state = jnp.where(on_even, chip_start, decay_even * chip_start + partner_triple[0])
+    end_grad = jnp.where(on_even, partner_triple[1] + decay_odd * chip_end_grad, chip_end_grad)
     conv_grads, suffix_ddt = jax.vmap(
         suffix_back, in_axes=(None, 0, 0, 0, 0, 1, 0, 0), out_axes=(0, 1)
     )(prompt_end_late, suffix_inner, *suffix_items)

time: 208 us -> 225 us (1.082)
  local copies, waits for them, and re-layouts: 52.3 us -> 62.5 us
  other arithmetic: 65 us -> 72.9 us
  waiting for transfers between devices: 28.1 us -> 24.8 us
    ppermute x1, waiting for transfers between devices: 3.59 us -> 0.01 us  [shards(): lax.ppermute(own_triple, 'suf', [(j, j ^ 1) for j in range(num_ways)])]
    select_n x1 -> x0, other arithmetic: 3.5 us -> none  [shards(): odd = jnp.where(core == 0, partner_triple, own_triple)]
    rev x4, local copies, waits for them, and re-layouts: 0.26 us -> 3.32 us  [block_outer(): d_log = jnp.flip(jnp.cumsum(jnp.flip(d_cum, -1), axis=-1), -1)]
    select_n x1, other arithmetic: 1.9 us -> 4.38 us  [shards(): jnp.where(core == 0, chip_state, jnp.where(wraps, chip_later, chip_suffix))]
    unnamed x185 -> x151, local copies, waits for them, and re-layouts: 6.58 us -> 6.46 us
  transfers between devices with their start and end apart: 10 -> 10, of which waited for: 2 -> 1; matrix products, arithmetic and copies ran while one was open for 34% -> 34% of each run, Pallas kernels for 7% -> 6%
where the time goes in v6:
time: 225 us; the launch traced here: 223 us
  other arithmetic  72.9 us (32%)
  local copies, waits for them, and re-layouts  62.5 us (28%)
  Pallas kernels  28.1 us (12%)
  waiting for transfers between devices  24.8 us (11%)
  matrix products  18.4 us (8%)
  starting transfers between devices  12.7 us (6%)
  between operations  3.14 us (1%)
    pallas_call x2, Pallas kernels, block_inner(): pl.pallas_call(functools.partial(_grad_kernel, steps_per_group), grid=(nh...  28.1 us
    ppermute x1, waiting for transfers between devices, shards(): incoming = lax.ppermute(outgoing, 'suf', route)  24.8 us
    reshape x2, other arithmetic, block_inner(): pl.pallas_call(functools.partial(_grad_kernel, steps_per_group), grid=(nh...  7.19 us
    mul x12, other arithmetic, causal_conv(): padded[tap_index:tap_index + num_tokens]  6.72 us
    unnamed x151, local copies, waits for them, and re-layouts  6.46 us
    reduce_sum x1, other arithmetic, block_outer(): jnp.sum(lam * S0, axis=(-2, -1))  5.95 us
    dot_general x2, matrix products, block_outer(): dc = dc + jnp.einsum('tgkp,gkpn->tgn', g_grow, S0, precision=EXACT_DOT)  5.54 us
    split x3, local copies, waits for them, and re-layouts, causal_conv(): padded = jnp.concatenate([context, values], axis=0)  5.33 us
  transfers between devices with their start and end apart: 10, of which 1 were waited for; matrix products, arithmetic and copies ran while one was open for 34% of the time, Pallas kernels for 6%

profile of v6, /device:TPU:1, one launch (start us, length us, event | category | flops | bytes accessed | tf_op | source)
XLA Modules:
  0.0 222.7 jit_solution(4609677416989951201)
XLA Ops:
  4.2 2.7 %collective-permute-start = (f32[7712]{0:T(1024)S(1)}, f32[7712]{0:T(1024)S(1)}, u32[]{:S(2)}, u32[]{:S(2)}) collective-permute-start(f32[7712]{0:T(1024)S(1)} %pad_maximum_fusion.10), channel_id=1, source_target_pairs={{0,4},{4,8},{8,12},{12,0},{1,5},{5,9},{9,13},{13,1},{2,6},{6,10},{... | collective-permute-start | bytes 92552 | tf_op jit(solution)/shard_map/ppermute | solution.py:220
  7.3 1.4 exponential_multiply_fusion.1
  12.0 1.5 slice_convert_fusion.6
  26.4 2.5 %fusion.34 = (f32[128,2048]{1,0:T(8,128)S(1)}, f32[128,2048]{1,0:T(8,128)}) fusion(f32[128,2048]{1,0:T(8,128)S(1)} %copy-done.8, f32[2048]{0:T(1024)} %bitcast.259, f32[2048]{0:T(1024)} %bitcast.255, f32[3,2048]{1,0:T(4,128)} %slice.278, f32[2048]{0:T(1024)} %bitcast.251, f32[2048]{0:T(1024)} %bitcast.247), kind=kLoop, calls=%fused_computation.76 | loop fusion | flops 3670016 | bytes 3203072 | tf_op jit(solution)/shard_map/jvp(jit(silu))/mul | solution.py:33
  29.3 1.6 multiply_bitcast_fusion.1
  31.7 5.6 %multiply_bitcast_fusion = (f32[128,2048]{1,0:T(8,128)}, f32[1,128,2048]{2,1,0:T(8,128)}, f32[1,128,2048]{2,1,0:T(8,128)}, f32[128,2048]{1,0:T(8,128)}) fusion(f32[1,128,2048]{2,1,0:T(8,128)} %convert_element_type.169, f32[2048]{0:T(1024)} %bitcast.260, f32[2048]{0:T(1024)} %bitcast.256, f32[1,3,2048]{2,1,0:T(4,128)} %slice_bitcast_fusion.4, ...), kind=kLoop, calls=%fused_computation.61 | loop fusion | flops 4194304 | bytes 5825024 | tf_op jit(solution)/shard_map/vmap()/squeeze;vmap()/reshape;vmap()/reshape | solution.py:102
  37.2 1.5 copy.123
  39.8 1.8 fusion.32
  43.7 2.0 pad_maximum_fusion
  45.7 1.4 collective-permute-start.3
  48.8 1.4 reshape.513
  50.2 1.3 reduce_sum.91
  53.2 1.3 exp.142
  55.2 4.4 %select_select_fusion = (f32[2,16,64,128]{3,2,1,0:T(8,128)S(1)}, f32[2,16,64,128]{3,2,1,0:T(8,128)}) fusion(f32[2,16,64,128]{3,2,1,0:T(8,128)} %copy-done.6, f32[3,2,16,64,128]{4,3,2,1,0:T(8,128)} %collective-permute-done.3, f32[2,16]{1,0:T(2,128)} %exp.142, f32[2,16]{1,0:T(2,128)S(1)} %get-tuple-element.112, pred[]{:T(512)S(6)} %ge.27, pred[]{:T(512)S(6)} %eq.55, ...), kind=kLoop, calls=%fused_computation.68 | loop fusion | flops 3407872 | bytes 8388994 | tf_op jit(solution)/shard_map/jit(_where)/select_n | solution.py:323
  59.6 24.8 %collective-permute-done.4 = f32[2,16,64,128]{3,2,1,0:T(8,128)} collective-permute-done((f32[2,16,64,128]{3,2,1,0:T(8,128)S(1)}, f32[2,16,64,128]{3,2,1,0:T(8,128)}, u32[]{:S(2)}, u32[]{:S(2)}) %collective-permute-start.4) | collective-permute-done | bytes 1048608 | tf_op jit(solution)/shard_map/ppermute | solution.py:327
  85.3 2.1 convert_element_type.163.g_ref
  87.4 1.5 copy.111
  89.5 1.6 negate_multiply_fusion
  91.1 1.6 copy.112
  92.7 1.9 reduce_window_sum.47
  94.6 1.4 slice.293
  96.0 1.4 copy.177
  97.3 1.4 exponential_bitcast_fusion
  98.7 1.5 copy.116
  100.2 1.3 broadcast_in_dim.54
  101.5 1.4 broadcast_in_dim.59.skip_ref
  102.9 1.4 multiply_reduce_fusion.2
  104.3 1.3 mul.870
  105.6 1.3 mul.892
  106.9 14.1 %shard_map.242 = (f32[128,2048]{1,0:T(8,128)}, f32[32,128]{1,0:T(8,128)}, f32[32,128]{1,0:T(8,128)}, f32[128,256]{1,0:T(8,128)}, f32[128,256]{1,0:T(8,128)}) custom-call(f32[128,2048]{1,0:T(8,128)} %copy-done.1, f32[128,2048]{1,0:T(8,128)} %convert_element_type.163.g_ref, f32[128,256]{1,0:T(8,128)} %copy-done.11, f32[128,256]{1,0:T(8,128)} %get-tuple-element.67.c_ref, ...), custom_call_target="tpu_custom_call" | custom-call | tf_op jit(solution)/shard_map/pallas_call | solution.py:102
  120.9 1.5 copy.140
  122.4 1.5 copy.137
  123.9 2.6 %copy.113 = f32[128,2048]{0,1:T(8,128)} copy(f32[128,2048]{1,0:T(8,128)} %get-tuple-element.30) | data formatting | bytes 2097152 | tf_op jit(solution)/shard_map/pallas_call | solution.py:102
  126.4 1.7 copy.164
  128.1 1.7 copy.166
  129.8 6.0 %multiply_reduce_fusion = (f32[2,16]{1,0:T(2,128)}, f32[2,16,64,128]{3,2,1,0:T(8,128)S(1)}, f32[2,16,64,128]{3,2,1,0:T(8,128)}, f32[2,16,64,128]{3,2,1,0:T(8,128)}) fusion(f32[3,2,16,64,128]{4,3,2,1,0:T(8,128)} %collective-permute-done.3, f32[2,16]{1,0:T(2,128)} %copy-done.73, f32[2,16,64,128]{3,2,1,0:T(8,128)} %get-tuple-element.66, ...), kind=kLoop, calls=%fused_computation.58 | loop fusion | flops 6553568 | bytes 10486407 | tf_op jit(solution)/shard_map/reduce_sum | solution.py:153
  136.7 1.7 fusion.3
  138.4 1.5 copy.139
  139.9 3.2 %multiply_reduce_fusion.1 = (f32[128,2,16]{0,2,1:T(8,128)S(1)}, f32[128,2,16,64]{0,3,2,1:T(8,128)}) fusion(f32[128,2048]{0,1:T(8,128)S(1)} %copy.119, f32[2,16,64,128]{3,2,1,0:T(8,128)} %get-tuple-element.46, f32[128,2,128,1]{2,1,0,3:T(2,128)S(1)} %bitcast.235), kind=kOutput, calls=%fused_computation.59 | convolution fusion | flops 403173376 | bytes 3293184 | tf_op jit(solution)/shard_map/gkpn,sgn->sgkp/dot_general | solution.py:147
  144.3 1.7 fusion.89
  146.1 1.3 fusion.109
  147.3 1.6 rev.14
  148.9 1.6 copy.141
  150.5 1.9 reduce_window_sum.49
  152.4 1.5 copy.142
  153.8 1.8 fusion.91
  156.6 1.5 fusion.107
  158.1 14.1 %vmap__.1 = (f32[128,2048]{1,0:T(8,128)}, f32[32,128]{1,0:T(8,128)}, f32[32,128]{1,0:T(8,128)}, f32[128,256]{1,0:T(8,128)}, f32[128,256]{1,0:T(8,128)}) custom-call(f32[128,2048]{1,0:T(8,128)} %get-tuple-element.57.x_ref, f32[128,2048]{1,0:T(8,128)} %get-tuple-element.132.g_ref, f32[128,256]{1,0:T(8,128)} %get-tuple-element.55.b_ref, ...), custom_call_target="tpu_custom_call" | custom-call | tf_op jit(solution)/shard_map/vmap()/pallas_call | solution.py:102
  172.2 2.0 broadcast_multiply_fusion
  179.0 3.7 %fusion.4 = f32[1,128,2,128]{1,3,2,0:T(8,128)} fusion(f32[1,128,2,128]{1,3,2,0:T(8,128)} %bitcast.243, f32[2,16,64,128]{3,2,1,0:T(8,128)} %get-tuple-element.73, f32[128,2,16,64]{0,3,2,1:T(8,128)S(1)} %bitcast.224, f32[128,2,16]{0,2,1:T(8,128)S(1)} %exponential_bitcast_fusion.1), kind=kOutput, calls=%fused_computation.18 | convolution fusion | flops 402948096 | bytes 2375680 | tf_op jit(solution)/shard_map/vmap(tgkp,gkpn->tgn)/dot_general | solution.py:142
  182.7 1.7 copy.169
  187.4 1.3 collective-permute-start.7
  188.7 2.6 %collective-permute-start.8 = (f32[3,2560]{1,0:T(4,128)}, f32[3,2560]{1,0:T(4,128)}, u32[]{:S(2)}, u32[]{:S(2)}) collective-permute-start(f32[3,2560]{1,0:T(4,128)} %pad_maximum_fusion.9), channel_id=1, source_target_pairs={{4,12},{5,13},{6,14},{7,15},{20,28},{21,29},{22,30},{23,31}} | collective-permute-start | bytes 92168 | tf_op jit(solution)/shard_map/ppermute | solution.py:378
  191.2 1.3 collective-permute-start.9
  193.2 2.9 %multiply_add_fusion = f32[128,2,16,64]{0,3,2,1:T(8,128)} fusion(f32[128,2,16,64]{0,3,2,1:T(8,128)} %bitcast.229, f32[128,2,16,64]{0,3,2,1:T(8,128)} %get-tuple-element.126, f32[128,2,16]{0,2,1:T(8,128)S(1)} %copy.118), kind=kLoop, calls=%fused_computation.66 | loop fusion | flops 524288 | bytes 3162112 | tf_op jit(solution)/shard_map/add | solution.py:148
  196.1 2.5 %copy.126 = f32[128,2048]{1,0:T(8,128)} copy(f32[128,2048]{0,1:T(8,128)} %bitcast.230) | data formatting | bytes 2097152 | tf_op jit(solution)/shard_map/reshape | solution.py:367
  198.7 2.0 broadcast_multiply_fusion.4
  201.1 1.4 pad_add_fusion.1
  204.4 3.1 %fusion.5 = f32[128,2,128]{0,2,1:T(8,128)S(1)} fusion(f32[128,2,128]{0,2,1:T(8,128)S(1)} %bitcast.240, f32[2,16,64,128]{3,2,1,0:T(8,128)} %get-tuple-element.46, f32[2,16,128,64]{2,3,1,0:T(8,128)S(1)} %bitcast.219, f32[2,16,128]{2,1,0:T(8,128)S(1)} %copy-done.40), kind=kOutput, calls=%fused_computation.19 | convolution fusion | flops 402948096 | bytes 2375680 | tf_op jit(solution)/shard_map/gkpn,sgkp,gks->sgn/dot_general | solution.py:149
  208.8 1.8 fusion.6
  211.0 2.3 %collective-permute-start.6 = (f32[3,2560]{1,0:T(4,128)S(1)}, f32[3,2560]{1,0:T(4,128)S(1)}, u32[]{:S(2)}, u32[]{:S(2)}) collective-permute-start(f32[3,2560]{1,0:T(4,128)S(1)} %pad_maximum_fusion.8), channel_id=1, source_target_pairs={{4,0},{8,4},{12,8},{5,1},{9,5},{13,9},{6,2},{10,6},{14,10},{7,3},{... | collective-permute-start | bytes 92168 | tf_op jit(solution)/shard_map/ppermute | solution.py:22
  214.2 2.1 split.67
  216.3 1.6 split.69
  217.9 1.5 split.68
  (262 shorter events, 47.8 us)
Async XLA Ops:
  0.6 18.7 %copy-start.15 = (bf16[128,2048]{1,0:T(8,128)(2,1)S(1)}, bf16[128,2048]{1,0:T(8,128)(2,1)}, u32[]{:S(2)}) copy-start(bf16[128,2048]{1,0:T(8,128)(2,1)} %param.21) | copy-start | bytes 1572868
  4.2 17.6 %collective-permute-start = (f32[7712]{0:T(1024)S(1)}, f32[7712]{0:T(1024)S(1)}, u32[]{:S(2)}, u32[]{:S(2)}) collective-permute-start(f32[7712]{0:T(1024)S(1)} %pad_maximum_fusion.10), channel_id=1, source_target_pairs={{0,4},{4,8},{8,12},{12,0},{1,5},{5,9},{9,13},{13,1},{2,6},{6,10},{... | collective-permute-start | bytes 92552 | tf_op jit(solution)/shard_map/ppermute | solution.py:220
  6.9 15.0 %collective-permute-start.1 = (f32[7712]{0:T(1024)S(1)}, f32[7712]{0:T(1024)S(1)}, u32[]{:S(2)}, u32[]{:S(2)}) collective-permute-start(f32[7712]{0:T(1024)S(1)} %pad_maximum_fusion.10), channel_id=1, source_target_pairs={{0,8},{4,12},{8,0},{12,4},{1,9},{5,13},{9,1},{13,5},{2,10},{6,14},... | collective-permute-start | bytes 92552 | tf_op jit(solution)/shard_map/ppermute | solution.py:220
  6.9 15.1 %collective-permute-start.2 = (f32[7712]{0:T(1024)S(1)}, f32[7712]{0:T(1024)S(1)}, u32[]{:S(2)}, u32[]{:S(2)}) collective-permute-start(f32[7712]{0:T(1024)S(1)} %pad_maximum_fusion.10), channel_id=1, source_target_pairs={{0,12},{4,0},{8,4},{12,8},{1,13},{5,1},{9,5},{13,9},{2,14},{6,2},{... | collective-permute-start | bytes 92552 | tf_op jit(solution)/shard_map/ppermute | solution.py:220
  9.5 5.3 %copy-start.68 = (f32[2,16]{1,0:T(2,128)}, f32[2,16]{1,0:T(2,128)S(1)}, u32[]{:S(2)}) copy-start(f32[2,16]{1,0:T(2,128)S(1)} %mul.837) | copy-start | bytes 388
  11.1 13.8 %copy-start.56 = (f32[1,256]{1,0:T(1,128)}, f32[1,256]{1,0:T(1,128)S(1)}, u32[]{:S(2)}) copy-start(f32[1,256]{1,0:T(1,128)S(1)} %get-tuple-element.117) | copy-start | bytes 3076
  11.1 13.8 %copy-start.59 = (f32[1,256]{1,0:T(1,128)}, f32[1,256]{1,0:T(1,128)S(1)}, u32[]{:S(2)}) copy-start(f32[1,256]{1,0:T(1,128)S(1)} %get-tuple-element.118) | copy-start | bytes 3076
  11.1 13.8 %copy-start.62 = (f32[1,256]{1,0:T(1,128)}, f32[1,256]{1,0:T(1,128)S(1)}, u32[]{:S(2)}) copy-start(f32[1,256]{1,0:T(1,128)S(1)} %get-tuple-element.120) | copy-start | bytes 3076
  11.1 13.8 %copy-start.65 = (f32[1,256]{1,0:T(1,128)}, f32[1,256]{1,0:T(1,128)S(1)}, u32[]{:S(2)}) copy-start(f32[1,256]{1,0:T(1,128)S(1)} %get-tuple-element.119) | copy-start | bytes 3076
  11.1 9.3 %copy-start.42 = (bf16[1,128,256]{2,1,0:T(8,128)(2,1)S(1)}, bf16[1,128,256]{2,1,0:T(8,128)(2,1)}, u32[]{:S(2)}) copy-start(bf16[1,128,256]{2,1,0:T(8,128)(2,1)} %param.28) | copy-start | bytes 196612
  12.0 12.9 %copy-start.48 = (f32[1,256]{1,0:T(1,128)}, f32[1,256]{1,0:T(1,128)S(1)}, u32[]{:S(2)}) copy-start(f32[1,256]{1,0:T(1,128)S(1)} %get-tuple-element.113) | copy-start | bytes 3076
  12.0 12.9 %copy-start.50 = (f32[1,256]{1,0:T(1,128)}, f32[1,256]{1,0:T(1,128)S(1)}, u32[]{:S(2)}) copy-start(f32[1,256]{1,0:T(1,128)S(1)} %get-tuple-element.114) | copy-start | bytes 3076
  12.0 12.9 %copy-start.52 = (f32[1,256]{1,0:T(1,128)}, f32[1,256]{1,0:T(1,128)S(1)}, u32[]{:S(2)}) copy-start(f32[1,256]{1,0:T(1,128)S(1)} %get-tuple-element.116) | copy-start | bytes 3076
  12.0 12.9 %copy-start.54 = (f32[1,256]{1,0:T(1,128)}, f32[1,256]{1,0:T(1,128)S(1)}, u32[]{:S(2)}) copy-start(f32[1,256]{1,0:T(1,128)S(1)} %get-tuple-element.115) | copy-start | bytes 3076
  17.5 2.9 %copy-start.43 = (bf16[1,128,256]{2,1,0:T(8,128)(2,1)S(1)}, bf16[1,128,256]{2,1,0:T(8,128)(2,1)}, u32[]{:S(2)}) copy-start(bf16[1,128,256]{2,1,0:T(8,128)(2,1)} %param.27) | copy-start | bytes 196612
  18.4 2.1 copy-start.16
  22.7 3.7 %copy-start.8 = (f32[128,2048]{1,0:T(8,128)S(1)}, f32[128,2048]{1,0:T(8,128)}, u32[]{:S(2)}) copy-start(f32[128,2048]{1,0:T(8,128)} %convert_element_type.162) | copy-start | bytes 3145732
  22.8 2.1 copy-start.14
  41.5 2.1 copy-start.5
  45.7 9.5 %collective-permute-start.3 = (f32[3,2,16,64,128]{4,3,2,1,0:T(8,128)}, f32[3,2,16,64,128]{4,3,2,1,0:T(8,128)}, u32[]{:S(2)}, u32[]{:S(2)}) collective-permute-start(f32[3,2,16,64,128]{4,3,2,1,0:T(8,128)} %pad_maximum_fusion), channel_id=1, source_target_pairs={{0,4},{4,0},{8,12},{12,8},{1,5},{5,1},{9,13},{13,9},{2,6},{6,2},{1... | collective-permute-start | bytes 9437192 | tf_op jit(solution)/shard_map/ppermute | solution.py:304
  55.2 4.4 %copy-start.72 = (f32[2,16]{1,0:T(2,128)}, f32[2,16]{1,0:T(2,128)S(1)}, u32[]{:S(2)}) copy-start(f32[2,16]{1,0:T(2,128)S(1)} %get-tuple-element.111) | copy-start | bytes 388
  55.2 4.4 %copy-start.73 = (f32[2,16]{1,0:T(2,128)}, f32[2,16]{1,0:T(2,128)S(1)}, u32[]{:S(2)}) copy-start(f32[2,16]{1,0:T(2,128)S(1)} %get-tuple-element.112) | copy-start | bytes 388
  59.6 24.8 %collective-permute-start.4 = (f32[2,16,64,128]{3,2,1,0:T(8,128)S(1)}, f32[2,16,64,128]{3,2,1,0:T(8,128)}, u32[]{:S(2)}, u32[]{:S(2)}) collective-permute-start(f32[2,16,64,128]{3,2,1,0:T(8,128)S(1)} %get-tuple-element.65), channel_id=1, source_target_pairs={{0,8},{4,12},{8,0},{12,4},{1,9},{5,13},{9,1},{13,5},{2,10},{6,14},... | collective-permute-start | bytes 3145736 | tf_op jit(solution)/shard_map/ppermute | solution.py:327
  84.4 45.4 %collective-permute-start.5 = (f32[2,16,64,128]{3,2,1,0:T(8,128)}, f32[2,16,64,128]{3,2,1,0:T(8,128)}, u32[]{:S(2)}, u32[]{:S(2)}) collective-permute-start(f32[2,16,64,128]{3,2,1,0:T(8,128)} %collective-permute-done.4), channel_id=1, source_target_pairs={{0,4},{4,0},{8,12},{12,8},{1,5},{5,1},{9,13},{13,9},{2,6},{6,2},{1... | collective-permute-start | bytes 3145736 | tf_op jit(solution)/shard_map/ppermute | solution.py:328
  129.8 6.9 %copy-start.34 = (f32[128,2,16]{0,2,1:T(8,128)S(1)}, f32[128,2,16]{0,2,1:T(8,128)}, u32[]{:S(2)}) copy-start(f32[128,2,16]{0,2,1:T(8,128)} %get-tuple-element.104) | copy-start | bytes 49156
  158.1 14.1 %copy-start.32 = (f32[1,2048]{1,0:T(1,128)S(1)}, f32[1,2048]{1,0:T(1,128)}, u32[]{:S(2)}) copy-start(f32[1,2048]{1,0:T(1,128)} %get-tuple-element.109) | copy-start | bytes 24580
  172.2 2.0 copy-start.26
  172.2 2.0 copy-start.28
  172.2 2.0 copy-start.30
  174.6 2.2 copy-start.21
  174.6 2.2 copy-start.39
  174.6 2.2 copy-start.66
  174.6 2.2 copy-start.57
  174.6 2.2 copy-start.60
  174.6 2.2 copy-start.63
  176.1 2.1 copy-start.38
  179.0 5.4 %copy-start.13 = (f32[1,128,256]{2,1,0:T(8,128)S(1)}, f32[1,128,256]{2,1,0:T(8,128)}, u32[]{:S(2)}) copy-start(f32[1,128,256]{2,1,0:T(8,128)} %copy-done.12) | copy-start | bytes 393220
  184.3 2.4 %copy-start.24 = (f32[3,2048]{1,0:T(4,128)S(1)}, f32[3,2048]{1,0:T(4,128)}, u32[]{:S(2)}) copy-start(f32[3,2048]{1,0:T(4,128)} %slice_bitcast_fusion.3) | copy-start | bytes 73732
  184.3 2.4 %copy-start.44 = (f32[3,256]{1,0:T(4,128)S(1)}, f32[3,256]{1,0:T(4,128)}, u32[]{:S(2)}) copy-start(f32[3,256]{1,0:T(4,128)} %slice_bitcast_fusion.6) | copy-start | bytes 9220
  187.4 32.1 %collective-permute-start.7 = (f32[3,2560]{1,0:T(4,128)}, f32[3,2560]{1,0:T(4,128)}, u32[]{:S(2)}, u32[]{:S(2)}) collective-permute-start(f32[3,2560]{1,0:T(4,128)} %pad_maximum_fusion.9), channel_id=1, source_target_pairs={{0,12},{1,13},{2,14},{3,15},{16,28},{17,29},{18,30},{19,31}} | collective-permute-start | bytes 92168 | tf_op jit(solution)/shard_map/ppermute | solution.py:378
  188.7 30.8 %collective-permute-start.8 = (f32[3,2560]{1,0:T(4,128)}, f32[3,2560]{1,0:T(4,128)}, u32[]{:S(2)}, u32[]{:S(2)}) collective-permute-start(f32[3,2560]{1,0:T(4,128)} %pad_maximum_fusion.9), channel_id=1, source_target_pairs={{4,12},{5,13},{6,14},{7,15},{20,28},{21,29},{22,30},{23,31}} | collective-permute-start | bytes 92168 | tf_op jit(solution)/shard_map/ppermute | solution.py:378
  191.2 28.3 %collective-permute-start.9 = (f32[3,2560]{1,0:T(4,128)}, f32[3,2560]{1,0:T(4,128)}, u32[]{:S(2)}, u32[]{:S(2)}) collective-permute-start(f32[3,2560]{1,0:T(4,128)} %pad_maximum_fusion.9), channel_id=1, source_target_pairs={{8,12},{9,13},{10,14},{11,15},{24,28},{25,29},{26,30},{27,31}} | collective-permute-start | bytes 92168 | tf_op jit(solution)/shard_map/ppermute | solution.py:378
  196.1 2.6 %copy-start.33 = (f32[1,2048]{1,0:T(1,128)S(1)}, f32[1,2048]{1,0:T(1,128)}, u32[]{:S(2)}) copy-start(f32[1,2048]{1,0:T(1,128)} %get-tuple-element.109) | copy-start | bytes 24580
  198.7 2.0 copy-start.27
  198.7 2.0 copy-start.29
  198.7 2.0 copy-start.31
  204.4 3.3 %copy-start.20 = (f32[128,256]{1,0:T(8,128)S(1)}, f32[128,256]{1,0:T(8,128)}, u32[]{:S(2)}) copy-start(f32[128,256]{1,0:T(8,128)} %get-tuple-element.128) | copy-start | bytes 393220
  204.4 3.3 %copy-start.67 = (f32[1,256]{1,0:T(1,128)S(1)}, f32[1,256]{1,0:T(1,128)}, u32[]{:S(2)}) copy-start(f32[1,256]{1,0:T(1,128)} %copy-done.65) | copy-start | bytes 3076
  204.4 3.4 %copy-start.58 = (f32[1,256]{1,0:T(1,128)S(1)}, f32[1,256]{1,0:T(1,128)}, u32[]{:S(2)}) copy-start(f32[1,256]{1,0:T(1,128)} %copy-done.56) | copy-start | bytes 3076
  204.4 3.4 %copy-start.61 = (f32[1,256]{1,0:T(1,128)S(1)}, f32[1,256]{1,0:T(1,128)}, u32[]{:S(2)}) copy-start(f32[1,256]{1,0:T(1,128)} %copy-done.59) | copy-start | bytes 3076
  204.4 3.4 %copy-start.64 = (f32[1,256]{1,0:T(1,128)S(1)}, f32[1,256]{1,0:T(1,128)}, u32[]{:S(2)}) copy-start(f32[1,256]{1,0:T(1,128)} %copy-done.62) | copy-start | bytes 3076
  208.7 2.0 copy-start.55
  208.7 2.1 copy-start.49
  208.8 2.1 copy-start.51
  208.8 2.1 copy-start.53
  210.7 2.6 %copy-start.69 = (f32[2,16]{1,0:T(2,128)S(1)}, f32[2,16]{1,0:T(2,128)}, u32[]{:S(2)}) copy-start(f32[2,16]{1,0:T(2,128)} %copy-done.68) | copy-start | bytes 388
  210.7 2.6 %copy-start.70 = (f32[32,128]{1,0:T(8,128)S(1)}, f32[32,128]{1,0:T(8,128)}, u32[]{:S(2)}) copy-start(f32[32,128]{1,0:T(8,128)} %get-tuple-element.38) | copy-start | bytes 49156
  210.7 2.6 %copy-start.37 = (f32[32,1,128]{2,1,0:T(1,128)S(1)}, f32[32,1,128]{2,1,0:T(1,128)}, u32[]{:S(2)}) copy-start(f32[32,1,128]{2,1,0:T(1,128)} %param.29) | copy-start | bytes 49156
  210.8 2.6 %copy-start.74 = (f32[32]{0:T(128)S(1)}, f32[32]{0:T(128)}, u32[]{:S(2)}) copy-start(f32[32]{0:T(128)} %param.38) | copy-start | bytes 388
  210.9 8.6 %copy-start.25 = (f32[3,2048]{1,0:T(4,128)S(1)}, f32[3,2048]{1,0:T(4,128)}, u32[]{:S(2)}) copy-start(f32[3,2048]{1,0:T(4,128)} %slice_bitcast_fusion.3) | copy-start | bytes 73732
  210.9 8.6 %copy-start.45 = (f32[3,256]{1,0:T(4,128)S(1)}, f32[3,256]{1,0:T(4,128)}, u32[]{:S(2)}) copy-start(f32[3,256]{1,0:T(4,128)} %slice_bitcast_fusion.6) | copy-start | bytes 9220
  211.0 8.6 %copy-start.47 = (f32[3,256]{1,0:T(4,128)S(1)}, f32[3,256]{1,0:T(4,128)}, u32[]{:S(2)}) copy-start(f32[3,256]{1,0:T(4,128)} %copy-done.46) | copy-start | bytes 9220
  211.0 8.5 %collective-permute-start.6 = (f32[3,2560]{1,0:T(4,128)S(1)}, f32[3,2560]{1,0:T(4,128)S(1)}, u32[]{:S(2)}, u32[]{:S(2)}) collective-permute-start(f32[3,2560]{1,0:T(4,128)S(1)} %pad_maximum_fusion.8), channel_id=1, source_target_pairs={{4,0},{8,4},{12,8},{5,1},{9,5},{13,9},{6,2},{10,6},{14,10},{7,3},{... | collective-permute-start | bytes 92168 | tf_op jit(solution)/shard_map/ppermute | solution.py:22
  216.3 5.5 %copy-start.7 = (f32[131,2048]{1,0:T(8,128)S(1)}, f32[131,2048]{1,0:T(8,128)}, u32[]{:S(2)}) copy-start(f32[131,2048]{1,0:T(8,128)} %pad_add_fusion.1) | copy-start | bytes 3219460
  (21 other events, 25.7 us)

commit v7 on v3

--- a/solution.py
+++ b/solution.py
@@ -150,7 +150,10 @@
         q_end = jnp.sum(xa * lam_b, axis=-1).transpose(1, 2, 0)
         d_step = d_step + to_end * q_end
         wq = push * q_end
-        end_total = jnp.sum(wq, axis=-1) + jnp.exp(cum[..., -1]) * jnp.sum(lam * S0, axis=(-2, -1))
+        end_total = jnp.sum(wq, axis=-1) + jnp.exp(cum[..., -1]) * jnp.sum(
+            jnp.einsum("gkpn,n->gkp", lam * S0, jnp.ones((S0.shape[-1],), jnp.float32), precision=EXACT_DOT),
+            axis=-1,
+        )
         d_cum = d_cum - wq
         d_cum = d_cum.at[..., -1].add(end_total)
     d_log = jnp.flip(jnp.cumsum(jnp.flip(d_cum, -1), axis=-1), -1)

time: 208 us -> 207 us (level)
  matrix products: 16.2 us -> 19.7 us
  other arithmetic: 65 us -> 61.7 us
    reduce_sum x1, other arithmetic: 5.48 us -> 0.09 us  [block_outer(): jnp.sum(jnp.einsum('gkpn,n->gkp', lam * S0, jnp.ones((S0.shape[-1],), jnp...]
    select_n x0 -> x1, other arithmetic: none -> 4.43 us  [shards(): jnp.where(core == 0, chip_start, decay_even * chip_start + even[0])]
    dot_general x0 -> x1, matrix products: none -> 2.53 us  [block_outer(): jnp.einsum('gkpn,n->gkp', lam * S0, jnp.ones((S0.shape[-1],), jnp.float32...]
    unnamed x185 -> x191, local copies, waits for them, and re-layouts: 6.58 us -> 5.78 us
  transfers between devices with their start and end apart: 10 -> 10, of which waited for: 2 -> 2; matrix products, arithmetic and copies ran while one was open for 34% -> 32% of each run, Pallas kernels for 7% -> 7%
where the time goes in v7:
time: 207 us; the launch traced here: 205 us
  other arithmetic  61.7 us (30%)
  local copies, waits for them, and re-layouts  50.5 us (24%)
  Pallas kernels  28.2 us (14%)
  waiting for transfers between devices  28.1 us (14%)
  matrix products  19.7 us (10%)
  starting transfers between devices  13.3 us (6%)
  between operations  3.37 us (2%)
    pallas_call x2, Pallas kernels, block_inner(): pl.pallas_call(functools.partial(_grad_kernel, steps_per_group), grid=(nh...  28.2 us
    ppermute x1, waiting for transfers between devices, shards(): incoming = lax.ppermute(outgoing, 'suf', route)  24.4 us
    reshape x2, other arithmetic, block_inner(): pl.pallas_call(functools.partial(_grad_kernel, steps_per_group), grid=(nh...  7.1 us
    mul x12, other arithmetic, causal_conv(): padded[tap_index:tap_index + num_tokens]  6.47 us
    unnamed x191, local copies, waits for them, and re-layouts  5.78 us
    split x3, local copies, waits for them, and re-layouts, causal_conv(): padded = jnp.concatenate([context, values], axis=0)  5.33 us
    ppermute x3, starting transfers between devices, shards(): lax.ppermute(ctx_grads, 'suf', [(sender, num_ways - 1)])  5.29 us
    dot_general x2, matrix products, block_outer(): dc = dc + jnp.einsum('tgkp,gkpn->tgn', g_grow, S0, precision=EXACT_DOT)  5.23 us
  transfers between devices with their start and end apart: 10, of which 2 were waited for; matrix products, arithmetic and copies ran while one was open for 32% of the time, Pallas kernels for 7%

profile of v7, /device:TPU:1, one launch (start us, length us, event | category | flops | bytes accessed | tf_op | source)
XLA Modules:
  0.0 204.9 jit_solution(1101361562970301587)
XLA Ops:
  4.2 2.7 %collective-permute-start = (f32[7712]{0:T(1024)S(1)}, f32[7712]{0:T(1024)S(1)}, u32[]{:S(2)}, u32[]{:S(2)}) collective-permute-start(f32[7712]{0:T(1024)S(1)} %pad_maximum_fusion.10), channel_id=1, source_target_pairs={{0,4},{4,8},{8,12},{12,0},{1,5},{5,9},{9,13},{13,1},{2,6},{6,10},{... | collective-permute-start | bytes 92552 | tf_op jit(solution)/shard_map/ppermute | solution.py:223
  7.3 1.4 exponential_multiply_fusion.1
  12.0 1.5 slice_convert_fusion.6
  16.2 1.2 fusion.115
  19.3 1.1 convert_element_type.162
  20.4 1.1 convert_element_type.169
  26.2 2.5 %fusion.39 = (f32[128,2048]{1,0:T(8,128)S(1)}, f32[128,2048]{1,0:T(8,128)}) fusion(f32[128,2048]{1,0:T(8,128)S(1)} %copy-done.22, f32[2048]{0:T(1024)} %bitcast.272, f32[2048]{0:T(1024)} %bitcast.268, f32[3,2048]{1,0:T(4,128)} %slice.288, f32[2048]{0:T(1024)} %bitcast.264, f32[2048]{0:T(1024)} %bitcast.260), kind=kLoop, calls=%fused_computation.85 | loop fusion | flops 3670016 | bytes 3203072 | tf_op jit(solution)/shard_map/jvp(jit(silu))/mul | solution.py:33
  29.1 1.7 multiply_bitcast_fusion.1
  31.6 5.4 %multiply_bitcast_fusion = (f32[128,2048]{1,0:T(8,128)}, f32[1,128,2048]{2,1,0:T(8,128)}, f32[1,128,2048]{2,1,0:T(8,128)}, f32[128,2048]{1,0:T(8,128)}) fusion(f32[1,128,2048]{2,1,0:T(8,128)} %convert_element_type.169, f32[2048]{0:T(1024)} %bitcast.273, f32[2048]{0:T(1024)} %bitcast.269, f32[1,3,2048]{2,1,0:T(4,128)} %slice_bitcast_fusion.5, ...), kind=kLoop, calls=%fused_computation.74 | loop fusion | flops 4194304 | bytes 5825024 | tf_op jit(solution)/shard_map/vmap()/squeeze;vmap()/reshape;vmap()/reshape | solution.py:102
  37.0 1.5 copy.146
  38.5 1.1 reshape.510
  39.7 1.8 convolution_bitcast_fusion.5
  41.4 1.0 convolution_bitcast_fusion.3
  42.5 1.0 convolution_bitcast_fusion.4
  43.6 1.9 pad_maximum_fusion
  45.5 1.4 collective-permute-start.3
  48.9 3.6 %collective-permute-done.3 = f32[3,2,16,64,128]{4,3,2,1,0:T(8,128)} collective-permute-done((f32[3,2,16,64,128]{4,3,2,1,0:T(8,128)}, f32[3,2,16,64,128]{4,3,2,1,0:T(8,128)}, u32[]{:S(2)}, u32[]{:S(2)}) %collective-permute-start.3) | collective-permute-done | bytes 3145760 | tf_op jit(solution)/shard_map/ppermute | solution.py:307
  52.6 3.5 %broadcast_select_fusion.1 = (f32[3,2,16,64,128]{4,3,2,1,0:T(8,128)S(1)}, f32[3,2,16,64,128]{4,3,2,1,0:T(8,128)S(1)}) fusion(f32[3,2,16,64,128]{4,3,2,1,0:T(8,128)} %collective-permute-done.3, pred[]{:T(512)S(6)} %eq.58, f32[1,2,16,64,128]{4,3,2,1,0:T(8,128)} %copy-done.17, f32[1,2,16,64,128]{4,3,2,1,0:T(8,128)} %copy-done.18, ...), kind=kLoop, calls=%fused_computation.9 | loop fusion | flops 3145728 | bytes 12582913 | tf_op jit(solution)/shard_map/jit(_where)/select_n | solution.py:309
  56.1 2.0 fusion.31
  58.1 24.4 %collective-permute-done.4 = f32[2,16,64,128]{3,2,1,0:T(8,128)} collective-permute-done((f32[2,16,64,128]{3,2,1,0:T(8,128)S(1)}, f32[2,16,64,128]{3,2,1,0:T(8,128)}, u32[]{:S(2)}, u32[]{:S(2)}) %collective-permute-start.4) | collective-permute-done | bytes 1048608 | tf_op jit(solution)/shard_map/ppermute | solution.py:327
  82.5 1.2 collective-permute-start.5
  83.8 2.1 %convert_element_type.163.g_ref = f32[128,2048]{1,0:T(8,128)} convert(bf16[128,2048]{1,0:T(8,128)(2,1)} %param.25) | non-fusion elementwise | flops 262144 | bytes 1572864 | tf_op jit(solution)/shard_map/convert_element_type | solution.py:248
  85.9 1.5 copy.134
  87.9 1.6 negate_multiply_fusion
  89.5 1.6 copy.135
  91.1 1.9 reduce_window_sum.47
  92.9 1.4 slice.303
  94.3 1.3 copy.202
  95.7 1.4 exponential_bitcast_fusion
  97.1 1.5 copy.139
  98.5 1.3 broadcast_in_dim.60
  99.9 1.4 broadcast_in_dim.62.skip_ref
  101.2 1.3 multiply_reduce_fusion.1
  102.6 1.2 mul.870
  103.8 1.3 mul.892
  105.1 14.1 %shard_map.242 = (f32[128,2048]{1,0:T(8,128)}, f32[32,128]{1,0:T(8,128)}, f32[32,128]{1,0:T(8,128)}, f32[128,256]{1,0:T(8,128)}, f32[128,256]{1,0:T(8,128)}) custom-call(f32[128,2048]{1,0:T(8,128)} %copy-done.13, f32[128,2048]{1,0:T(8,128)} %convert_element_type.163.g_ref, f32[128,256]{1,0:T(8,128)} %copy-done.27, f32[128,256]{1,0:T(8,128)} %get-tuple-element.64.c_ref, ...), custom_call_target="tpu_custom_call" | custom-call | tf_op jit(solution)/shard_map/pallas_call | solution.py:102
  119.2 1.5 copy.163
  120.6 1.5 copy.160
  122.1 2.6 %copy.136 = f32[128,2048]{0,1:T(8,128)} copy(f32[128,2048]{1,0:T(8,128)} %get-tuple-element.30) | data formatting | bytes 2097152 | tf_op jit(solution)/shard_map/pallas_call | solution.py:102
  124.7 1.7 copy.189
  126.3 1.7 copy.191
  128.0 4.4 %add_select_fusion = (f32[2,16,64,128]{3,2,1,0:T(8,128)S(1)}, f32[2,16,64,128]{3,2,1,0:T(8,128)S(1)}, f32[2,16,64,128]{3,2,1,0:T(8,128)}) fusion(f32[2,16,64,128]{3,2,1,0:T(8,128)} %get-tuple-element.63, f32[3,2,16,64,128]{4,3,2,1,0:T(8,128)} %copy-done, f32[2,16]{1,0:T(2,128)} %mul.892, f32[2,16]{1,0:T(2,128)} %copy-done.91, pred[]{:T(512)S(6)} %eq.62, ...), kind=kLoop, calls=%fused_computation.76 | loop fusion | flops 6029312 | bytes 10486279 | tf_op jit(solution)/shard_map/jit(_where)/select_n | solution.py:358
  132.4 2.1 %multiply_reduce_fusion = (f32[128,2,16]{0,2,1:T(8,128)S(1)}, f32[128,2,16,64]{0,3,2,1:T(8,128)}) fusion(f32[128,2048]{0,1:T(8,128)S(1)} %copy-done.4, f32[2,16,64,128]{3,2,1,0:T(8,128)S(1)} %get-tuple-element.73, f32[128,2,128,1]{2,1,0,3:T(2,128)S(1)} %bitcast.248), kind=kOutput, calls=%fused_computation.72 | convolution fusion | flops 403173376 | bytes 3293184 | tf_op jit(solution)/shard_map/gkpn,sgn->sgkp/dot_general | solution.py:147
  134.5 2.5 %fusion.34 = f32[1,2,16,64]{3,0,2,1:T(1,128)S(1)} fusion(f32[2,16,64,128]{3,2,1,0:T(8,128)S(1)} %get-tuple-element.73, f32[2,16,64,128]{3,2,1,0:T(8,128)S(1)} %get-tuple-element.72), kind=kOutput, calls=%fused_computation.70 | convolution fusion | flops 3407872 | bytes 2105344 | tf_op jit(solution)/shard_map/gkpn,n->gkp/dot_general | solution.py:154
  137.2 2.3 %fusion.3 = f32[128,2,16]{0,2,1:T(8,128)S(1)} fusion(f32[2,16,64,128]{3,2,1,0:T(8,128)} %copy-done.11, f32[128,2,16,64]{0,3,2,1:T(8,128)S(1)} %bitcast.237, f32[128,2,16]{0,2,1:T(8,128)S(1)} %copy-done.53, f32[128,2,128,1]{2,1,0,3:T(2,128)S(1)} %bitcast.250), kind=kOutput, calls=%fused_computation.19 | convolution fusion | flops 403435520 | bytes 2260992 | tf_op jit(solution)/shard_map/tgn,gkpn->tgkp/dot_general | solution.py:141
  141.9 14.1 %vmap__.1 = (f32[128,2048]{1,0:T(8,128)}, f32[32,128]{1,0:T(8,128)}, f32[32,128]{1,0:T(8,128)}, f32[128,256]{1,0:T(8,128)}, f32[128,256]{1,0:T(8,128)}) custom-call(f32[128,2048]{1,0:T(8,128)} %get-tuple-element.54.x_ref, f32[128,2048]{1,0:T(8,128)} %get-tuple-element.133.g_ref, f32[128,256]{1,0:T(8,128)} %get-tuple-element.52.b_ref, ...), custom_call_target="tpu_custom_call" | custom-call | tf_op jit(solution)/shard_map/vmap()/pallas_call | solution.py:102
  156.1 1.7 broadcast_multiply_fusion
  162.6 3.4 %fusion.4 = f32[1,128,2,128]{1,3,2,0:T(8,128)} fusion(f32[1,128,2,128]{1,3,2,0:T(8,128)} %bitcast.256, f32[2,16,64,128]{3,2,1,0:T(8,128)S(1)} %copy-done.14, f32[128,2,16,64]{0,3,2,1:T(8,128)S(1)} %bitcast.240, f32[128,2,16]{0,2,1:T(8,128)S(1)} %exponential_bitcast_fusion.1), kind=kOutput, calls=%fused_computation.23 | convolution fusion | flops 402948096 | bytes 2375680 | tf_op jit(solution)/shard_map/vmap(tgkp,gkpn->tgn)/dot_general | solution.py:142
  166.0 1.7 copy.194
  167.7 1.1 broadcast_multiply_fusion.12
  170.2 1.4 pad_maximum_fusion.9
  171.6 1.3 collective-permute-start.7
  172.9 2.5 %collective-permute-start.8 = (f32[3,2560]{1,0:T(4,128)}, f32[3,2560]{1,0:T(4,128)}, u32[]{:S(2)}, u32[]{:S(2)}) collective-permute-start(f32[3,2560]{1,0:T(4,128)} %pad_maximum_fusion.9), channel_id=1, source_target_pairs={{4,12},{5,13},{6,14},{7,15},{20,28},{21,29},{22,30},{23,31}} | collective-permute-start | bytes 92168 | tf_op jit(solution)/shard_map/ppermute | solution.py:378
  175.4 1.5 collective-permute-start.9
  177.6 1.2 multiply_add_fusion
  178.9 1.6 copy.149
  182.3 1.4 pad_add_fusion.1
  184.3 1.1 fusion.2
  186.1 2.6 %fusion.5 = f32[128,2,128]{0,2,1:T(8,128)S(1)} fusion(f32[128,2,128]{0,2,1:T(8,128)S(1)} %bitcast.253, f32[2,16,64,128]{3,2,1,0:T(8,128)S(1)} %copy-done.2, f32[2,16,128,64]{2,3,1,0:T(8,128)S(1)} %bitcast.235, f32[2,16,128]{2,1,0:T(8,128)} %copy.151), kind=kOutput, calls=%fused_computation.24 | convolution fusion | flops 402948096 | bytes 2375680 | tf_op jit(solution)/shard_map/gkpn,sgkp,gks->sgn/dot_general | solution.py:149
  190.4 1.8 fusion.6
  193.2 2.3 %collective-permute-start.6 = (f32[3,2560]{1,0:T(4,128)S(1)}, f32[3,2560]{1,0:T(4,128)S(1)}, u32[]{:S(2)}, u32[]{:S(2)}) collective-permute-start(f32[3,2560]{1,0:T(4,128)S(1)} %pad_maximum_fusion.8), channel_id=1, source_target_pairs={{4,0},{8,4},{12,8},{5,1},{9,5},{13,9},{6,2},{10,6},{14,10},{7,3},{... | collective-permute-start | bytes 92168 | tf_op jit(solution)/shard_map/ppermute | solution.py:22
  196.3 2.1 %split.67 = bf16[1,128,2048]{2,1,0:T(8,128)(2,1)} slice(f32[1,131,2048]{2,1,0:T(8,128)} %copy-done.25), slice={[0:1], [3:131], [0:2048]} | slice | bytes 1048576 | tf_op jit(solution)/shard_map/vmap(transpose(jvp()))/split | solution.py:26
  198.5 1.6 split.69
  200.1 1.5 split.68
  (305 shorter events, 37.4 us)
Async XLA Ops:
  0.6 18.6 %copy-start.33 = (bf16[128,2048]{1,0:T(8,128)(2,1)S(1)}, bf16[128,2048]{1,0:T(8,128)(2,1)}, u32[]{:S(2)}) copy-start(bf16[128,2048]{1,0:T(8,128)(2,1)} %param.21) | copy-start | bytes 1572868
  4.2 17.5 %collective-permute-start = (f32[7712]{0:T(1024)S(1)}, f32[7712]{0:T(1024)S(1)}, u32[]{:S(2)}, u32[]{:S(2)}) collective-permute-start(f32[7712]{0:T(1024)S(1)} %pad_maximum_fusion.10), channel_id=1, source_target_pairs={{0,4},{4,8},{8,12},{12,0},{1,5},{5,9},{9,13},{13,1},{2,6},{6,10},{... | collective-permute-start | bytes 92552 | tf_op jit(solution)/shard_map/ppermute | solution.py:223
  6.9 14.9 %collective-permute-start.1 = (f32[7712]{0:T(1024)S(1)}, f32[7712]{0:T(1024)S(1)}, u32[]{:S(2)}, u32[]{:S(2)}) collective-permute-start(f32[7712]{0:T(1024)S(1)} %pad_maximum_fusion.10), channel_id=1, source_target_pairs={{0,8},{4,12},{8,0},{12,4},{1,9},{5,13},{9,1},{13,5},{2,10},{6,14},... | collective-permute-start | bytes 92552 | tf_op jit(solution)/shard_map/ppermute | solution.py:223
  6.9 14.9 %collective-permute-start.2 = (f32[7712]{0:T(1024)S(1)}, f32[7712]{0:T(1024)S(1)}, u32[]{:S(2)}, u32[]{:S(2)}) collective-permute-start(f32[7712]{0:T(1024)S(1)} %pad_maximum_fusion.10), channel_id=1, source_target_pairs={{0,12},{4,0},{8,4},{12,8},{1,13},{5,1},{9,5},{13,9},{2,14},{6,2},{... | collective-permute-start | bytes 92552 | tf_op jit(solution)/shard_map/ppermute | solution.py:223
  9.5 5.3 %copy-start.84 = (f32[2,16]{1,0:T(2,128)}, f32[2,16]{1,0:T(2,128)S(1)}, u32[]{:S(2)}) copy-start(f32[2,16]{1,0:T(2,128)S(1)} %mul.837) | copy-start | bytes 388
  11.1 13.6 %copy-start.76 = (f32[1,256]{1,0:T(1,128)}, f32[1,256]{1,0:T(1,128)S(1)}, u32[]{:S(2)}) copy-start(f32[1,256]{1,0:T(1,128)S(1)} %get-tuple-element.118) | copy-start | bytes 3076
  11.1 13.6 %copy-start.78 = (f32[1,256]{1,0:T(1,128)}, f32[1,256]{1,0:T(1,128)S(1)}, u32[]{:S(2)}) copy-start(f32[1,256]{1,0:T(1,128)S(1)} %get-tuple-element.119) | copy-start | bytes 3076
  11.1 13.6 %copy-start.80 = (f32[1,256]{1,0:T(1,128)}, f32[1,256]{1,0:T(1,128)S(1)}, u32[]{:S(2)}) copy-start(f32[1,256]{1,0:T(1,128)S(1)} %get-tuple-element.121) | copy-start | bytes 3076
  11.1 13.6 %copy-start.82 = (f32[1,256]{1,0:T(1,128)}, f32[1,256]{1,0:T(1,128)S(1)}, u32[]{:S(2)}) copy-start(f32[1,256]{1,0:T(1,128)S(1)} %get-tuple-element.120) | copy-start | bytes 3076
  11.1 9.2 %copy-start.63 = (bf16[1,128,256]{2,1,0:T(8,128)(2,1)S(1)}, bf16[1,128,256]{2,1,0:T(8,128)(2,1)}, u32[]{:S(2)}) copy-start(bf16[1,128,256]{2,1,0:T(8,128)(2,1)} %param.28) | copy-start | bytes 196612
  12.0 12.7 %copy-start.68 = (f32[1,256]{1,0:T(1,128)}, f32[1,256]{1,0:T(1,128)S(1)}, u32[]{:S(2)}) copy-start(f32[1,256]{1,0:T(1,128)S(1)} %get-tuple-element.114) | copy-start | bytes 3076
  12.0 12.8 %copy-start.70 = (f32[1,256]{1,0:T(1,128)}, f32[1,256]{1,0:T(1,128)S(1)}, u32[]{:S(2)}) copy-start(f32[1,256]{1,0:T(1,128)S(1)} %get-tuple-element.115) | copy-start | bytes 3076
  12.0 12.8 %copy-start.72 = (f32[1,256]{1,0:T(1,128)}, f32[1,256]{1,0:T(1,128)S(1)}, u32[]{:S(2)}) copy-start(f32[1,256]{1,0:T(1,128)S(1)} %get-tuple-element.117) | copy-start | bytes 3076
  12.0 12.8 %copy-start.74 = (f32[1,256]{1,0:T(1,128)}, f32[1,256]{1,0:T(1,128)S(1)}, u32[]{:S(2)}) copy-start(f32[1,256]{1,0:T(1,128)S(1)} %get-tuple-element.116) | copy-start | bytes 3076
  17.4 2.9 %copy-start.64 = (bf16[1,128,256]{2,1,0:T(8,128)(2,1)S(1)}, bf16[1,128,256]{2,1,0:T(8,128)(2,1)}, u32[]{:S(2)}) copy-start(bf16[1,128,256]{2,1,0:T(8,128)(2,1)} %param.27) | copy-start | bytes 196612
  21.7 20.8 %copy-start.6 = (f32[128,2048]{0,1:T(8,128)}, f32[128,2048]{0,1:T(8,128)S(1)}, u32[]{:S(2)}) copy-start(f32[128,2048]{0,1:T(8,128)S(1)} %copy.144) | copy-start | bytes 3145732
  22.6 3.7 %copy-start.22 = (f32[128,2048]{1,0:T(8,128)S(1)}, f32[128,2048]{1,0:T(8,128)}, u32[]{:S(2)}) copy-start(f32[128,2048]{1,0:T(8,128)} %convert_element_type.162) | copy-start | bytes 3145732
  29.1 10.6 %copy-start.3 = (f32[128,2048]{0,1:T(8,128)}, f32[128,2048]{0,1:T(8,128)S(1)}, u32[]{:S(2)}) copy-start(f32[128,2048]{0,1:T(8,128)S(1)} %copy.142) | copy-start | bytes 3145732
  38.5 2.9 %copy-start.8 = (f32[1,128,2048]{1,2,0:T(8,128)}, f32[1,128,2048]{1,2,0:T(8,128)S(1)}, u32[]{:S(2)}) copy-start(f32[1,128,2048]{1,2,0:T(8,128)S(1)} %copy.146) | copy-start | bytes 3145732
  41.4 2.2 %copy-start.16 = (f32[1,2,16,64,128]{4,3,2,1,0:T(8,128)}, f32[1,2,16,64,128]{4,3,2,1,0:T(8,128)S(1)}, u32[]{:S(2)}) copy-start(f32[1,2,16,64,128]{4,3,2,1,0:T(8,128)S(1)} %convolution_bitcast_fusion.5) | copy-start | bytes 3145732
  45.5 7.0 %collective-permute-start.3 = (f32[3,2,16,64,128]{4,3,2,1,0:T(8,128)}, f32[3,2,16,64,128]{4,3,2,1,0:T(8,128)}, u32[]{:S(2)}, u32[]{:S(2)}) collective-permute-start(f32[3,2,16,64,128]{4,3,2,1,0:T(8,128)} %pad_maximum_fusion), channel_id=1, source_target_pairs={{0,4},{4,0},{8,12},{12,8},{1,5},{5,1},{9,13},{13,9},{2,6},{6,2},{1... | collective-permute-start | bytes 9437192 | tf_op jit(solution)/shard_map/ppermute | solution.py:307
  48.9 7.2 %copy-start.90 = (f32[2,16]{1,0:T(2,128)}, f32[2,16]{1,0:T(2,128)S(1)}, u32[]{:S(2)}) copy-start(f32[2,16]{1,0:T(2,128)S(1)} %get-tuple-element.112) | copy-start | bytes 388
  48.9 7.2 %copy-start.91 = (f32[2,16]{1,0:T(2,128)}, f32[2,16]{1,0:T(2,128)S(1)}, u32[]{:S(2)}) copy-start(f32[2,16]{1,0:T(2,128)S(1)} %get-tuple-element.113) | copy-start | bytes 388
  48.9 7.2 %copy-start.94 = (f32[2,16]{1,0:T(2,128)S(1)}, f32[2,16]{1,0:T(2,128)}, u32[]{:S(2)}) copy-start(f32[2,16]{1,0:T(2,128)} %exp.142) | copy-start | bytes 388
  58.1 24.5 %collective-permute-start.4 = (f32[2,16,64,128]{3,2,1,0:T(8,128)S(1)}, f32[2,16,64,128]{3,2,1,0:T(8,128)}, u32[]{:S(2)}, u32[]{:S(2)}) collective-permute-start(f32[2,16,64,128]{3,2,1,0:T(8,128)S(1)} %get-tuple-element.62), channel_id=1, source_target_pairs={{0,8},{4,12},{8,0},{12,4},{1,9},{5,13},{9,1},{13,5},{2,10},{6,14},... | collective-permute-start | bytes 3145736 | tf_op jit(solution)/shard_map/ppermute | solution.py:327
  82.5 45.5 %collective-permute-start.5 = (f32[2,16,64,128]{3,2,1,0:T(8,128)}, f32[2,16,64,128]{3,2,1,0:T(8,128)}, u32[]{:S(2)}, u32[]{:S(2)}) collective-permute-start(f32[2,16,64,128]{3,2,1,0:T(8,128)} %collective-permute-done.4), channel_id=1, source_target_pairs={{0,4},{4,0},{8,12},{12,8},{1,5},{5,1},{9,13},{13,9},{2,6},{6,2},{1... | collective-permute-start | bytes 3145736 | tf_op jit(solution)/shard_map/ppermute | solution.py:328
  128.0 4.4 %copy-start.4 = (f32[128,2048]{0,1:T(8,128)S(1)}, f32[128,2048]{0,1:T(8,128)}, u32[]{:S(2)}) copy-start(f32[128,2048]{0,1:T(8,128)} %copy-done.3) | copy-start | bytes 3145732
  132.4 2.1 %copy-start.11 = (f32[2,16,64,128]{3,2,1,0:T(8,128)}, f32[2,16,64,128]{3,2,1,0:T(8,128)S(1)}, u32[]{:S(2)}) copy-start(f32[2,16,64,128]{3,2,1,0:T(8,128)S(1)} %get-tuple-element.72) | copy-start | bytes 3145732
  134.5 2.6 %copy-start.7 = (f32[128,2048]{0,1:T(8,128)S(1)}, f32[128,2048]{0,1:T(8,128)}, u32[]{:S(2)}) copy-start(f32[128,2048]{0,1:T(8,128)} %copy-done.6) | copy-start | bytes 3145732
  134.5 2.6 %copy-start.53 = (f32[128,2,16]{0,2,1:T(8,128)S(1)}, f32[128,2,16]{0,2,1:T(8,128)}, u32[]{:S(2)}) copy-start(f32[128,2,16]{0,2,1:T(8,128)} %get-tuple-element.105) | copy-start | bytes 49156
  137.1 2.6 %copy-start.30 = (f32[2,16,128]{1,0,2:T(2,128)S(1)}, f32[2,16,128]{1,0,2:T(2,128)}, u32[]{:S(2)}) copy-start(f32[2,16,128]{1,0,2:T(2,128)} %copy.139) | copy-start | bytes 49156
  137.2 2.6 %copy-start.31 = (f32[2,16,128]{1,0,2:T(2,128)S(1)}, f32[2,16,128]{1,0,2:T(2,128)}, u32[]{:S(2)}) copy-start(f32[2,16,128]{1,0,2:T(2,128)} %copy.134) | copy-start | bytes 49156
  137.2 2.8 %copy-start.38 = (f32[2,16,128]{1,0,2:T(2,128)S(1)}, f32[2,16,128]{1,0,2:T(2,128)}, u32[]{:S(2)}) copy-start(f32[2,16,128]{1,0,2:T(2,128)} %copy.163) | copy-start | bytes 49156
  141.9 14.2 %copy-start.24 = (f32[1,128,2048]{2,1,0:T(8,128)S(1)}, f32[1,128,2048]{2,1,0:T(8,128)}, u32[]{:S(2)}) copy-start(f32[1,128,2048]{2,1,0:T(8,128)} %get-tuple-element.55) | copy-start | bytes 3145732
  141.9 14.2 %copy-start.51 = (f32[1,2048]{1,0:T(1,128)S(1)}, f32[1,2048]{1,0:T(1,128)}, u32[]{:S(2)}) copy-start(f32[1,2048]{1,0:T(1,128)} %get-tuple-element.110) | copy-start | bytes 24580
  158.2 2.2 %copy-start.41 = (f32[1,128,256]{2,1,0:T(8,128)S(1)}, f32[1,128,256]{2,1,0:T(8,128)}, u32[]{:S(2)}) copy-start(f32[1,128,256]{2,1,0:T(8,128)} %get-tuple-element.53) | copy-start | bytes 393220
  158.2 2.2 %copy-start.61 = (f32[128,256]{1,0:T(8,128)S(1)}, f32[128,256]{1,0:T(8,128)}, u32[]{:S(2)}) copy-start(f32[128,256]{1,0:T(8,128)} %get-tuple-element.34) | copy-start | bytes 393220
  158.2 2.2 %copy-start.83 = (f32[1,256]{1,0:T(1,128)S(1)}, f32[1,256]{1,0:T(1,128)}, u32[]{:S(2)}) copy-start(f32[1,256]{1,0:T(1,128)} %copy-done.82) | copy-start | bytes 3076
  158.2 2.2 %copy-start.77 = (f32[1,256]{1,0:T(1,128)S(1)}, f32[1,256]{1,0:T(1,128)}, u32[]{:S(2)}) copy-start(f32[1,256]{1,0:T(1,128)} %copy-done.76) | copy-start | bytes 3076
  158.2 2.2 %copy-start.79 = (f32[1,256]{1,0:T(1,128)S(1)}, f32[1,256]{1,0:T(1,128)}, u32[]{:S(2)}) copy-start(f32[1,256]{1,0:T(1,128)} %copy-done.78) | copy-start | bytes 3076
  158.2 2.2 %copy-start.81 = (f32[1,256]{1,0:T(1,128)S(1)}, f32[1,256]{1,0:T(1,128)}, u32[]{:S(2)}) copy-start(f32[1,256]{1,0:T(1,128)} %copy-done.80) | copy-start | bytes 3076
  158.3 4.3 %copy-start.14 = (f32[2,16,64,128]{3,2,1,0:T(8,128)S(1)}, f32[2,16,64,128]{3,2,1,0:T(8,128)}, u32[]{:S(2)}) copy-start(f32[2,16,64,128]{3,2,1,0:T(8,128)} %get-tuple-element.74) | copy-start | bytes 3145732
  159.7 2.1 %copy-start.60 = (f32[128,256]{1,0:T(8,128)S(1)}, f32[128,256]{1,0:T(8,128)}, u32[]{:S(2)}) copy-start(f32[128,256]{1,0:T(8,128)} %get-tuple-element.35) | copy-start | bytes 393220
  159.7 2.8 %copy-start.9 = (f32[1,128,2048]{1,2,0:T(8,128)S(1)}, f32[1,128,2048]{1,2,0:T(8,128)}, u32[]{:S(2)}) copy-start(f32[1,128,2048]{1,2,0:T(8,128)} %copy-done.8) | copy-start | bytes 3145732
  162.6 5.1 %copy-start.29 = (f32[1,128,256]{2,1,0:T(8,128)S(1)}, f32[1,128,256]{2,1,0:T(8,128)}, u32[]{:S(2)}) copy-start(f32[1,128,256]{2,1,0:T(8,128)} %copy-done.28) | copy-start | bytes 393220
  167.6 10.0 %copy-start.20 = (f32[128,2,16,64]{0,3,2,1:T(8,128)S(1)}, f32[128,2,16,64]{0,3,2,1:T(8,128)}, u32[]{:S(2)}) copy-start(f32[128,2,16,64]{0,3,2,1:T(8,128)} %get-tuple-element.127) | copy-start | bytes 3145732
  167.7 10.0 %copy-start.21 = (f32[128,2048]{0,1:T(8,128)S(1)}, f32[128,2048]{0,1:T(8,128)}, u32[]{:S(2)}) copy-start(f32[128,2048]{0,1:T(8,128)} %copy.136) | copy-start | bytes 3145732
  170.2 7.4 %copy-start.66 = (f32[3,256]{1,0:T(4,128)}, f32[3,256]{1,0:T(4,128)S(1)}, u32[]{:S(2)}) copy-start(f32[3,256]{1,0:T(4,128)S(1)} %slice_bitcast_fusion.6) | copy-start | bytes 9220
  171.6 30.1 %collective-permute-start.7 = (f32[3,2560]{1,0:T(4,128)}, f32[3,2560]{1,0:T(4,128)}, u32[]{:S(2)}, u32[]{:S(2)}) collective-permute-start(f32[3,2560]{1,0:T(4,128)} %pad_maximum_fusion.9), channel_id=1, source_target_pairs={{0,12},{1,13},{2,14},{3,15},{16,28},{17,29},{18,30},{19,31}} | collective-permute-start | bytes 92168 | tf_op jit(solution)/shard_map/ppermute | solution.py:378
  172.9 28.8 %collective-permute-start.8 = (f32[3,2560]{1,0:T(4,128)}, f32[3,2560]{1,0:T(4,128)}, u32[]{:S(2)}, u32[]{:S(2)}) collective-permute-start(f32[3,2560]{1,0:T(4,128)} %pad_maximum_fusion.9), channel_id=1, source_target_pairs={{4,12},{5,13},{6,14},{7,15},{20,28},{21,29},{22,30},{23,31}} | collective-permute-start | bytes 92168 | tf_op jit(solution)/shard_map/ppermute | solution.py:378
  175.4 26.3 %collective-permute-start.9 = (f32[3,2560]{1,0:T(4,128)}, f32[3,2560]{1,0:T(4,128)}, u32[]{:S(2)}, u32[]{:S(2)}) collective-permute-start(f32[3,2560]{1,0:T(4,128)} %pad_maximum_fusion.9), channel_id=1, source_target_pairs={{8,12},{9,13},{10,14},{11,15},{24,28},{25,29},{26,30},{27,31}} | collective-permute-start | bytes 92168 | tf_op jit(solution)/shard_map/ppermute | solution.py:378
  186.1 2.7 %copy-start.40 = (f32[128,256]{1,0:T(8,128)S(1)}, f32[128,256]{1,0:T(8,128)}, u32[]{:S(2)}) copy-start(f32[128,256]{1,0:T(8,128)} %get-tuple-element.129) | copy-start | bytes 393220
  190.4 2.1 %copy-start.69 = (f32[1,256]{1,0:T(1,128)S(1)}, f32[1,256]{1,0:T(1,128)}, u32[]{:S(2)}) copy-start(f32[1,256]{1,0:T(1,128)} %copy-done.68) | copy-start | bytes 3076
  190.4 2.1 %copy-start.71 = (f32[1,256]{1,0:T(1,128)S(1)}, f32[1,256]{1,0:T(1,128)}, u32[]{:S(2)}) copy-start(f32[1,256]{1,0:T(1,128)} %copy-done.70) | copy-start | bytes 3076
  190.4 2.1 %copy-start.73 = (f32[1,256]{1,0:T(1,128)S(1)}, f32[1,256]{1,0:T(1,128)}, u32[]{:S(2)}) copy-start(f32[1,256]{1,0:T(1,128)} %copy-done.72) | copy-start | bytes 3076
  192.4 3.0 %copy-start.86 = (f32[2,16]{1,0:T(2,128)S(1)}, f32[2,16]{1,0:T(2,128)}, u32[]{:S(2)}) copy-start(f32[2,16]{1,0:T(2,128)} %copy-done.84) | copy-start | bytes 388
  192.4 3.0 %copy-start.87 = (f32[32,128]{1,0:T(8,128)S(1)}, f32[32,128]{1,0:T(8,128)}, u32[]{:S(2)}) copy-start(f32[32,128]{1,0:T(8,128)} %get-tuple-element.38) | copy-start | bytes 49156
  192.4 3.1 %copy-start.57 = (f32[32,1,128]{2,1,0:T(1,128)S(1)}, f32[32,1,128]{2,1,0:T(1,128)}, u32[]{:S(2)}) copy-start(f32[32,1,128]{2,1,0:T(1,128)} %param.29) | copy-start | bytes 49156
  192.4 3.1 %copy-start.93 = (f32[32]{0:T(128)S(1)}, f32[32]{0:T(128)}, u32[]{:S(2)}) copy-start(f32[32]{0:T(128)} %param.38) | copy-start | bytes 388
  192.6 9.1 %copy-start.44 = (f32[3,2048]{1,0:T(4,128)S(1)}, f32[3,2048]{1,0:T(4,128)}, u32[]{:S(2)}) copy-start(f32[3,2048]{1,0:T(4,128)} %slice_bitcast_fusion.4) | copy-start | bytes 73732
  192.6 9.1 %copy-start.65 = (f32[3,256]{1,0:T(4,128)S(1)}, f32[3,256]{1,0:T(4,128)}, u32[]{:S(2)}) copy-start(f32[3,256]{1,0:T(4,128)} %slice_bitcast_fusion.7) | copy-start | bytes 9220
  192.6 9.1 %copy-start.67 = (f32[3,256]{1,0:T(4,128)S(1)}, f32[3,256]{1,0:T(4,128)}, u32[]{:S(2)}) copy-start(f32[3,256]{1,0:T(4,128)} %copy-done.66) | copy-start | bytes 9220
  193.2 8.5 %collective-permute-start.6 = (f32[3,2560]{1,0:T(4,128)S(1)}, f32[3,2560]{1,0:T(4,128)S(1)}, u32[]{:S(2)}, u32[]{:S(2)}) collective-permute-start(f32[3,2560]{1,0:T(4,128)S(1)} %pad_maximum_fusion.8), channel_id=1, source_target_pairs={{4,0},{8,4},{12,8},{5,1},{9,5},{13,9},{6,2},{10,6},{14,10},{7,3},{... | collective-permute-start | bytes 92168 | tf_op jit(solution)/shard_map/ppermute | solution.py:22
  198.5 5.5 %copy-start.19 = (f32[131,2048]{1,0:T(8,128)S(1)}, f32[131,2048]{1,0:T(8,128)}, u32[]{:S(2)}) copy-start(f32[131,2048]{1,0:T(8,128)} %pad_add_fusion.1) | copy-start | bytes 3219460
  (41 other events, 56.6 us)
